TPU v7x, 128 devices: a whole 4x4x4 slice. The times are simulated.
128 devices in a mesh: row: 16 (over x, y), col: 8 (over z, core).
Axes of the slice: x: 4, y: 4, z: 4, core: 2. Of those that a mesh axis runs over, the one named last changes fastest.
Arguments:
- pattern_in: int32 [64, 16], replicated, may hold values from 0 to 63, as said below
- pattern_mid: int32 [64, 16], replicated, may hold values from 0 to 63, as said below
- pattern_out: int32 [64, 16], replicated, may hold values from 0 to 63, as said below
- density_blocks: float32 [4, 16, 2, 8, 256, 256], P(None, 'row', None, 'col'), as said below
Outputs:
- purified_blocks: float32 [4, 16, 2, 8, 256, 256], P(None, 'row', None, 'col')
Inputs may be any that keep to these rules, and one draw needn't show every extreme that they name: `pattern_in`: slot l * 8 + c of block row I names a block column congruent to c modulo 8; no column stands twice in a row; slot I mod 8 of row I names I; J stands in row I exactly when I stands in row J. `pattern_mid`: as for pattern_in. `pattern_out`: as for pattern_in. `density_blocks`: the block of row J for column I is the transpose of the block of row I for column J.
All inputs are finite; a program needn't handle non-finite values.
Results may differ from a plain program's by a relative error of at most 0.0091.
Values may be sent and summed in bfloat16 or wider, within the bound.
No kernel may reach another device: no remote copies, remote signals or barrier semaphores. Data moves between devices by JAX's collectives and lax.ppermute only.
A program may use at most 128 MiB of HBM per device.

v0:
```python
import jax
import jax.numpy as jnp
from jax import lax
from jax.sharding import PartitionSpec as P

ITERS = 2


def purify_section(owned, cur_list, next_list, grid_rows, grid_cols, row_index, col_index):
    block_rows = owned.shape[0]
    slot_pairs = owned.shape[2]
    edge_size = owned.shape[4]
    total_rows = cur_list.shape[0]
    slot_count = cur_list.shape[1]
    occupied = total_rows * edge_size / 2.0
    panels = owned.astype(jnp.bfloat16)
    owned_slots = owned[:, 0, :, 0]
    my_rows = lax.dynamic_index_in_dim(
        cur_list.reshape(block_rows, grid_rows, slot_count), row_index, axis=1, keepdims=False
    )
    my_residue = lax.dynamic_index_in_dim(
        my_rows.reshape(block_rows, slot_pairs, grid_cols), col_index, axis=2, keepdims=False
    )
    own_index = jnp.arange(block_rows, dtype=jnp.int32) * grid_rows + row_index
    diag_term = jnp.sum(
        jnp.where(my_residue == own_index[:, None], jnp.trace(owned_slots, axis1=2, axis2=3), 0.0)
    )
    next_trace = None
    trace_now = lax.psum(diag_term, ("row", "col"))
    gathered_rows = lax.all_gather(panels, "col", axis=3, tiled=True).reshape(
        block_rows, slot_count, edge_size, edge_size
    )
    next_rows = lax.dynamic_index_in_dim(
        next_list.reshape(block_rows, grid_rows, slot_count), row_index, axis=1, keepdims=False
    )
    out_cols = lax.dynamic_index_in_dim(
        next_rows.reshape(block_rows, slot_pairs, grid_cols), col_index, axis=2, keepdims=False
    )
    inner_safe = jnp.maximum(my_rows, 0)
    valid_inner = my_rows >= 0
    valid_out = out_cols >= 0
    column_panels = lax.all_gather(panels, "row", axis=1, tiled=True).reshape(
        total_rows * slot_pairs, edge_size, edge_size
    )
    residue_lists = lax.dynamic_index_in_dim(
        cur_list.reshape(total_rows, slot_pairs, grid_cols), col_index, axis=2, keepdims=False
    )
    candidates = residue_lists[inner_safe]
    matches = (
        (candidates[:, None, :, :] == out_cols[:, :, None, None])
        & valid_inner[:, None, :, None]
        & valid_out[:, :, None, None]
    )
    chosen = jnp.sum(matches * jnp.arange(slot_pairs, dtype=jnp.int32), axis=-1)
    present = jnp.any(matches, axis=-1)
    position = inner_safe[:, None, :] * slot_pairs + chosen
    picked = jnp.where(
        present[..., None, None], column_panels[position], jnp.zeros((), jnp.bfloat16)
    )
    product = jnp.einsum(
        "ikuv,ilkvw->iluw", gathered_rows, picked, preferred_element_type=jnp.float32
    )
    keep = (my_residue[:, None, :] == out_cols[:, :, None]) & valid_out[:, :, None]
    previous = jnp.sum(jnp.where(keep[..., None, None], owned_slots[:, None], 0.0), axis=2)
    updated = jnp.where(trace_now > occupied, product, 2.0 * previous - product)
    return (updated.reshape(block_rows, 1, slot_pairs, 1, edge_size, edge_size), next_trace)


def shards(pattern_in, pattern_mid, pattern_out, density_blocks):
    grid_rows = lax.axis_size("row")
    grid_cols = lax.axis_size("col")
    row_index = lax.axis_index("row")
    col_index = lax.axis_index("col")
    all_lists = (pattern_in, pattern_mid, pattern_out)
    current = density_blocks
    for iteration in range(ITERS):
        current, known_trace = purify_section(
            current,
            all_lists[iteration],
            all_lists[iteration + 1],
            grid_rows,
            grid_cols,
            row_index,
            col_index,
        )
    return current


def solution(mesh):
    in_specs = (P(), P(), P(), P(None, "row", None, "col", None, None))
    out_specs = P(None, "row", None, "col", None, None)
    return jax.shard_map(shards, mesh=mesh, in_specs=in_specs, out_specs=out_specs, check_vma=False)
```

profile of v0, /device:TPU:0, one launch (start us, length us, event | category | flops | bytes accessed | tf_op | source)
XLA Modules:
  0.0 391.4 jit_solution(4681731561013483844)
XLA Ops:
  6.5 2.8 convert_element_type.11
  9.5 0.7 all-gather.9.cloned.1.call-update
  10.2 1.8 copy.96
  12.1 0.1 constant_dynamic-slice_fusion.5
  12.2 0.1 copy.128
  12.3 0.1 reshape.154
  12.5 0.1 copy.94
  12.6 0.1 copy.95
  12.7 1.9 fusion.9
  14.6 0.7 select_reduce_fusion.6
  15.3 72.0 %psum.14 = f32[]{:T(128)} all-reduce(f32[]{:T(128)} %select_reduce_fusion.6), channel_id=1, replica_groups=mesh['row'=16,'col'=8] {'row','col'}, use_global_device_ids=true, to_apply=%region_2.3 | all-reduce | flops 1 | bytes 8 | tf_op jit(solution)/shard_map/psum | solution.py:29
  87.4 0.1 copy.127
  87.5 0.1 reshape.152
  87.6 0.2 compare_reduce_fusion.1
  87.9 0.1 copy.91
  88.1 0.1 copy.131
  88.2 0.1 reshape.160
  88.3 0.2 compare_reduce_fusion
  88.6 0.1 copy.111
  88.8 0.1 copy.98
  88.9 0.6 gather_fusion
  89.5 0.1 copy.124
  89.6 0.1 copy.92
  89.7 0.1 fusion.17
  89.9 0.1 copy.116
  90.0 0.1 compare_and_fusion
  90.1 1.7 select_reduce_fusion.1
  91.8 2.0 copy.106
  94.4 30.2 %all-gather.7.cloned.1.call-done = bf16[4,16,2,1,256,256]{5,4,3,2,1,0:T(8,128)(2,1)} async-done(((bf16[4,1,2,1,256,256]{5,4,3,2,1,0:T(8,128)(2,1)}), bf16[4,16,2,1,256,256]{5,4,3,2,1,0:T(8,128)(2,1)}) %all-gather.7.cloned.1.call-update) | async-done | bytes 16777232 | tf_op jit(solution)/shard_map/all_gather | solution.py:42
  124.6 14.7 %gather_fusion.1 = bf16[128,256,256]{2,1,0:T(8,128)(2,1)} fusion(bf16[128,256,256]{2,1,0:T(8,128)(2,1)} %bitcast.85, s32[1024]{0:T(1024)S(1)} %pad_clamp_fusion.2), kind=kCustom, calls=%fused_computation.1 | custom fusion | bytes 33554944 | tf_op jit(solution)/shard_map/gather | solution.py:58
  139.3 21.2 %copy.102 = bf16[128,256,256]{1,2,0:T(8,128)(2,1)} copy(bf16[128,256,256]{2,1,0:T(8,128)(2,1)} %gather_fusion.1) | data formatting | bytes 33554432 | tf_op jit(solution)/shard_map/gather | solution.py:58
  160.5 15.1 %all-gather.9.cloned.1.call-done = bf16[4,1,2,8,256,256]{5,4,3,2,1,0:T(8,128)(2,1)} async-done(((bf16[4,1,2,1,256,256]{5,4,3,2,1,0:T(8,128)(2,1)}), bf16[4,1,2,8,256,256]{5,4,3,2,1,0:T(8,128)(2,1)}) %all-gather.9.cloned.1.call-update) | async-done | bytes 8388624 | tf_op jit(solution)/shard_map/all_gather | solution.py:30
  175.5 12.1 %select_reduce_fusion.2 = (f32[4,2]{1,0:T(4,128)S(1)}, bf16[4,2,256,256]{2,3,1,0:T(8,128)(2,1)}, f32[4,2,256,256]{2,3,1,0:T(8,128)}) fusion(pred[256,256]{0,1:T(8,128)(4,1)S(1)} %iota_compare_fusion, f32[4,2,256,256]{2,3,1,0:T(8,128)S(1)} %copy.106, bf16[4,16,256,256,1]{3,2,1,4,0:T(8,128)(2,1)} %bitcast.101, bf16[4,2,16,256,256]{3,4,2,1,0:T(8,128)(2,1)} %bitcast.87, ...), kind=kOutput, calls=%fused_computation.19 | convolution fusion | flops 4306501632 | bytes 30474400 | tf_op jit(solution)/shard_map/ikuv,ilkvw->iluw/dot_general | solution.py:60
  187.7 0.5 all-gather.11.cloned.1.call-update
  188.3 0.1 copy.108
  188.4 0.6 gather_fusion.2
  189.0 0.1 copy.126
  189.1 0.1 fusion.16
  189.3 0.8 select_reduce_fusion.5
  190.1 66.8 %psum.15 = f32[]{:T(128)} all-reduce(f32[]{:T(128)} %select_reduce_fusion.5), channel_id=1, replica_groups=mesh['row'=16,'col'=8] {'row','col'}, use_global_device_ids=true, to_apply=%region_8.9 | all-reduce | flops 1 | bytes 8 | tf_op jit(solution)/shard_map/psum | solution.py:29
  256.8 2.1 copy.117
  259.0 1.7 select_reduce_fusion
  260.7 1.9 copy.118
  263.4 11.6 %copy.114 = bf16[4,2,2048,256]{3,2,1,0:T(8,128)(2,1)} copy(bf16[4,2,2048,256]{2,3,1,0:T(8,128)(2,1)} %all-gather.13.cloned.1.call-done) | data formatting | bytes 16777216 | tf_op jit(solution)/shard_map/all_gather | solution.py:30
  274.9 81.5 %all-gather.11.cloned.1.call-done = bf16[4,32,256,256]{2,3,1,0:T(8,128)(2,1)} async-done(((bf16[4,2,256,256]{2,3,1,0:T(8,128)(2,1)}), bf16[4,32,256,256]{2,3,1,0:T(8,128)(2,1)}) %all-gather.11.cloned.1.call-update) | async-done | bytes 16777232 | tf_op jit(solution)/shard_map/all_gather | solution.py:42
  356.4 14.1 %gather_fusion.3 = bf16[128,256,256]{1,2,0:T(8,128)(2,1)} fusion(bf16[128,256,256]{1,2,0:T(8,128)(2,1)} %bitcast.86, s32[1024]{0:T(1024)S(1)} %pad_clamp_fusion), kind=kCustom, calls=%fused_computation.3 | custom fusion | bytes 33554944 | tf_op jit(solution)/shard_map/gather | solution.py:58
  370.4 11.6 %fusion.8 = f32[4,1,2,1,256,256]{4,5,2,0,3,1:T(8,128)} fusion(f32[4,2,256,256]{2,3,1,0:T(8,128)S(1)} %copy.118, bf16[4,16,256,256,1]{3,2,1,4,0:T(8,128)(2,1)} %bitcast.89, bf16[4,2,16,256,256]{3,4,2,1,0:T(8,128)(2,1)} %bitcast.88, pred[4,2,16]{2,1,0:T(4,128)(4,1)S(1)} %copy.112, pred[]{:T(512)S(6)} %gt.7), kind=kOutput, calls=%fused_computation.16 | convolution fusion | flops 4304928768 | bytes 29360256 | tf_op jit(solution)/shard_map/ikuv,ilkvw->iluw/dot_general | solution.py:60
  382.0 2.9 copy.119
  (41 shorter events, 1.1 us)
Async XLA Ops:
  6.5 3.7 copy-start
  6.5 5.5 %copy-start.2 = (s32[64,16]{0,1:T(8,128)S(1)}, s32[64,16]{0,1:T(8,128)}, u32[]{:S(2)}) copy-start(s32[64,16]{0,1:T(8,128)} %param.4) | copy-start | bytes 12292
  6.5 118.1 %all-gather.7.cloned.1.call-start = ((), (), s32[]{:S(2)}) async-start(), calls=%async_computation | async-start | bytes 17825792 | tf_op jit(solution)/shard_map/all_gather | solution.py:42
  9.4 77.9 %copy-start.1 = (s32[64,16]{0,1:T(8,128)S(1)}, s32[64,16]{0,1:T(8,128)}, u32[]{:S(2)}) copy-start(s32[64,16]{0,1:T(8,128)} %param.5) | copy-start | bytes 12292
  9.4 78.6 %copy-start.3 = (s32[64,16]{0,1:T(8,128)S(1)}, s32[64,16]{0,1:T(8,128)}, u32[]{:S(2)}) copy-start(s32[64,16]{0,1:T(8,128)} %param.6) | copy-start | bytes 12292
  9.4 166.1 %all-gather.9.cloned.1.call-start = ((), (), s32[]{:S(2)}) async-start(), calls=%async_computation.1 | async-start | bytes 9437184 | tf_op jit(solution)/shard_map/all_gather | solution.py:30
  10.2 253.2 %all-gather.13.cloned.1.call-start = ((), (), s32[]{:S(2)}) async-start(), calls=%async_computation.3 | async-start | bytes 9437184 | tf_op jit(solution)/shard_map/all_gather | solution.py:30
  187.7 168.7 %all-gather.11.cloned.1.call-start = ((), (), s32[]{:S(2)}) async-start(), calls=%async_computation.2 | async-start | bytes 17825792 | tf_op jit(solution)/shard_map/all_gather | solution.py:42
Sparse Core Ops, SparseCore 0:
  9.5 115.0 all-gather.6
  126.3 49.1 all-gather.8
  187.8 54.5 all-gather.12
  244.5 111.8 all-gather.10
where the time goes:
time: 393 us; the launch traced here: 391 us
  blocking collectives  139 us (35%)
  waiting for transfers between devices  128 us (33%)
  local copies, waits for them, and re-layouts  75.8 us (19%)
  matrix products  23.7 us (6%)
  between operations  14.5 us (4%)
  other arithmetic  10.5 us (3%)
    psum x2, blocking collectives, purify_section(): trace_now = lax.psum(diag_term, ('row', 'col'))  139 us
    all_gather x2, waiting for transfers between devices, purify_section(): lax.all_gather(panels, 'row', axis=1, tiled=True)  112 us
    gather x3, local copies, waits for them, and re-layouts, purify_section(): column_panels[position]  49.9 us
    dot_general x2, matrix products, purify_section(): jnp.einsum('ikuv,ilkvw->iluw', gathered_rows, picked, preferred_element_t...  23.7 us
    all_gather x2, waiting for transfers between devices, purify_section(): lax.all_gather(panels, 'col', axis=3, tiled=True)  15.1 us
    all_gather x1, local copies, waits for them, and re-layouts, purify_section(): lax.all_gather(panels, 'col', axis=3, tiled=True)  11.6 us
  transfers between devices with their start and end apart: 4, of which 3 were waited for; matrix products, arithmetic and copies ran while one was open for 17% of the time, Pallas kernels for 0%

commit v1 on v0

v1 whole, which is shorter than its diff:
```python
import functools

import jax
import jax.numpy as jnp
from jax import lax
from jax.experimental import pallas as pl
from jax.experimental.pallas import tpu as pltpu
from jax.sharding import PartitionSpec as P

ITERS = 2


def product_kernel(n_ref, o_ref, a_ref, b_ref, prev_ref, misc_ref,
                   rows_hbm, cols_hbm, owned_ref, out_ref, abuf, bbuf, sem):
    n = n_ref[0]
    out_ref[...] = jnp.zeros_like(out_ref)

    def copies(t, slot):
        ca = pltpu.make_async_copy(rows_hbm.at[a_ref[t]], abuf.at[slot], sem.at[0, slot])
        cb = pltpu.make_async_copy(cols_hbm.at[b_ref[t]], bbuf.at[slot], sem.at[1, slot])
        return ca, cb

    @pl.when(n > 0)
    def _():
        ca, cb = copies(0, 0)
        ca.start()
        cb.start()

    def body(t, carry):
        slot = t % 2
        ca, cb = copies(t, slot)
        ca.wait()
        cb.wait()

        @pl.when(t + 1 < n)
        def _():
            na, nb = copies(t + 1, 1 - slot)
            na.start()
            nb.start()

        o = o_ref[t]
        out_ref[o] += jnp.dot(abuf[slot], bbuf[slot], preferred_element_type=jnp.float32)
        return carry

    lax.fori_loop(0, n, body, 0)

    take_product = misc_ref[0] > 0
    for o in range(out_ref.shape[0]):
        p = prev_ref[o]
        prev = jnp.where(p >= 0, owned_ref[jnp.maximum(p, 0)], 0.0)
        acc = out_ref[o]
        out_ref[o] = jnp.where(take_product, acc, 2.0 * prev - acc)


def run_product(n, o_t, a_t, b_t, prev_t, misc, rows, cols, owned):
    nout, edge, _ = owned.shape
    max_terms = o_t.shape[0]
    grid_spec = pltpu.PrefetchScalarGridSpec(
        num_scalar_prefetch=6,
        grid=(1,),
        in_specs=[
            pl.BlockSpec(memory_space=pl.ANY),
            pl.BlockSpec(memory_space=pl.ANY),
            pl.BlockSpec((nout, edge, edge), lambda g, *refs: (0, 0, 0)),
        ],
        out_specs=pl.BlockSpec((nout, edge, edge), lambda g, *refs: (0, 0, 0)),
        scratch_shapes=[
            pltpu.VMEM((2, edge, edge), rows.dtype),
            pltpu.VMEM((2, edge, edge), cols.dtype),
            pltpu.SemaphoreType.DMA((2, 2)),
        ],
    )
    flops = 2 * edge * edge * edge * max_terms // 4
    cost = pl.CostEstimate(
        flops=flops, transcendentals=0, bytes_accessed=(max_terms // 2) * edge * edge * 4 + 3 * nout * edge * edge * 4
    )
    return pl.pallas_call(
        product_kernel,
        grid_spec=grid_spec,
        out_shape=jax.ShapeDtypeStruct(owned.shape, jnp.float32),
        cost_estimate=cost,
    )(n, o_t, a_t, b_t, prev_t, misc, rows, cols, owned)


def col_gather(x, grid_cols):
    plus2 = [(j, (j + 2) % grid_cols) for j in range(grid_cols)]
    minus2 = [(j, (j - 2) % grid_cols) for j in range(grid_cols)]
    sib = [(j, j ^ 1) for j in range(grid_cols)]
    half = x.shape[0] // 2
    from_minus = lax.ppermute(x, "col", plus2)
    from_plus = lax.ppermute(x, "col", minus2)
    sib_own = lax.ppermute(x, "col", sib)
    far_a = lax.ppermute(from_minus[:half], "col", plus2)
    far_b = lax.ppermute(from_plus[half:], "col", minus2)
    far = jnp.concatenate([far_a, far_b], axis=0)
    sib_near = lax.ppermute(jnp.stack([from_minus, from_plus]), "col", sib)
    sib_far = lax.ppermute(far, "col", sib)
    pieces = jnp.stack([x, from_minus, from_plus, far, sib_own, sib_near[0], sib_near[1], sib_far])
    return pieces


def piece_classes(col_index, grid_cols):
    j = col_index
    s = j ^ 1
    offs = jnp.stack([j, j - 2, j + 2, j + 4, s, s - 2, s + 2, s + 4])
    return offs % grid_cols


def purify_section(owned, cur_list, next_list, trace_now, grid_rows, grid_cols, row_index, col_index):
    block_rows = owned.shape[0]
    slot_pairs = owned.shape[2]
    edge = owned.shape[4]
    total_rows = cur_list.shape[0]
    slot_count = cur_list.shape[1]
    occupied = total_rows * edge / 2.0
    owned4 = owned.reshape(block_rows, slot_pairs, edge, edge)
    panels = owned4.astype(jnp.bfloat16)

    cols = lax.all_gather(panels, "row", axis=0, tiled=False)
    cols = cols.reshape(total_rows * slot_pairs, edge, edge)
    pieces = col_gather(panels, grid_cols)
    rows = pieces.reshape(grid_cols * block_rows * slot_pairs, edge, edge)

    cls = piece_classes(col_index, grid_cols)
    piece_of = jnp.zeros((grid_cols,), jnp.int32).at[cls].set(jnp.arange(grid_cols, dtype=jnp.int32))

    my_ids = jnp.arange(block_rows, dtype=jnp.int32) * grid_rows + row_index
    my_cur = cur_list[my_ids]
    my_next = next_list[my_ids]
    out_cols = my_next.reshape(block_rows, slot_pairs, grid_cols)[:, :, col_index]
    k_ids = jnp.arange(slot_count, dtype=jnp.int32)
    k_class = k_ids % grid_cols
    k_pair = k_ids // grid_cols
    a_idx = (piece_of[k_class][None, :] * block_rows + jnp.arange(block_rows, dtype=jnp.int32)[:, None]) * slot_pairs \
        + k_pair[None, :]
    inner = my_cur
    cand = cur_list.reshape(total_rows, slot_pairs, grid_cols)[:, :, col_index][inner]
    match = cand[:, None, :, :] == out_cols[:, :, None, None]
    valid = jnp.any(match, axis=-1)
    lsel = jnp.argmax(match, axis=-1).astype(jnp.int32)
    b_idx = ((inner % grid_rows) * block_rows + inner // grid_rows)[:, None, :] * slot_pairs + lsel
    nout = block_rows * slot_pairs
    o_ids = jnp.broadcast_to(jnp.arange(nout, dtype=jnp.int32).reshape(block_rows, slot_pairs, 1), valid.shape)
    a_full = jnp.broadcast_to(a_idx[:, None, :], valid.shape)
    flat_valid = valid.reshape(-1)
    order = jnp.argsort(jnp.logical_not(flat_valid), stable=True)
    n_terms = jnp.sum(flat_valid.astype(jnp.int32)).reshape(1)
    o_t = o_ids.reshape(-1)[order]
    a_t = a_full.reshape(-1)[order]
    b_t = b_idx.reshape(-1)[order]

    my_res = my_cur.reshape(block_rows, slot_pairs, grid_cols)[:, :, col_index]
    keep = my_res[:, None, :] == out_cols[:, :, None]
    prev_l = jnp.argmax(keep, axis=-1).astype(jnp.int32)
    prev_t = jnp.where(
        jnp.any(keep, axis=-1), jnp.arange(block_rows, dtype=jnp.int32)[:, None] * slot_pairs + prev_l, -1
    ).reshape(-1)
    misc = (trace_now > occupied).astype(jnp.int32).reshape(1)

    updated = run_product(n_terms, o_t, a_t, b_t, prev_t, misc, rows, cols, owned4.reshape(nout, edge, edge))
    return updated.reshape(block_rows, 1, slot_pairs, 1, edge, edge)


def local_trace(owned, cur_list, grid_rows, grid_cols, row_index, col_index):
    block_rows = owned.shape[0]
    slot_pairs = owned.shape[2]
    slot_count = cur_list.shape[1]
    own_index = jnp.arange(block_rows, dtype=jnp.int32) * grid_rows + row_index
    my_rows = cur_list[own_index]
    my_residue = my_rows.reshape(block_rows, slot_pairs, grid_cols)[:, :, col_index]
    owned_slots = owned[:, 0, :, 0]
    return jnp.sum(jnp.where(my_residue == own_index[:, None], jnp.trace(owned_slots, axis1=2, axis2=3), 0.0))


def shards(pattern_in, pattern_mid, pattern_out, density_blocks):
    grid_rows = lax.axis_size("row")
    grid_cols = lax.axis_size("col")
    row_index = lax.axis_index("row")
    col_index = lax.axis_index("col")
    all_lists = (pattern_in, pattern_mid, pattern_out)
    current = density_blocks
    for iteration in range(ITERS):
        diag_term = local_trace(current, all_lists[iteration], grid_rows, grid_cols, row_index, col_index)
        trace_now = lax.psum(diag_term, ("row", "col"))
        current = purify_section(
            current, all_lists[iteration], all_lists[iteration + 1], trace_now,
            grid_rows, grid_cols, row_index, col_index,
        )
    return current


def solution(mesh):
    in_specs = (P(), P(), P(), P(None, "row", None, "col", None, None))
    out_specs = P(None, "row", None, "col", None, None)
    return jax.shard_map(shards, mesh=mesh, in_specs=in_specs, out_specs=out_specs, check_vma=False)
```

time: 393 us -> 438 us (1.11); the launches traced: 391 us -> 432 us
  Pallas kernels: 0 us -> 153 us
  waiting for transfers between devices: 128 us -> 24.1 us
  local copies, waits for them, and re-layouts: 75.8 us -> 47 us
  matrix products: 23.7 us -> 0 us
  other arithmetic: 10.5 us -> 24.9 us
  starting transfers between devices: 0.12 us -> 14.5 us
  blocking collectives: 139 us -> 153 us
    pallas_call x0 -> x2, Pallas kernels: none -> 153 us  [run_product(): pl.pallas_call(product_kernel, grid_spec=grid_spec, out_shape=jax.ShapeDt...]
    all_gather x4 -> x2, waiting for transfers between devices: 127 us -> 0.01 us  [purify_section(): cols = lax.all_gather(panels, 'row', axis=0, tiled=False)]
    gather x7 -> x14, local copies, waits for them, and re-layouts: 51.3 us -> 14.3 us  [the longest x2 3.55 us: purify_section(): o_t = o_ids.reshape(-1)[order]]
    ppermute x0 -> x14, waiting for transfers between devices: none -> 24.1 us  [the longest x2 24 us: col_gather(): from_minus = lax.ppermute(x, 'col', plus2)]
    dot_general x2 -> x0, matrix products: 23.7 us -> none  [purify_section(): jnp.einsum('ikuv,ilkvw->iluw', gathered_rows, picked, preferred_element_t...]
    unnamed x12 -> x28, local copies, waits for them, and re-layouts: 2.14 us -> 22 us
    psum x2, blocking collectives: 139 us -> 153 us  [shards(): trace_now = lax.psum(diag_term, ('row', 'col'))]
    ppermute x0 -> x14, starting transfers between devices: none -> 14.4 us  [the longest x2 5.35 us: col_gather(): from_plus = lax.ppermute(x, 'col', minus2)]
  transfers between devices with their start and end apart: 4 -> 16, of which waited for: 3 -> 2; matrix products, arithmetic and copies ran while one was open for 17% -> 15% of each run, Pallas kernels for 0% -> 0%
where the time goes in v1:
time: 438 us; the launch traced here: 432 us
  blocking collectives  153 us (35%)
  Pallas kernels  153 us (35%)
  local copies, waits for them, and re-layouts  47 us (11%)
  other arithmetic  24.9 us (6%)
  waiting for transfers between devices  24.1 us (6%)
  between operations  14.8 us (3%)
  starting transfers between devices  14.5 us (3%)
    psum x2, blocking collectives, shards(): trace_now = lax.psum(diag_term, ('row', 'col'))  153 us
    pallas_call x2, Pallas kernels, run_product(): pl.pallas_call(product_kernel, grid_spec=grid_spec, out_shape=jax.ShapeDt...  153 us
    ppermute x2, waiting for transfers between devices, col_gather(): from_minus = lax.ppermute(x, 'col', plus2)  24 us
    unnamed x28, local copies, waits for them, and re-layouts  22 us
  transfers between devices with their start and end apart: 16, of which 2 were waited for; matrix products, arithmetic and copies ran while one was open for 15% of the time, Pallas kernels for 0%

profile of v1, /device:TPU:0, one launch (start us, length us, event | category | flops | bytes accessed | tf_op | source)
XLA Modules:
  0.0 431.9 jit_solution(965925187019369106)
XLA Ops:
  6.6 3.3 bitcast_dynamic-update-slice_fusion.6
  10.0 2.7 bitcast_convert_fusion
  12.6 2.0 collective-permute-start
  14.7 2.1 collective-permute-start.1
  23.6 2.5 sort.32
  26.1 0.7 select_reduce_fusion.1
  26.9 0.7 compare_reduce_fusion
  27.5 12.6 %collective-permute-done = bf16[4,2,256,256]{3,2,1,0:T(8,128)(2,1)S(1)} collective-permute-done((bf16[4,2,256,256]{3,2,1,0:T(8,128)(2,1)}, bf16[4,2,256,256]{3,2,1,0:T(8,128)(2,1)S(1)}, u32[]{:S(2)}, u32[]{:S(2)}) %collective-permute-start) | collective-permute-done | bytes 1048608 | tf_op jit(solution)/shard_map/ppermute | solution.py:90
  40.2 2.7 pad_maximum_fusion
  42.9 1.4 collective-permute-start.2
  44.4 1.9 slice.47
  46.3 1.9 collective-permute-start.3
  48.1 75.9 %psum.14 = f32[]{:T(128)} all-reduce(f32[]{:T(128)} %select_reduce_fusion.1), channel_id=1, replica_groups=mesh['row'=16,'col'=8] {'row','col'}, use_global_device_ids=true, to_apply=%region_15.16 | all-reduce | flops 1 | bytes 8 | tf_op jit(solution)/shard_map/psum | solution.py:184
  124.9 1.7 gather_fusion.10
  126.7 1.7 gather_fusion.11
  128.6 1.8 gather_fusion.9
  131.0 0.7 convert_reduce_fusion
  131.7 1.1 constant_dynamic-update-slice_fusion.1
  132.9 1.1 constant_dynamic-update-slice_fusion.4
  134.0 2.3 constant_dynamic-update-slice_fusion.3
  136.3 1.1 bitcast_dynamic-update-slice_fusion.5
  137.4 2.3 bitcast_dynamic-update-slice_fusion.4
  139.6 3.1 constant_dynamic-update-slice_fusion.2
  142.8 1.0 bitcast_dynamic-update-slice_fusion.3
  143.8 73.3 %shard_map.46.owned_ref = f32[8,256,256]{2,1,0:T(8,128)} custom-call(s32[1]{0:T(128)} %bitcast.22.n_ref, s32[128]{0:T(128)} %gather_fusion.9, s32[128]{0:T(128)} %gather_fusion.10, s32[128]{0:T(128)} %gather_fusion.11, s32[8]{0:T(128)} %reshape.690.prev_ref, s32[1]{0:T(128)} %bitcast.25.misc_ref, bf16[64,256,256]{2,1,0:T(8,128)(2,1)} %bitcast.85, ...), custom_call_target="tpu_custom_call" | custom-call | flops 1073741824 | bytes 23068672 | tf_op jit(solution)/shard_map/pallas_call | solution.py:77
  217.1 3.7 fusion.18
  220.9 3.2 collective-permute-start.8
  225.7 11.4 %collective-permute-done.7 = bf16[4,2,256,256]{3,2,1,0:T(8,128)(2,1)S(1)} collective-permute-done((bf16[4,2,256,256]{3,2,1,0:T(8,128)(2,1)}, bf16[4,2,256,256]{3,2,1,0:T(8,128)(2,1)S(1)}, u32[]{:S(2)}, u32[]{:S(2)}) %collective-permute-start.7) | collective-permute-done | bytes 1048608 | tf_op jit(solution)/shard_map/ppermute | solution.py:90
  237.1 1.5 pad_maximum_fusion.1
  238.8 2.5 sort.31
  241.3 0.8 slice.48
  242.2 0.8 slice.49
  243.0 3.2 collective-permute-start.10
  246.3 1.8 gather_fusion.5
  248.1 1.8 gather_fusion.3
  250.6 1.8 gather_fusion.6
  252.4 0.7 convert_reduce_fusion.1
  254.1 77.4 %psum.15 = f32[]{:T(128)} all-reduce(f32[]{:T(128)} %fusion.1), channel_id=1, replica_groups=mesh['row'=16,'col'=8] {'row','col'}, use_global_device_ids=true, to_apply=%region_18.19 | all-reduce | flops 1 | bytes 8 | tf_op jit(solution)/shard_map/psum | solution.py:184
  332.0 1.1 constant_dynamic-update-slice_fusion.10
  333.1 1.1 constant_dynamic-update-slice_fusion.6
  334.2 1.1 constant_dynamic-update-slice_fusion.5
  335.3 1.1 constant_dynamic-update-slice_fusion.9
  336.5 1.1 constant_dynamic-update-slice_fusion.8
  337.5 1.1 bitcast_dynamic-update-slice_fusion.2
  338.6 2.3 bitcast_dynamic-update-slice_fusion.1
  340.8 3.1 constant_dynamic-update-slice_fusion.7
  344.0 1.0 bitcast_dynamic-update-slice_fusion
  345.0 80.0 %shard_map.47 = f32[8,256,256]{2,1,0:T(8,128)} custom-call(s32[1]{0:T(128)} %bitcast.6.n_ref, s32[128]{0:T(128)} %gather_fusion.3, s32[128]{0:T(128)} %gather_fusion.5, s32[128]{0:T(128)} %gather_fusion.6, s32[8]{0:T(128)} %reshape.685.prev_ref, s32[1]{0:T(128)} %bitcast.35.misc_ref, bf16[64,256,256]{2,1,0:T(8,128)(2,1)} %bitcast.43.rows_hbm, ...), custom_call_target="tpu_custom_call" | custom-call | flops 1073741824 | bytes 23068672 | tf_op jit(solution)/shard_map/pallas_call | solution.py:77
  (119 shorter events, 11.7 us)
Async XLA Ops:
  6.5 15.4 %copy-start = (f32[4,1,2,1,256,256]{5,4,3,2,1,0:T(8,128)S(1)}, f32[4,1,2,1,256,256]{5,4,3,2,1,0:T(8,128)}, u32[]{:S(2)}) copy-start(f32[4,1,2,1,256,256]{5,4,3,2,1,0:T(8,128)} %param.7) | copy-start | bytes 6291460
  6.5 10.3 %copy-start.3 = (s32[64,16]{0,1:T(8,128)S(1)}, s32[64,16]{0,1:T(8,128)}, u32[]{:S(2)}) copy-start(s32[64,16]{0,1:T(8,128)} %param.5) | copy-start | bytes 12292
  6.5 11.0 %copy-start.2 = (s32[64,16]{0,1:T(8,128)S(1)}, s32[64,16]{0,1:T(8,128)}, u32[]{:S(2)}) copy-start(s32[64,16]{0,1:T(8,128)} %param.4) | copy-start | bytes 12292
  6.5 12.0 %copy-start.4 = (s32[64,16]{0,1:T(8,128)S(1)}, s32[64,16]{0,1:T(8,128)}, u32[]{:S(2)}) copy-start(s32[64,16]{0,1:T(8,128)} %param.6) | copy-start | bytes 12292
  6.5 137.3 %all-gather.6.cloned.1.call-start = ((), (), s32[]{:S(2)}) async-start(), calls=%async_computation.1 | async-start | bytes 17825792 | tf_op jit(solution)/shard_map/all_gather | solution.py:119
  9.9 335.1 %all-gather.4.cloned.1.call-start = ((), (), s32[]{:S(2)}) async-start(), calls=%async_computation | async-start | bytes 17825792 | tf_op jit(solution)/shard_map/all_gather | solution.py:119
  12.6 27.5 %collective-permute-start = (bf16[4,2,256,256]{3,2,1,0:T(8,128)(2,1)}, bf16[4,2,256,256]{3,2,1,0:T(8,128)(2,1)S(1)}, u32[]{:S(2)}, u32[]{:S(2)}) collective-permute-start(bf16[4,2,256,256]{3,2,1,0:T(8,128)(2,1)} %bitcast_convert_fusion), channel_id=1, source_target_pairs={{0,2},{1,3},{2,4},{3,5},{4,6},{5,7},{6,0},{7,1},{8,10},{9,11},{10,... | collective-permute-start | bytes 3145736 | tf_op jit(solution)/shard_map/ppermute | solution.py:90
  14.7 25.5 %collective-permute-start.1 = (bf16[4,2,256,256]{3,2,1,0:T(8,128)(2,1)}, bf16[4,2,256,256]{3,2,1,0:T(8,128)(2,1)}, u32[]{:S(2)}, u32[]{:S(2)}) collective-permute-start(bf16[4,2,256,256]{3,2,1,0:T(8,128)(2,1)} %bitcast_convert_fusion), channel_id=1, source_target_pairs={{0,6},{1,7},{2,0},{3,1},{4,2},{5,3},{6,4},{7,5},{8,14},{9,15},{10,... | collective-permute-start | bytes 3145736 | tf_op jit(solution)/shard_map/ppermute | solution.py:91
  16.8 120.6 %collective-permute-start.4 = (bf16[4,2,256,256]{3,2,1,0:T(8,128)(2,1)}, bf16[4,2,256,256]{3,2,1,0:T(8,128)(2,1)}, u32[]{:S(2)}, u32[]{:S(2)}) collective-permute-start(bf16[4,2,256,256]{3,2,1,0:T(8,128)(2,1)} %bitcast_convert_fusion), channel_id=1, source_target_pairs={{0,1},{1,0},{2,3},{3,2},{4,5},{5,4},{6,7},{7,6},{8,9},{9,8},{10,11... | collective-permute-start | bytes 3145736 | tf_op jit(solution)/shard_map/ppermute | solution.py:92
  42.9 96.7 %collective-permute-start.5 = (bf16[2,4,2,256,256]{4,3,2,1,0:T(8,128)(2,1)}, bf16[2,4,2,256,256]{4,3,2,1,0:T(8,128)(2,1)}, u32[]{:S(2)}, u32[]{:S(2)}) collective-permute-start(bf16[2,4,2,256,256]{4,3,2,1,0:T(8,128)(2,1)} %pad_maximum_fusion), channel_id=1, source_target_pairs={{0,1},{1,0},{2,3},{3,2},{4,5},{5,4},{6,7},{7,6},{8,9},{9,8},{10,11... | collective-permute-start | bytes 6291464 | tf_op jit(solution)/shard_map/ppermute | solution.py:96
  42.9 88.7 %collective-permute-start.2 = (bf16[2,2,256,256]{3,2,1,0:T(8,128)(2,1)S(1)}, bf16[2,2,256,256]{3,2,1,0:T(8,128)(2,1)}, u32[]{:S(2)}, u32[]{:S(2)}) collective-permute-start(bf16[2,2,256,256]{3,2,1,0:T(8,128)(2,1)S(1)} %slice.46), channel_id=1, source_target_pairs={{0,2},{1,3},{2,4},{3,5},{4,6},{5,7},{6,0},{7,1},{8,10},{9,11},{10,... | collective-permute-start | bytes 1572872 | tf_op jit(solution)/shard_map/ppermute | solution.py:93
  46.3 86.5 %collective-permute-start.3 = (bf16[2,2,256,256]{3,2,1,0:T(8,128)(2,1)}, bf16[2,2,256,256]{3,2,1,0:T(8,128)(2,1)S(1)}, u32[]{:S(2)}, u32[]{:S(2)}) collective-permute-start(bf16[2,2,256,256]{3,2,1,0:T(8,128)(2,1)} %slice.47), channel_id=1, source_target_pairs={{0,6},{1,7},{2,0},{3,1},{4,2},{5,3},{6,4},{7,5},{8,14},{9,15},{10,... | collective-permute-start | bytes 1572872 | tf_op jit(solution)/shard_map/ppermute | solution.py:94
  132.8 10.0 %collective-permute-start.6 = (bf16[4,2,256,256]{3,2,1,0:T(8,128)(2,1)S(1)}, bf16[4,2,256,256]{3,2,1,0:T(8,128)(2,1)S(1)}, u32[]{:S(2)}, u32[]{:S(2)}) collective-permute-start(bf16[4,2,256,256]{3,2,1,0:T(8,128)(2,1)S(1)} %constant_dynamic-update-slice_fusion), channel_id=1, source_target_pairs={{0,1},{1,0},{2,3},{3,2},{4,5},{5,4},{6,7},{7,6},{8,9},{9,8},{10,11... | collective-permute-start | bytes 3145736 | tf_op jit(solution)/shard_map/ppermute | solution.py:97
  220.8 33.1 %copy-start.1 = (bf16[8,256,256]{2,1,0:T(8,128)(2,1)S(1)}, bf16[8,256,256]{2,1,0:T(8,128)(2,1)}, u32[]{:S(2)}) copy-start(bf16[8,256,256]{2,1,0:T(8,128)(2,1)} %get-tuple-element.21) | copy-start | bytes 3145732
  220.8 16.3 %collective-permute-start.7 = (bf16[4,2,256,256]{3,2,1,0:T(8,128)(2,1)}, bf16[4,2,256,256]{3,2,1,0:T(8,128)(2,1)S(1)}, u32[]{:S(2)}, u32[]{:S(2)}) collective-permute-start(bf16[4,2,256,256]{3,2,1,0:T(8,128)(2,1)} %bitcast.87), channel_id=1, source_target_pairs={{0,2},{1,3},{2,4},{3,5},{4,6},{5,7},{6,0},{7,1},{8,10},{9,11},{10,... | collective-permute-start | bytes 3145736 | tf_op jit(solution)/shard_map/ppermute | solution.py:90
  220.9 16.2 %collective-permute-start.8 = (bf16[4,2,256,256]{3,2,1,0:T(8,128)(2,1)}, bf16[4,2,256,256]{3,2,1,0:T(8,128)(2,1)S(1)}, u32[]{:S(2)}, u32[]{:S(2)}) collective-permute-start(bf16[4,2,256,256]{3,2,1,0:T(8,128)(2,1)} %bitcast.88), channel_id=1, source_target_pairs={{0,6},{1,7},{2,0},{3,1},{4,2},{5,3},{6,4},{7,5},{8,14},{9,15},{10,... | collective-permute-start | bytes 3145736 | tf_op jit(solution)/shard_map/ppermute | solution.py:91
  238.6 102.2 %collective-permute-start.12 = (bf16[2,4,2,256,256]{4,3,2,1,0:T(8,128)(2,1)}, bf16[2,4,2,256,256]{4,3,2,1,0:T(8,128)(2,1)}, u32[]{:S(2)}, u32[]{:S(2)}) collective-permute-start(bf16[2,4,2,256,256]{4,3,2,1,0:T(8,128)(2,1)} %pad_maximum_fusion.1), channel_id=1, source_target_pairs={{0,1},{1,0},{2,3},{3,2},{4,5},{5,4},{6,7},{7,6},{8,9},{9,8},{10,11... | collective-permute-start | bytes 6291464 | tf_op jit(solution)/shard_map/ppermute | solution.py:96
  242.2 90.9 %collective-permute-start.9 = (bf16[2,2,256,256]{3,2,1,0:T(8,128)(2,1)}, bf16[2,2,256,256]{3,2,1,0:T(8,128)(2,1)}, u32[]{:S(2)}, u32[]{:S(2)}) collective-permute-start(bf16[2,2,256,256]{3,2,1,0:T(8,128)(2,1)} %slice.48), channel_id=1, source_target_pairs={{0,2},{1,3},{2,4},{3,5},{4,6},{5,7},{6,0},{7,1},{8,10},{9,11},{10,... | collective-permute-start | bytes 1572872 | tf_op jit(solution)/shard_map/ppermute | solution.py:93
  243.0 91.1 %collective-permute-start.10 = (bf16[2,2,256,256]{3,2,1,0:T(8,128)(2,1)}, bf16[2,2,256,256]{3,2,1,0:T(8,128)(2,1)}, u32[]{:S(2)}, u32[]{:S(2)}) collective-permute-start(bf16[2,2,256,256]{3,2,1,0:T(8,128)(2,1)} %slice.49), channel_id=1, source_target_pairs={{0,6},{1,7},{2,0},{3,1},{4,2},{5,3},{6,4},{7,5},{8,14},{9,15},{10,... | collective-permute-start | bytes 1572872 | tf_op jit(solution)/shard_map/ppermute | solution.py:94
  253.8 84.7 %collective-permute-start.11 = (bf16[4,2,256,256]{3,2,1,0:T(8,128)(2,1)S(1)}, bf16[4,2,256,256]{3,2,1,0:T(8,128)(2,1)}, u32[]{:S(2)}, u32[]{:S(2)}) collective-permute-start(bf16[4,2,256,256]{3,2,1,0:T(8,128)(2,1)S(1)} %bitcast.89), channel_id=1, source_target_pairs={{0,1},{1,0},{2,3},{3,2},{4,5},{5,4},{6,7},{7,6},{8,9},{9,8},{10,11... | collective-permute-start | bytes 3145736 | tf_op jit(solution)/shard_map/ppermute | solution.py:92
  335.3 8.7 %collective-permute-start.13 = (bf16[4,2,256,256]{3,2,1,0:T(8,128)(2,1)S(1)}, bf16[4,2,256,256]{3,2,1,0:T(8,128)(2,1)S(1)}, u32[]{:S(2)}, u32[]{:S(2)}) collective-permute-start(bf16[4,2,256,256]{3,2,1,0:T(8,128)(2,1)S(1)} %constant_dynamic-update-slice_fusion.5), channel_id=1, source_target_pairs={{0,1},{1,0},{2,3},{3,2},{4,5},{5,4},{6,7},{7,6},{8,9},{9,8},{10,11... | collective-permute-start | bytes 3145736 | tf_op jit(solution)/shard_map/ppermute | solution.py:97
Sparse Core Ops, SparseCore 0:
  10.0 115.7 all-gather.5
  220.9 119.1 all-gather.3

commit v2 on v1

--- a/solution.py
+++ b/solution.py
@@ -1,5 +1,3 @@
-import functools
-
 import jax
 import jax.numpy as jnp
 from jax import lax
@@ -10,39 +8,15 @@
 ITERS = 2
 
 
-def product_kernel(n_ref, o_ref, a_ref, b_ref, prev_ref, misc_ref,
-                   rows_hbm, cols_hbm, owned_ref, out_ref, abuf, bbuf, sem):
-    n = n_ref[0]
+def product_kernel(n_ref, o_ref, a_ref, b_ref, prev_ref, misc_ref, rows_ref, cols_ref, owned_ref, out_ref):
     out_ref[...] = jnp.zeros_like(out_ref)
 
-    def copies(t, slot):
-        ca = pltpu.make_async_copy(rows_hbm.at[a_ref[t]], abuf.at[slot], sem.at[0, slot])
-        cb = pltpu.make_async_copy(cols_hbm.at[b_ref[t]], bbuf.at[slot], sem.at[1, slot])
-        return ca, cb
-
-    @pl.when(n > 0)
-    def _():
-        ca, cb = copies(0, 0)
-        ca.start()
-        cb.start()
-
     def body(t, carry):
-        slot = t % 2
-        ca, cb = copies(t, slot)
-        ca.wait()
-        cb.wait()
-
-        @pl.when(t + 1 < n)
-        def _():
-            na, nb = copies(t + 1, 1 - slot)
-            na.start()
-            nb.start()
-
         o = o_ref[t]
-        out_ref[o] += jnp.dot(abuf[slot], bbuf[slot], preferred_element_type=jnp.float32)
+        out_ref[o] += jnp.dot(rows_ref[a_ref[t]], cols_ref[b_ref[t]], preferred_element_type=jnp.float32)
         return carry
 
-    lax.fori_loop(0, n, body, 0)
+    lax.fori_loop(0, n_ref[0], body, 0)
 
     take_product = misc_ref[0] > 0
     for o in range(out_ref.shape[0]):
@@ -55,30 +29,17 @@
 def run_product(n, o_t, a_t, b_t, prev_t, misc, rows, cols, owned):
     nout, edge, _ = owned.shape
     max_terms = o_t.shape[0]
-    grid_spec = pltpu.PrefetchScalarGridSpec(
-        num_scalar_prefetch=6,
-        grid=(1,),
-        in_specs=[
-            pl.BlockSpec(memory_space=pl.ANY),
-            pl.BlockSpec(memory_space=pl.ANY),
-            pl.BlockSpec((nout, edge, edge), lambda g, *refs: (0, 0, 0)),
-        ],
-        out_specs=pl.BlockSpec((nout, edge, edge), lambda g, *refs: (0, 0, 0)),
-        scratch_shapes=[
-            pltpu.VMEM((2, edge, edge), rows.dtype),
-            pltpu.VMEM((2, edge, edge), cols.dtype),
-            pltpu.SemaphoreType.DMA((2, 2)),
-        ],
-    )
+    smem = pl.BlockSpec(memory_space=pltpu.SMEM)
+    vmem = pl.BlockSpec(memory_space=pltpu.VMEM)
     flops = 2 * edge * edge * edge * max_terms // 4
-    cost = pl.CostEstimate(
-        flops=flops, transcendentals=0, bytes_accessed=(max_terms // 2) * edge * edge * 4 + 3 * nout * edge * edge * 4
-    )
+    nbytes = (rows.size + cols.size) * 2 + 2 * owned.size * 4
     return pl.pallas_call(
         product_kernel,
-        grid_spec=grid_spec,
+        in_specs=[smem] * 6 + [vmem] * 3,
+        out_specs=vmem,
         out_shape=jax.ShapeDtypeStruct(owned.shape, jnp.float32),
-        cost_estimate=cost,
+        cost_estimate=pl.CostEstimate(flops=flops, transcendentals=0, bytes_accessed=nbytes),
+        compiler_params=pltpu.CompilerParams(vmem_limit_bytes=48 * 1024 * 1024),
     )(n, o_t, a_t, b_t, prev_t, misc, rows, cols, owned)
 
 
@@ -181,7 +142,7 @@
     current = density_blocks
     for iteration in range(ITERS):
         diag_term = local_trace(current, all_lists[iteration], grid_rows, grid_cols, row_index, col_index)
-        trace_now = lax.psum(diag_term, ("row", "col"))
+        trace_now = lax.psum(lax.psum(diag_term, "col"), "row")
         current = purify_section(
             current, all_lists[iteration], all_lists[iteration + 1], trace_now,
             grid_rows, grid_cols, row_index, col_index,

time: 438 us -> 297 us (0.68)
  Pallas kernels: 153 us -> 46.7 us
  blocking collectives: 153 us -> 130 us
  waiting for transfers between devices: 24.1 us -> 17.4 us
    pallas_call x2, Pallas kernels: 153 us -> 46.7 us  [run_product(): pl.pallas_call(product_kernel, in_specs=[smem] * 6 + [vmem] * 3, out_spec...]
    psum x2 -> x4, blocking collectives: 153 us -> 130 us  [shards(): trace_now = lax.psum(lax.psum(diag_term, 'col'), 'row')]
    ppermute x2, waiting for transfers between devices: 24 us -> 13.9 us  [col_gather(): from_minus = lax.ppermute(x, 'col', plus2)]
    unnamed x28 -> x36, local copies, waits for them, and re-layouts: 22 us -> 25.9 us
  transfers between devices with their start and end apart: 16 -> 16, of which waited for: 2 -> 3; matrix products, arithmetic and copies ran while one was open for 15% -> 22% of each run, Pallas kernels for 0% -> 0%
where the time goes in v2:
time: 297 us; the launch traced here: 294 us
  blocking collectives  130 us (44%)
  local copies, waits for them, and re-layouts  48.6 us (16%)
  Pallas kernels  46.7 us (16%)
  other arithmetic  23 us (8%)
  waiting for transfers between devices  17.4 us (6%)
  between operations  14.9 us (5%)
  starting transfers between devices  14.2 us (5%)
    psum x4, blocking collectives, shards(): trace_now = lax.psum(lax.psum(diag_term, 'col'), 'row')  130 us
    pallas_call x2, Pallas kernels, run_product(): pl.pallas_call(product_kernel, in_specs=[smem] * 6 + [vmem] * 3, out_spec...  46.7 us
    unnamed x36, local copies, waits for them, and re-layouts  25.9 us
    ppermute x2, waiting for transfers between devices, col_gather(): from_minus = lax.ppermute(x, 'col', plus2)  13.9 us
  transfers between devices with their start and end apart: 16, of which 3 were waited for; matrix products, arithmetic and copies ran while one was open for 22% of the time, Pallas kernels for 0%

profile of v2, /device:TPU:0, one launch (start us, length us, event | category | flops | bytes accessed | tf_op | source)
XLA Modules:
  0.0 294.4 jit_solution(12608777826149299486)
XLA Ops:
  6.6 3.3 %bitcast_dynamic-update-slice_fusion.6 = (bf16[8,4,2,256,256]{4,3,2,1,0:T(8,128)(2,1)}, bf16[4,1,2,1,256,256]{5,4,3,2,1,0:T(8,128)(2,1)}) fusion(f32[4,1,2,1,256,256]{5,4,3,2,1,0:T(8,128)} %param.7), kind=kLoop, calls=%fused_computation.25 | loop fusion | flops 524287 | bytes 4194304
  10.0 2.7 bitcast_convert_fusion
  12.6 2.0 collective-permute-start
  14.7 2.1 collective-permute-start.1
  24.2 26.3 %psum.28 = f32[]{:T(128)} all-reduce(f32[]{:T(128)} %select_reduce_fusion.1), channel_id=1, replica_groups=mesh['row'=16,'col'=8] {'col'}, use_global_device_ids=true, to_apply=%region_15.16 | all-reduce | flops 1 | bytes 8 | tf_op jit(solution)/shard_map/psum | solution.py:145
  50.5 2.5 sort.32
  53.8 3.0 %pad_maximum_fusion = bf16[2,4,2,256,256]{4,3,2,1,0:T(8,128)(2,1)} fusion(bf16[1,4,2,256,256]{4,3,2,1,0:T(8,128)(2,1)} %bitcast.28, bf16[1,4,2,256,256]{4,3,2,1,0:T(8,128)(2,1)S(1)} %bitcast.91), kind=kLoop, calls=%fused_computation.13 | loop fusion | flops 1048576 | bytes 4194304 | tf_op jit(solution)/shard_map/stack | solution.py:57
  56.9 0.8 slice.46
  57.7 1.9 slice.47
  59.6 3.2 %collective-permute-start.3 = (bf16[2,2,256,256]{3,2,1,0:T(8,128)(2,1)}, bf16[2,2,256,256]{3,2,1,0:T(8,128)(2,1)}, u32[]{:S(2)}, u32[]{:S(2)}) collective-permute-start(bf16[2,2,256,256]{3,2,1,0:T(8,128)(2,1)} %slice.47), channel_id=1, source_target_pairs={{0,6},{1,7},{2,0},{3,1},{4,2},{5,3},{6,4},{7,5},{8,14},{9,15},{10,... | collective-permute-start | bytes 1572872 | tf_op jit(solution)/shard_map/ppermute | solution.py:55
  62.9 42.8 %psum.29 = f32[]{:T(128)} all-reduce(f32[]{:T(128)} %psum.28), channel_id=1, replica_groups=mesh['row'=16,'col'=8] {'row'}, use_global_device_ids=true, to_apply=%region_16.17 | all-reduce | flops 1 | bytes 8 | tf_op jit(solution)/shard_map/psum | solution.py:145
  106.0 1.2 gather_fusion.10
  107.3 1.2 gather_fusion.11
  108.7 1.2 gather_fusion.9
  111.3 1.1 constant_dynamic-update-slice_fusion.1
  112.4 1.1 constant_dynamic-update-slice_fusion
  113.6 1.1 constant_dynamic-update-slice_fusion.4
  114.7 2.3 constant_dynamic-update-slice_fusion.3
  116.9 1.1 bitcast_dynamic-update-slice_fusion.5
  118.0 2.3 bitcast_dynamic-update-slice_fusion.4
  120.3 3.1 %constant_dynamic-update-slice_fusion.2 = bf16[8,4,2,256,256]{4,3,2,1,0:T(8,128)(2,1)} fusion(bf16[8,4,2,256,256]{4,3,2,1,0:T(8,128)(2,1)} %bitcast_dynamic-update-slice_fusion.4, bf16[2,4,2,256,256]{4,3,2,1,0:T(8,128)(2,1)} %collective-permute-done.5), kind=kLoop, calls=%fused_computation.29 | loop fusion | bytes 4194304
  123.4 1.0 bitcast_dynamic-update-slice_fusion.3
  124.5 1.1 all-gather.6.cloned.1.call-done
  125.6 22.9 %shard_map.46.owned_ref = f32[8,256,256]{2,1,0:T(8,128)S(1)} custom-call(s32[1]{0:T(128)} %bitcast.22.n_ref, s32[128]{0:T(128)S(1)} %gather_fusion.9, s32[128]{0:T(128)S(1)} %gather_fusion.10, s32[128]{0:T(128)S(1)} %gather_fusion.11, s32[8]{0:T(128)S(1)} %reshape.690.prev_ref, s32[1]{0:T(128)} %bitcast.25.misc_ref, bf16[64,256,256]{2,1,0:T(8,128)(2,1)} %bitcast.85, ...), custom_call_target="tpu_custom_call" | custom-call | flops 1073741824 | bytes 29360128 | tf_op jit(solution)/shard_map/pallas_call | solution.py:36
  148.5 1.4 fusion.18
  149.9 1.4 copy-done.1
  151.4 3.2 %collective-permute-start.8 = (bf16[4,2,256,256]{3,2,1,0:T(8,128)(2,1)}, bf16[4,2,256,256]{3,2,1,0:T(8,128)(2,1)S(1)}, u32[]{:S(2)}, u32[]{:S(2)}) collective-permute-start(bf16[4,2,256,256]{3,2,1,0:T(8,128)(2,1)} %bitcast.88), channel_id=1, source_target_pairs={{0,6},{1,7},{2,0},{3,1},{4,2},{5,3},{6,4},{7,5},{8,14},{9,15},{10,... | collective-permute-start | bytes 3145736 | tf_op jit(solution)/shard_map/ppermute | solution.py:52
  156.2 13.9 %collective-permute-done.7 = bf16[4,2,256,256]{3,2,1,0:T(8,128)(2,1)S(1)} collective-permute-done((bf16[4,2,256,256]{3,2,1,0:T(8,128)(2,1)}, bf16[4,2,256,256]{3,2,1,0:T(8,128)(2,1)S(1)}, u32[]{:S(2)}, u32[]{:S(2)}) %collective-permute-start.7) | collective-permute-done | bytes 1048608 | tf_op jit(solution)/shard_map/ppermute | solution.py:51
  170.1 1.6 pad_maximum_fusion.1
  171.9 2.5 sort.31
  175.2 1.2 collective-permute-start.9
  177.3 2.0 collective-permute-start.10
  179.3 1.2 gather_fusion.5
  180.6 1.2 gather_fusion.3
  183.5 1.2 gather_fusion.6
  184.7 17.7 %psum.30 = f32[]{:T(128)} all-reduce(f32[]{:T(128)} %fusion.1), channel_id=1, replica_groups=mesh['row'=16,'col'=8] {'col'}, use_global_device_ids=true, to_apply=%region_19.20 | all-reduce | flops 1 | bytes 8 | tf_op jit(solution)/shard_map/psum | solution.py:145
  202.4 42.8 %psum.31 = f32[]{:T(128)} all-reduce(f32[]{:T(128)} %psum.30), channel_id=1, replica_groups=mesh['row'=16,'col'=8] {'row'}, use_global_device_ids=true, to_apply=%region_20.21 | all-reduce | flops 1 | bytes 8 | tf_op jit(solution)/shard_map/psum | solution.py:145
  245.8 1.1 constant_dynamic-update-slice_fusion.10
  246.9 1.2 constant_dynamic-update-slice_fusion.6
  248.1 1.1 constant_dynamic-update-slice_fusion.5
  249.3 2.3 constant_dynamic-update-slice_fusion.9
  251.6 2.3 constant_dynamic-update-slice_fusion.8
  253.9 1.1 bitcast_dynamic-update-slice_fusion.2
  255.0 2.3 bitcast_dynamic-update-slice_fusion.1
  257.2 3.1 %constant_dynamic-update-slice_fusion.7 = bf16[8,4,2,256,256]{4,3,2,1,0:T(8,128)(2,1)} fusion(bf16[8,4,2,256,256]{4,3,2,1,0:T(8,128)(2,1)} %bitcast_dynamic-update-slice_fusion.1, bf16[2,4,2,256,256]{4,3,2,1,0:T(8,128)(2,1)} %collective-permute-done.12), kind=kLoop, calls=%fused_computation.34 | loop fusion | bytes 4194304
  260.4 1.0 bitcast_dynamic-update-slice_fusion
  261.4 2.3 all-gather.4.cloned.1.call-done
  263.7 23.9 %shard_map.47 = f32[8,256,256]{2,1,0:T(8,128)} custom-call(s32[1]{0:T(128)} %bitcast.6.n_ref, s32[128]{0:T(128)S(1)} %gather_fusion.3, s32[128]{0:T(128)S(1)} %gather_fusion.5, s32[128]{0:T(128)S(1)} %gather_fusion.6, s32[8]{0:T(128)S(1)} %reshape.685.prev_ref, s32[1]{0:T(128)} %bitcast.35.misc_ref, bf16[64,256,256]{2,1,0:T(8,128)(2,1)} %bitcast.43.rows_ref, ...), custom_call_target="tpu_custom_call" | custom-call | flops 1073741824 | bytes 29360128 | tf_op jit(solution)/shard_map/pallas_call | solution.py:36
  (129 shorter events, 14.9 us)
Async XLA Ops:
  6.5 15.4 %copy-start = (f32[4,1,2,1,256,256]{5,4,3,2,1,0:T(8,128)S(1)}, f32[4,1,2,1,256,256]{5,4,3,2,1,0:T(8,128)}, u32[]{:S(2)}) copy-start(f32[4,1,2,1,256,256]{5,4,3,2,1,0:T(8,128)} %param.7) | copy-start | bytes 6291460
  6.5 10.3 %copy-start.7 = (s32[64,16]{0,1:T(8,128)S(1)}, s32[64,16]{0,1:T(8,128)}, u32[]{:S(2)}) copy-start(s32[64,16]{0,1:T(8,128)} %param.5) | copy-start | bytes 12292
  6.5 11.0 %copy-start.6 = (s32[64,16]{0,1:T(8,128)S(1)}, s32[64,16]{0,1:T(8,128)}, u32[]{:S(2)}) copy-start(s32[64,16]{0,1:T(8,128)} %param.4) | copy-start | bytes 12292
  6.5 12.0 %copy-start.8 = (s32[64,16]{0,1:T(8,128)S(1)}, s32[64,16]{0,1:T(8,128)}, u32[]{:S(2)}) copy-start(s32[64,16]{0,1:T(8,128)} %param.6) | copy-start | bytes 12292
  6.5 119.0 %all-gather.6.cloned.1.call-start = ((), (), s32[]{:S(2)}) async-start(), calls=%async_computation.1 | async-start | bytes 17825792 | tf_op jit(solution)/shard_map/all_gather | solution.py:80
  9.9 253.8 %all-gather.4.cloned.1.call-start = ((), (), s32[]{:S(2)}) async-start(), calls=%async_computation | async-start | bytes 17825792 | tf_op jit(solution)/shard_map/all_gather | solution.py:80
  12.6 41.2 %collective-permute-start = (bf16[4,2,256,256]{3,2,1,0:T(8,128)(2,1)}, bf16[4,2,256,256]{3,2,1,0:T(8,128)(2,1)S(1)}, u32[]{:S(2)}, u32[]{:S(2)}) collective-permute-start(bf16[4,2,256,256]{3,2,1,0:T(8,128)(2,1)} %bitcast_convert_fusion), channel_id=1, source_target_pairs={{0,2},{1,3},{2,4},{3,5},{4,6},{5,7},{6,0},{7,1},{8,10},{9,11},{10,... | collective-permute-start | bytes 3145736 | tf_op jit(solution)/shard_map/ppermute | solution.py:51
  14.7 39.2 %collective-permute-start.1 = (bf16[4,2,256,256]{3,2,1,0:T(8,128)(2,1)}, bf16[4,2,256,256]{3,2,1,0:T(8,128)(2,1)}, u32[]{:S(2)}, u32[]{:S(2)}) collective-permute-start(bf16[4,2,256,256]{3,2,1,0:T(8,128)(2,1)} %bitcast_convert_fusion), channel_id=1, source_target_pairs={{0,6},{1,7},{2,0},{3,1},{4,2},{5,3},{6,4},{7,5},{8,14},{9,15},{10,... | collective-permute-start | bytes 3145736 | tf_op jit(solution)/shard_map/ppermute | solution.py:52
  16.8 101.2 %collective-permute-start.4 = (bf16[4,2,256,256]{3,2,1,0:T(8,128)(2,1)}, bf16[4,2,256,256]{3,2,1,0:T(8,128)(2,1)}, u32[]{:S(2)}, u32[]{:S(2)}) collective-permute-start(bf16[4,2,256,256]{3,2,1,0:T(8,128)(2,1)} %bitcast_convert_fusion), channel_id=1, source_target_pairs={{0,1},{1,0},{2,3},{3,2},{4,5},{5,4},{6,7},{7,6},{8,9},{9,8},{10,11... | collective-permute-start | bytes 3145736 | tf_op jit(solution)/shard_map/ppermute | solution.py:53
  56.9 63.4 %collective-permute-start.5 = (bf16[2,4,2,256,256]{4,3,2,1,0:T(8,128)(2,1)}, bf16[2,4,2,256,256]{4,3,2,1,0:T(8,128)(2,1)}, u32[]{:S(2)}, u32[]{:S(2)}) collective-permute-start(bf16[2,4,2,256,256]{4,3,2,1,0:T(8,128)(2,1)} %pad_maximum_fusion), channel_id=1, source_target_pairs={{0,1},{1,0},{2,3},{3,2},{4,5},{5,4},{6,7},{7,6},{8,9},{9,8},{10,11... | collective-permute-start | bytes 6291464 | tf_op jit(solution)/shard_map/ppermute | solution.py:57
  57.7 53.6 %collective-permute-start.2 = (bf16[2,2,256,256]{3,2,1,0:T(8,128)(2,1)}, bf16[2,2,256,256]{3,2,1,0:T(8,128)(2,1)}, u32[]{:S(2)}, u32[]{:S(2)}) collective-permute-start(bf16[2,2,256,256]{3,2,1,0:T(8,128)(2,1)} %slice.46), channel_id=1, source_target_pairs={{0,2},{1,3},{2,4},{3,5},{4,6},{5,7},{6,0},{7,1},{8,10},{9,11},{10,... | collective-permute-start | bytes 1572872 | tf_op jit(solution)/shard_map/ppermute | solution.py:54
  59.6 52.8 %collective-permute-start.3 = (bf16[2,2,256,256]{3,2,1,0:T(8,128)(2,1)}, bf16[2,2,256,256]{3,2,1,0:T(8,128)(2,1)}, u32[]{:S(2)}, u32[]{:S(2)}) collective-permute-start(bf16[2,2,256,256]{3,2,1,0:T(8,128)(2,1)} %slice.47), channel_id=1, source_target_pairs={{0,6},{1,7},{2,0},{3,1},{4,2},{5,3},{6,4},{7,5},{8,14},{9,15},{10,... | collective-permute-start | bytes 1572872 | tf_op jit(solution)/shard_map/ppermute | solution.py:55
  113.5 9.9 %collective-permute-start.6 = (bf16[4,2,256,256]{3,2,1,0:T(8,128)(2,1)S(1)}, bf16[4,2,256,256]{3,2,1,0:T(8,128)(2,1)S(1)}, u32[]{:S(2)}, u32[]{:S(2)}) collective-permute-start(bf16[4,2,256,256]{3,2,1,0:T(8,128)(2,1)S(1)} %constant_dynamic-update-slice_fusion), channel_id=1, source_target_pairs={{0,1},{1,0},{2,3},{3,2},{4,5},{5,4},{6,7},{7,6},{8,9},{9,8},{10,11... | collective-permute-start | bytes 3145736 | tf_op jit(solution)/shard_map/ppermute | solution.py:58
  149.9 1.4 copy-start.1
  151.3 51.1 %copy-start.3 = (bf16[8,256,256]{2,1,0:T(8,128)(2,1)S(1)}, bf16[8,256,256]{2,1,0:T(8,128)(2,1)}, u32[]{:S(2)}) copy-start(bf16[8,256,256]{2,1,0:T(8,128)(2,1)} %get-tuple-element.21) | copy-start | bytes 3145732
  151.3 18.7 %collective-permute-start.7 = (bf16[4,2,256,256]{3,2,1,0:T(8,128)(2,1)}, bf16[4,2,256,256]{3,2,1,0:T(8,128)(2,1)S(1)}, u32[]{:S(2)}, u32[]{:S(2)}) collective-permute-start(bf16[4,2,256,256]{3,2,1,0:T(8,128)(2,1)} %bitcast.87), channel_id=1, source_target_pairs={{0,2},{1,3},{2,4},{3,5},{4,6},{5,7},{6,0},{7,1},{8,10},{9,11},{10,... | collective-permute-start | bytes 3145736 | tf_op jit(solution)/shard_map/ppermute | solution.py:51
  151.4 18.7 %collective-permute-start.8 = (bf16[4,2,256,256]{3,2,1,0:T(8,128)(2,1)}, bf16[4,2,256,256]{3,2,1,0:T(8,128)(2,1)S(1)}, u32[]{:S(2)}, u32[]{:S(2)}) collective-permute-start(bf16[4,2,256,256]{3,2,1,0:T(8,128)(2,1)} %bitcast.88), channel_id=1, source_target_pairs={{0,6},{1,7},{2,0},{3,1},{4,2},{5,3},{6,4},{7,5},{8,14},{9,15},{10,... | collective-permute-start | bytes 3145736 | tf_op jit(solution)/shard_map/ppermute | solution.py:52
  170.0 11.9 %copy-start.4 = (bf16[4,2,256,256]{3,2,1,0:T(8,128)(2,1)}, bf16[4,2,256,256]{3,2,1,0:T(8,128)(2,1)S(1)}, u32[]{:S(2)}) copy-start(bf16[4,2,256,256]{3,2,1,0:T(8,128)(2,1)S(1)} %collective-permute-done.7) | copy-start | bytes 3145732
  170.0 75.8 %copy-start.5 = (bf16[4,2,256,256]{3,2,1,0:T(8,128)(2,1)}, bf16[4,2,256,256]{3,2,1,0:T(8,128)(2,1)S(1)}, u32[]{:S(2)}) copy-start(bf16[4,2,256,256]{3,2,1,0:T(8,128)(2,1)S(1)} %collective-permute-done.8) | copy-start | bytes 3145732
  171.7 85.6 %collective-permute-start.12 = (bf16[2,4,2,256,256]{4,3,2,1,0:T(8,128)(2,1)}, bf16[2,4,2,256,256]{4,3,2,1,0:T(8,128)(2,1)}, u32[]{:S(2)}, u32[]{:S(2)}) collective-permute-start(bf16[2,4,2,256,256]{4,3,2,1,0:T(8,128)(2,1)} %pad_maximum_fusion.1), channel_id=1, source_target_pairs={{0,1},{1,0},{2,3},{3,2},{4,5},{5,4},{6,7},{7,6},{8,9},{9,8},{10,11... | collective-permute-start | bytes 6291464 | tf_op jit(solution)/shard_map/ppermute | solution.py:57
  175.2 71.6 %collective-permute-start.9 = (bf16[2,2,256,256]{3,2,1,0:T(8,128)(2,1)}, bf16[2,2,256,256]{3,2,1,0:T(8,128)(2,1)}, u32[]{:S(2)}, u32[]{:S(2)}) collective-permute-start(bf16[2,2,256,256]{3,2,1,0:T(8,128)(2,1)} %slice.48), channel_id=1, source_target_pairs={{0,2},{1,3},{2,4},{3,5},{4,6},{5,7},{6,0},{7,1},{8,10},{9,11},{10,... | collective-permute-start | bytes 1572872 | tf_op jit(solution)/shard_map/ppermute | solution.py:54
  177.3 70.8 %collective-permute-start.10 = (bf16[2,2,256,256]{3,2,1,0:T(8,128)(2,1)}, bf16[2,2,256,256]{3,2,1,0:T(8,128)(2,1)}, u32[]{:S(2)}, u32[]{:S(2)}) collective-permute-start(bf16[2,2,256,256]{3,2,1,0:T(8,128)(2,1)} %slice.49), channel_id=1, source_target_pairs={{0,6},{1,7},{2,0},{3,1},{4,2},{5,3},{6,4},{7,5},{8,14},{9,15},{10,... | collective-permute-start | bytes 1572872 | tf_op jit(solution)/shard_map/ppermute | solution.py:55
  202.4 52.6 %collective-permute-start.11 = (bf16[4,2,256,256]{3,2,1,0:T(8,128)(2,1)S(1)}, bf16[4,2,256,256]{3,2,1,0:T(8,128)(2,1)}, u32[]{:S(2)}, u32[]{:S(2)}) collective-permute-start(bf16[4,2,256,256]{3,2,1,0:T(8,128)(2,1)S(1)} %bitcast.89), channel_id=1, source_target_pairs={{0,1},{1,0},{2,3},{3,2},{4,5},{5,4},{6,7},{7,6},{8,9},{9,8},{10,11... | collective-permute-start | bytes 3145736 | tf_op jit(solution)/shard_map/ppermute | solution.py:53
  246.9 16.8 %copy-start.2 = (f32[8,256,256]{2,1,0:T(8,128)S(1)}, f32[8,256,256]{2,1,0:T(8,128)}, u32[]{:S(2)}) copy-start(f32[8,256,256]{2,1,0:T(8,128)} %copy-done.1) | copy-start | bytes 6291460
  249.2 11.2 %collective-permute-start.13 = (bf16[4,2,256,256]{3,2,1,0:T(8,128)(2,1)S(1)}, bf16[4,2,256,256]{3,2,1,0:T(8,128)(2,1)S(1)}, u32[]{:S(2)}, u32[]{:S(2)}) collective-permute-start(bf16[4,2,256,256]{3,2,1,0:T(8,128)(2,1)S(1)} %constant_dynamic-update-slice_fusion.5), channel_id=1, source_target_pairs={{0,1},{1,0},{2,3},{3,2},{4,5},{5,4},{6,7},{7,6},{8,9},{9,8},{10,11... | collective-permute-start | bytes 3145736 | tf_op jit(solution)/shard_map/ppermute | solution.py:58
Sparse Core Ops, SparseCore 0:
  10.0 115.5 all-gather.5
  151.4 112.2 all-gather.3

commit v3 on v2

--- a/solution.py
+++ b/solution.py
@@ -8,39 +8,41 @@
 ITERS = 2
 
 
-def product_kernel(n_ref, o_ref, a_ref, b_ref, prev_ref, misc_ref, rows_ref, cols_ref, owned_ref, out_ref):
-    out_ref[...] = jnp.zeros_like(out_ref)
+def product_kernel(a_ref, b_ref, v_ref, prev_ref, misc_ref, rows_ref, cols_ref, owned_ref, out_ref):
+    nout = out_ref.shape[0]
+    terms = a_ref.shape[0] // nout
+    take_product = misc_ref[0] > 0
 
-    def body(t, carry):
-        o = o_ref[t]
-        out_ref[o] += jnp.dot(rows_ref[a_ref[t]], cols_ref[b_ref[t]], preferred_element_type=jnp.float32)
+    def body(o, carry):
+        acc = None
+        for k in range(terms):
+            t = o * terms + k
+            d = jnp.dot(rows_ref[a_ref[t]], cols_ref[b_ref[t]], preferred_element_type=jnp.float32)
+            d = jnp.where(v_ref[t] > 0, d, 0.0)
+            acc = d if acc is None else acc + d
+        p = prev_ref[o]
+        prev = jnp.where(p >= 0, owned_ref[jnp.maximum(p, 0)], 0.0)
+        out_ref[o] = jnp.where(take_product, acc, 2.0 * prev - acc)
         return carry
 
-    lax.fori_loop(0, n_ref[0], body, 0)
-
-    take_product = misc_ref[0] > 0
-    for o in range(out_ref.shape[0]):
-        p = prev_ref[o]
-        prev = jnp.where(p >= 0, owned_ref[jnp.maximum(p, 0)], 0.0)
-        acc = out_ref[o]
-        out_ref[o] = jnp.where(take_product, acc, 2.0 * prev - acc)
+    lax.fori_loop(0, nout, body, 0)
 
 
-def run_product(n, o_t, a_t, b_t, prev_t, misc, rows, cols, owned):
+def run_product(a_t, b_t, v_t, prev_t, misc, rows, cols, owned):
     nout, edge, _ = owned.shape
-    max_terms = o_t.shape[0]
+    max_terms = a_t.shape[0]
     smem = pl.BlockSpec(memory_space=pltpu.SMEM)
     vmem = pl.BlockSpec(memory_space=pltpu.VMEM)
-    flops = 2 * edge * edge * edge * max_terms // 4
+    flops = 2 * edge * edge * edge * max_terms
     nbytes = (rows.size + cols.size) * 2 + 2 * owned.size * 4
     return pl.pallas_call(
         product_kernel,
-        in_specs=[smem] * 6 + [vmem] * 3,
+        in_specs=[smem] * 5 + [vmem] * 3,
         out_specs=vmem,
         out_shape=jax.ShapeDtypeStruct(owned.shape, jnp.float32),
         cost_estimate=pl.CostEstimate(flops=flops, transcendentals=0, bytes_accessed=nbytes),
         compiler_params=pltpu.CompilerParams(vmem_limit_bytes=48 * 1024 * 1024),
-    )(n, o_t, a_t, b_t, prev_t, misc, rows, cols, owned)
+    )(a_t, b_t, v_t, prev_t, misc, rows, cols, owned)
 
 
 def col_gather(x, grid_cols):
@@ -101,14 +103,9 @@
     lsel = jnp.argmax(match, axis=-1).astype(jnp.int32)
     b_idx = ((inner % grid_rows) * block_rows + inner // grid_rows)[:, None, :] * slot_pairs + lsel
     nout = block_rows * slot_pairs
-    o_ids = jnp.broadcast_to(jnp.arange(nout, dtype=jnp.int32).reshape(block_rows, slot_pairs, 1), valid.shape)
-    a_full = jnp.broadcast_to(a_idx[:, None, :], valid.shape)
-    flat_valid = valid.reshape(-1)
-    order = jnp.argsort(jnp.logical_not(flat_valid), stable=True)
-    n_terms = jnp.sum(flat_valid.astype(jnp.int32)).reshape(1)
-    o_t = o_ids.reshape(-1)[order]
-    a_t = a_full.reshape(-1)[order]
-    b_t = b_idx.reshape(-1)[order]
+    a_t = jnp.broadcast_to(a_idx[:, None, :], valid.shape).reshape(-1)
+    b_t = b_idx.reshape(-1)
+    v_t = valid.astype(jnp.int32).reshape(-1)
 
     my_res = my_cur.reshape(block_rows, slot_pairs, grid_cols)[:, :, col_index]
     keep = my_res[:, None, :] == out_cols[:, :, None]
@@ -118,7 +115,7 @@
     ).reshape(-1)
     misc = (trace_now > occupied).astype(jnp.int32).reshape(1)
 
-    updated = run_product(n_terms, o_t, a_t, b_t, prev_t, misc, rows, cols, owned4.reshape(nout, edge, edge))
+    updated = run_product(a_t, b_t, v_t, prev_t, misc, rows, cols, owned4.reshape(nout, edge, edge))
     return updated.reshape(block_rows, 1, slot_pairs, 1, edge, edge)
 
 

time: 297 us -> 279 us (0.939)
  Pallas kernels: 46.7 us -> 29.2 us
  waiting for transfers between devices: 17.4 us -> 26.3 us
  local copies, waits for them, and re-layouts: 48.6 us -> 41.1 us
  other arithmetic: 23 us -> 16.6 us
  blocking collectives: 130 us -> 134 us
    pallas_call x2, Pallas kernels: 46.7 us -> 29.2 us  [run_product(): pl.pallas_call(product_kernel, in_specs=[smem] * 5 + [vmem] * 3, out_spec...]
    ppermute x2, waiting for transfers between devices: 13.9 us -> 22 us  [col_gather(): from_minus = lax.ppermute(x, 'col', plus2)]
    gather x6 -> x0, local copies, waits for them, and re-layouts: 7.36 us -> none  [the longest x2 2.46 us: purify_section(): o_t = o_ids.reshape(-1)[order]]
    sort x2 -> x0, other arithmetic: 5.08 us -> none  [purify_section(): order = jnp.argsort(jnp.logical_not(flat_valid), stable=True)]
    psum x4, blocking collectives: 130 us -> 134 us  [shards(): trace_now = lax.psum(lax.psum(diag_term, 'col'), 'row')]
  transfers between devices with their start and end apart: 16 -> 16, of which waited for: 3 -> 3; matrix products, arithmetic and copies ran while one was open for 22% -> 19% of each run, Pallas kernels for 0% -> 0%
where the time goes in v3:
time: 279 us; the launch traced here: 277 us
  blocking collectives  134 us (48%)
  local copies, waits for them, and re-layouts  41.1 us (15%)
  Pallas kernels  29.2 us (10%)
  waiting for transfers between devices  26.3 us (9%)
  other arithmetic  16.6 us (6%)
  between operations  14.9 us (5%)
  starting transfers between devices  14.2 us (5%)
    psum x4, blocking collectives, shards(): trace_now = lax.psum(lax.psum(diag_term, 'col'), 'row')  134 us
    pallas_call x2, Pallas kernels, run_product(): pl.pallas_call(product_kernel, in_specs=[smem] * 5 + [vmem] * 3, out_spec...  29.2 us
    unnamed x36, local copies, waits for them, and re-layouts  25.9 us
    ppermute x2, waiting for transfers between devices, col_gather(): from_minus = lax.ppermute(x, 'col', plus2)  22 us
  transfers between devices with their start and end apart: 16, of which 3 were waited for; matrix products, arithmetic and copies ran while one was open for 19% of the time, Pallas kernels for 0%

profile of v3, /device:TPU:0, one launch (start us, length us, event | category | flops | bytes accessed | tf_op | source)
XLA Modules:
  0.0 276.6 jit_solution(16854326200469060237)
XLA Ops:
  6.6 3.3 %bitcast_dynamic-update-slice_fusion.6 = (bf16[8,4,2,256,256]{4,3,2,1,0:T(8,128)(2,1)}, bf16[4,1,2,1,256,256]{5,4,3,2,1,0:T(8,128)(2,1)}) fusion(f32[4,1,2,1,256,256]{5,4,3,2,1,0:T(8,128)} %param.7), kind=kLoop, calls=%fused_computation.19 | loop fusion | flops 524287 | bytes 4194304
  10.0 2.7 bitcast_convert_fusion
  12.6 2.0 collective-permute-start
  14.7 2.1 collective-permute-start.1
  20.1 0.7 select_reduce_fusion.1
  21.4 29.1 %psum.28 = f32[]{:T(128)} all-reduce(f32[]{:T(128)} %select_reduce_fusion.1), channel_id=1, replica_groups=mesh['row'=16,'col'=8] {'col'}, use_global_device_ids=true, to_apply=%region_11.12 | all-reduce | flops 1 | bytes 8 | tf_op jit(solution)/shard_map/psum | solution.py:142
  51.9 0.7 gather_fusion
  53.2 0.7 compare_reduce_fusion.1
  53.9 3.0 %pad_maximum_fusion = bf16[2,4,2,256,256]{4,3,2,1,0:T(8,128)(2,1)} fusion(bf16[1,4,2,256,256]{4,3,2,1,0:T(8,128)(2,1)} %bitcast.26, bf16[1,4,2,256,256]{4,3,2,1,0:T(8,128)(2,1)S(1)} %bitcast.89), kind=kLoop, calls=%fused_computation.7 | loop fusion | flops 1048576 | bytes 4194304 | tf_op jit(solution)/shard_map/stack | solution.py:59
  56.9 0.8 slice.34
  57.8 1.9 slice.35
  59.6 3.2 %collective-permute-start.3 = (bf16[2,2,256,256]{3,2,1,0:T(8,128)(2,1)}, bf16[2,2,256,256]{3,2,1,0:T(8,128)(2,1)}, u32[]{:S(2)}, u32[]{:S(2)}) collective-permute-start(bf16[2,2,256,256]{3,2,1,0:T(8,128)(2,1)} %slice.35), channel_id=1, source_target_pairs={{0,6},{1,7},{2,0},{3,1},{4,2},{5,3},{6,4},{7,5},{8,14},{9,15},{10,... | collective-permute-start | bytes 1572872 | tf_op jit(solution)/shard_map/ppermute | solution.py:57
  62.9 42.8 %psum.29 = f32[]{:T(128)} all-reduce(f32[]{:T(128)} %psum.28), channel_id=1, replica_groups=mesh['row'=16,'col'=8] {'row'}, use_global_device_ids=true, to_apply=%region_12.13 | all-reduce | flops 1 | bytes 8 | tf_op jit(solution)/shard_map/psum | solution.py:142
  107.0 1.1 constant_dynamic-update-slice_fusion.1
  108.0 1.1 constant_dynamic-update-slice_fusion
  109.2 1.1 constant_dynamic-update-slice_fusion.4
  110.3 2.3 constant_dynamic-update-slice_fusion.3
  112.6 1.1 bitcast_dynamic-update-slice_fusion.5
  113.7 2.3 bitcast_dynamic-update-slice_fusion.4
  115.9 3.1 %constant_dynamic-update-slice_fusion.2 = bf16[8,4,2,256,256]{4,3,2,1,0:T(8,128)(2,1)} fusion(bf16[8,4,2,256,256]{4,3,2,1,0:T(8,128)(2,1)} %bitcast_dynamic-update-slice_fusion.4, bf16[2,4,2,256,256]{4,3,2,1,0:T(8,128)(2,1)} %collective-permute-done.5), kind=kLoop, calls=%fused_computation.23 | loop fusion | bytes 4194304
  119.1 1.0 bitcast_dynamic-update-slice_fusion.3
  120.1 4.2 %all-gather.6.cloned.1.call-done = bf16[64,1,2,1,256,256]{5,4,3,2,1,0:T(8,128)(2,1)} async-done(((bf16[4,1,2,1,256,256]{5,4,3,2,1,0:T(8,128)(2,1)}), bf16[64,1,2,1,256,256]{5,4,3,2,1,0:T(8,128)(2,1)}) %all-gather.6.cloned.1.call-update) | async-done | bytes 16777232 | tf_op jit(solution)/shard_map/all_gather | solution.py:82
  124.3 13.9 %shard_map.46.owned_ref = f32[8,256,256]{2,1,0:T(8,128)S(1)} custom-call(s32[128]{0:T(128)S(1)} %reshape.645.a_ref, s32[128]{0:T(128)S(1)} %reshape.652.b_ref, s32[128]{0:T(128)S(1)} %reshape.665.v_ref, s32[8]{0:T(128)S(1)} %reshape.654.prev_ref, s32[1]{0:T(128)} %bitcast.23.misc_ref, bf16[64,256,256]{2,1,0:T(8,128)(2,1)} %bitcast.83, ...), custom_call_target="tpu_custom_call" | custom-call | flops 4294967296 | bytes 29360128 | tf_op jit(solution)/shard_map/pallas_call | solution.py:38
  138.3 1.4 fusion.18
  139.7 1.4 copy-done.1
  141.1 1.6 collective-permute-start.7
  142.7 1.7 collective-permute-start.8
  144.6 0.6 gather_fusion.2
  145.3 22.0 %collective-permute-done.7 = bf16[4,2,256,256]{3,2,1,0:T(8,128)(2,1)S(1)} collective-permute-done((bf16[4,2,256,256]{3,2,1,0:T(8,128)(2,1)}, bf16[4,2,256,256]{3,2,1,0:T(8,128)(2,1)S(1)}, u32[]{:S(2)}, u32[]{:S(2)}) %collective-permute-start.7) | collective-permute-done | bytes 1048608 | tf_op jit(solution)/shard_map/ppermute | solution.py:53
  167.4 1.6 pad_maximum_fusion.1
  169.0 0.7 compare_reduce_fusion.3
  169.7 0.8 slice.36
  170.5 1.5 collective-permute-start.9
  172.0 0.8 slice.37
  172.9 1.7 collective-permute-start.10
  175.0 0.7 fusion.1
  175.8 21.9 %psum.30 = f32[]{:T(128)} all-reduce(f32[]{:T(128)} %fusion.1), channel_id=1, replica_groups=mesh['row'=16,'col'=8] {'col'}, use_global_device_ids=true, to_apply=%region_15.16 | all-reduce | flops 1 | bytes 8 | tf_op jit(solution)/shard_map/psum | solution.py:142
  197.7 40.6 %psum.31 = f32[]{:T(128)} all-reduce(f32[]{:T(128)} %psum.30), channel_id=1, replica_groups=mesh['row'=16,'col'=8] {'row'}, use_global_device_ids=true, to_apply=%region_16.17 | all-reduce | flops 1 | bytes 8 | tf_op jit(solution)/shard_map/psum | solution.py:142
  238.9 1.1 constant_dynamic-update-slice_fusion.10
  240.0 1.2 constant_dynamic-update-slice_fusion.6
  241.2 1.1 constant_dynamic-update-slice_fusion.5
  242.4 2.3 constant_dynamic-update-slice_fusion.9
  244.7 2.3 constant_dynamic-update-slice_fusion.8
  247.0 1.1 bitcast_dynamic-update-slice_fusion.2
  248.1 2.3 bitcast_dynamic-update-slice_fusion.1
  250.3 3.1 %constant_dynamic-update-slice_fusion.7 = bf16[8,4,2,256,256]{4,3,2,1,0:T(8,128)(2,1)} fusion(bf16[8,4,2,256,256]{4,3,2,1,0:T(8,128)(2,1)} %bitcast_dynamic-update-slice_fusion.1, bf16[2,4,2,256,256]{4,3,2,1,0:T(8,128)(2,1)} %collective-permute-done.12), kind=kLoop, calls=%fused_computation.28 | loop fusion | bytes 4194304
  253.5 1.0 bitcast_dynamic-update-slice_fusion
  254.5 15.3 %shard_map.47 = f32[8,256,256]{2,1,0:T(8,128)} custom-call(s32[128]{0:T(128)S(1)} %reshape.645.a_ref, s32[128]{0:T(128)S(1)} %reshape.648.b_ref, s32[128]{0:T(128)S(1)} %reshape.664.v_ref, s32[8]{0:T(128)S(1)} %reshape.650.prev_ref, s32[1]{0:T(128)} %bitcast.33.misc_ref, bf16[64,256,256]{2,1,0:T(8,128)(2,1)} %bitcast.41.rows_ref, ...), custom_call_target="tpu_custom_call" | custom-call | flops 4294967296 | bytes 29360128 | tf_op jit(solution)/shard_map/pallas_call | solution.py:38
  (110 shorter events, 7.6 us)
Async XLA Ops:
  6.5 13.2 %copy-start = (f32[4,1,2,1,256,256]{5,4,3,2,1,0:T(8,128)S(1)}, f32[4,1,2,1,256,256]{5,4,3,2,1,0:T(8,128)}, u32[]{:S(2)}) copy-start(f32[4,1,2,1,256,256]{5,4,3,2,1,0:T(8,128)} %param.7) | copy-start | bytes 6291460
  6.5 10.3 %copy-start.7 = (s32[64,16]{0,1:T(8,128)S(1)}, s32[64,16]{0,1:T(8,128)}, u32[]{:S(2)}) copy-start(s32[64,16]{0,1:T(8,128)} %param.5) | copy-start | bytes 12292
  6.5 11.0 %copy-start.6 = (s32[64,16]{0,1:T(8,128)S(1)}, s32[64,16]{0,1:T(8,128)}, u32[]{:S(2)}) copy-start(s32[64,16]{0,1:T(8,128)} %param.4) | copy-start | bytes 12292
  6.5 12.0 %copy-start.8 = (s32[64,16]{0,1:T(8,128)S(1)}, s32[64,16]{0,1:T(8,128)}, u32[]{:S(2)}) copy-start(s32[64,16]{0,1:T(8,128)} %param.6) | copy-start | bytes 12292
  6.5 117.8 %all-gather.6.cloned.1.call-start = ((), (), s32[]{:S(2)}) async-start(), calls=%async_computation.1 | async-start | bytes 17825792 | tf_op jit(solution)/shard_map/all_gather | solution.py:82
  9.9 244.6 %all-gather.4.cloned.1.call-start = ((), (), s32[]{:S(2)}) async-start(), calls=%async_computation | async-start | bytes 17825792 | tf_op jit(solution)/shard_map/all_gather | solution.py:82
  12.6 41.2 %collective-permute-start = (bf16[4,2,256,256]{3,2,1,0:T(8,128)(2,1)}, bf16[4,2,256,256]{3,2,1,0:T(8,128)(2,1)S(1)}, u32[]{:S(2)}, u32[]{:S(2)}) collective-permute-start(bf16[4,2,256,256]{3,2,1,0:T(8,128)(2,1)} %bitcast_convert_fusion), channel_id=1, source_target_pairs={{0,2},{1,3},{2,4},{3,5},{4,6},{5,7},{6,0},{7,1},{8,10},{9,11},{10,... | collective-permute-start | bytes 3145736 | tf_op jit(solution)/shard_map/ppermute | solution.py:53
  14.7 39.2 %collective-permute-start.1 = (bf16[4,2,256,256]{3,2,1,0:T(8,128)(2,1)}, bf16[4,2,256,256]{3,2,1,0:T(8,128)(2,1)}, u32[]{:S(2)}, u32[]{:S(2)}) collective-permute-start(bf16[4,2,256,256]{3,2,1,0:T(8,128)(2,1)} %bitcast_convert_fusion), channel_id=1, source_target_pairs={{0,6},{1,7},{2,0},{3,1},{4,2},{5,3},{6,4},{7,5},{8,14},{9,15},{10,... | collective-permute-start | bytes 3145736 | tf_op jit(solution)/shard_map/ppermute | solution.py:54
  16.8 96.9 %collective-permute-start.4 = (bf16[4,2,256,256]{3,2,1,0:T(8,128)(2,1)}, bf16[4,2,256,256]{3,2,1,0:T(8,128)(2,1)}, u32[]{:S(2)}, u32[]{:S(2)}) collective-permute-start(bf16[4,2,256,256]{3,2,1,0:T(8,128)(2,1)} %bitcast_convert_fusion), channel_id=1, source_target_pairs={{0,1},{1,0},{2,3},{3,2},{4,5},{5,4},{6,7},{7,6},{8,9},{9,8},{10,11... | collective-permute-start | bytes 3145736 | tf_op jit(solution)/shard_map/ppermute | solution.py:55
  56.9 59.0 %collective-permute-start.5 = (bf16[2,4,2,256,256]{4,3,2,1,0:T(8,128)(2,1)}, bf16[2,4,2,256,256]{4,3,2,1,0:T(8,128)(2,1)}, u32[]{:S(2)}, u32[]{:S(2)}) collective-permute-start(bf16[2,4,2,256,256]{4,3,2,1,0:T(8,128)(2,1)} %pad_maximum_fusion), channel_id=1, source_target_pairs={{0,1},{1,0},{2,3},{3,2},{4,5},{5,4},{6,7},{7,6},{8,9},{9,8},{10,11... | collective-permute-start | bytes 6291464 | tf_op jit(solution)/shard_map/ppermute | solution.py:59
  57.8 49.2 %collective-permute-start.2 = (bf16[2,2,256,256]{3,2,1,0:T(8,128)(2,1)}, bf16[2,2,256,256]{3,2,1,0:T(8,128)(2,1)}, u32[]{:S(2)}, u32[]{:S(2)}) collective-permute-start(bf16[2,2,256,256]{3,2,1,0:T(8,128)(2,1)} %slice.34), channel_id=1, source_target_pairs={{0,2},{1,3},{2,4},{3,5},{4,6},{5,7},{6,0},{7,1},{8,10},{9,11},{10,... | collective-permute-start | bytes 1572872 | tf_op jit(solution)/shard_map/ppermute | solution.py:56
  59.6 48.4 %collective-permute-start.3 = (bf16[2,2,256,256]{3,2,1,0:T(8,128)(2,1)}, bf16[2,2,256,256]{3,2,1,0:T(8,128)(2,1)}, u32[]{:S(2)}, u32[]{:S(2)}) collective-permute-start(bf16[2,2,256,256]{3,2,1,0:T(8,128)(2,1)} %slice.35), channel_id=1, source_target_pairs={{0,6},{1,7},{2,0},{3,1},{4,2},{5,3},{6,4},{7,5},{8,14},{9,15},{10,... | collective-permute-start | bytes 1572872 | tf_op jit(solution)/shard_map/ppermute | solution.py:57
  109.1 9.9 %collective-permute-start.6 = (bf16[4,2,256,256]{3,2,1,0:T(8,128)(2,1)S(1)}, bf16[4,2,256,256]{3,2,1,0:T(8,128)(2,1)S(1)}, u32[]{:S(2)}, u32[]{:S(2)}) collective-permute-start(bf16[4,2,256,256]{3,2,1,0:T(8,128)(2,1)S(1)} %constant_dynamic-update-slice_fusion), channel_id=1, source_target_pairs={{0,1},{1,0},{2,3},{3,2},{4,5},{5,4},{6,7},{7,6},{8,9},{9,8},{10,11... | collective-permute-start | bytes 3145736 | tf_op jit(solution)/shard_map/ppermute | solution.py:60
  139.7 1.4 copy-start.1
  141.0 97.9 %copy-start.3 = (bf16[8,256,256]{2,1,0:T(8,128)(2,1)S(1)}, bf16[8,256,256]{2,1,0:T(8,128)(2,1)}, u32[]{:S(2)}) copy-start(bf16[8,256,256]{2,1,0:T(8,128)(2,1)} %get-tuple-element.17) | copy-start | bytes 3145732
  141.1 26.2 %collective-permute-start.7 = (bf16[4,2,256,256]{3,2,1,0:T(8,128)(2,1)}, bf16[4,2,256,256]{3,2,1,0:T(8,128)(2,1)S(1)}, u32[]{:S(2)}, u32[]{:S(2)}) collective-permute-start(bf16[4,2,256,256]{3,2,1,0:T(8,128)(2,1)} %bitcast.85), channel_id=1, source_target_pairs={{0,2},{1,3},{2,4},{3,5},{4,6},{5,7},{6,0},{7,1},{8,10},{9,11},{10,... | collective-permute-start | bytes 3145736 | tf_op jit(solution)/shard_map/ppermute | solution.py:53
  142.7 24.7 %collective-permute-start.8 = (bf16[4,2,256,256]{3,2,1,0:T(8,128)(2,1)}, bf16[4,2,256,256]{3,2,1,0:T(8,128)(2,1)S(1)}, u32[]{:S(2)}, u32[]{:S(2)}) collective-permute-start(bf16[4,2,256,256]{3,2,1,0:T(8,128)(2,1)} %bitcast.86), channel_id=1, source_target_pairs={{0,6},{1,7},{2,0},{3,1},{4,2},{5,3},{6,4},{7,5},{8,14},{9,15},{10,... | collective-permute-start | bytes 3145736 | tf_op jit(solution)/shard_map/ppermute | solution.py:54
  167.3 71.6 %copy-start.4 = (bf16[4,2,256,256]{3,2,1,0:T(8,128)(2,1)}, bf16[4,2,256,256]{3,2,1,0:T(8,128)(2,1)S(1)}, u32[]{:S(2)}) copy-start(bf16[4,2,256,256]{3,2,1,0:T(8,128)(2,1)S(1)} %collective-permute-done.7) | copy-start | bytes 3145732
  167.4 7.2 %copy-start.5 = (bf16[4,2,256,256]{3,2,1,0:T(8,128)(2,1)}, bf16[4,2,256,256]{3,2,1,0:T(8,128)(2,1)S(1)}, u32[]{:S(2)}) copy-start(bf16[4,2,256,256]{3,2,1,0:T(8,128)(2,1)S(1)} %collective-permute-done.8) | copy-start | bytes 3145732
  169.0 81.3 %collective-permute-start.12 = (bf16[2,4,2,256,256]{4,3,2,1,0:T(8,128)(2,1)}, bf16[2,4,2,256,256]{4,3,2,1,0:T(8,128)(2,1)}, u32[]{:S(2)}, u32[]{:S(2)}) collective-permute-start(bf16[2,4,2,256,256]{4,3,2,1,0:T(8,128)(2,1)} %pad_maximum_fusion.1), channel_id=1, source_target_pairs={{0,1},{1,0},{2,3},{3,2},{4,5},{5,4},{6,7},{7,6},{8,9},{9,8},{10,11... | collective-permute-start | bytes 6291464 | tf_op jit(solution)/shard_map/ppermute | solution.py:59
  170.5 69.5 %collective-permute-start.9 = (bf16[2,2,256,256]{3,2,1,0:T(8,128)(2,1)}, bf16[2,2,256,256]{3,2,1,0:T(8,128)(2,1)}, u32[]{:S(2)}, u32[]{:S(2)}) collective-permute-start(bf16[2,2,256,256]{3,2,1,0:T(8,128)(2,1)} %slice.36), channel_id=1, source_target_pairs={{0,2},{1,3},{2,4},{3,5},{4,6},{5,7},{6,0},{7,1},{8,10},{9,11},{10,... | collective-permute-start | bytes 1572872 | tf_op jit(solution)/shard_map/ppermute | solution.py:56
  172.9 68.3 %collective-permute-start.10 = (bf16[2,2,256,256]{3,2,1,0:T(8,128)(2,1)}, bf16[2,2,256,256]{3,2,1,0:T(8,128)(2,1)}, u32[]{:S(2)}, u32[]{:S(2)}) collective-permute-start(bf16[2,2,256,256]{3,2,1,0:T(8,128)(2,1)} %slice.37), channel_id=1, source_target_pairs={{0,6},{1,7},{2,0},{3,1},{4,2},{5,3},{6,4},{7,5},{8,14},{9,15},{10,... | collective-permute-start | bytes 1572872 | tf_op jit(solution)/shard_map/ppermute | solution.py:57
  197.7 50.4 %collective-permute-start.11 = (bf16[4,2,256,256]{3,2,1,0:T(8,128)(2,1)}, bf16[4,2,256,256]{3,2,1,0:T(8,128)(2,1)}, u32[]{:S(2)}, u32[]{:S(2)}) collective-permute-start(bf16[4,2,256,256]{3,2,1,0:T(8,128)(2,1)} %bitcast.87), channel_id=1, source_target_pairs={{0,1},{1,0},{2,3},{3,2},{4,5},{5,4},{6,7},{7,6},{8,9},{9,8},{10,11... | collective-permute-start | bytes 3145736 | tf_op jit(solution)/shard_map/ppermute | solution.py:55
  240.0 14.5 %copy-start.2 = (f32[8,256,256]{2,1,0:T(8,128)S(1)}, f32[8,256,256]{2,1,0:T(8,128)}, u32[]{:S(2)}) copy-start(f32[8,256,256]{2,1,0:T(8,128)} %copy-done.1) | copy-start | bytes 6291460
  242.3 11.2 %collective-permute-start.13 = (bf16[4,2,256,256]{3,2,1,0:T(8,128)(2,1)S(1)}, bf16[4,2,256,256]{3,2,1,0:T(8,128)(2,1)S(1)}, u32[]{:S(2)}, u32[]{:S(2)}) collective-permute-start(bf16[4,2,256,256]{3,2,1,0:T(8,128)(2,1)S(1)} %constant_dynamic-update-slice_fusion.5), channel_id=1, source_target_pairs={{0,1},{1,0},{2,3},{3,2},{4,5},{5,4},{6,7},{7,6},{8,9},{9,8},{10,11... | collective-permute-start | bytes 3145736 | tf_op jit(solution)/shard_map/ppermute | solution.py:60
Sparse Core Ops, SparseCore 0:
  10.0 114.2 all-gather.5
  141.2 111.3 all-gather.3

commit v4 on v3

--- a/solution.py
+++ b/solution.py
@@ -8,21 +8,58 @@
 ITERS = 2
 
 
-def product_kernel(a_ref, b_ref, v_ref, prev_ref, misc_ref, rows_ref, cols_ref, owned_ref, out_ref):
+def product_kernel(a_ref, b_ref, v_ref, prev_ref, misc_ref, rows_hbm, cols_hbm, owned_ref,
+                   out_ref, outb_ref, abuf, bbuf, asem, bsem):
     nout = out_ref.shape[0]
-    terms = a_ref.shape[0] // nout
+    terms = abuf.shape[1]
+    per_row = 2
+    nrows = nout // per_row
     take_product = misc_ref[0] > 0
 
+    def a_copy(i, slot, k):
+        return pltpu.make_async_copy(rows_hbm.at[a_ref[i * per_row * terms + k]], abuf.at[slot, k], asem.at[slot, k])
+
+    def b_copy(o, slot, k):
+        return pltpu.make_async_copy(cols_hbm.at[b_ref[o * terms + k]], bbuf.at[slot, k], bsem.at[slot, k])
+
+    for k in range(terms):
+        a_copy(0, 0, k).start()
+        b_copy(0, 0, k).start()
+
     def body(o, carry):
+        i = o // per_row
+        first = o % per_row == 0
+        aslot = i % 2
+        bslot = o % 2
+
+        @pl.when(first)
+        def _():
+            for k in range(terms):
+                a_copy(i, aslot, k).wait()
+
+            @pl.when(i + 1 < nrows)
+            def _():
+                for k in range(terms):
+                    a_copy(i + 1, 1 - aslot, k).start()
+
+        for k in range(terms):
+            b_copy(o, bslot, k).wait()
+
+        @pl.when(o + 1 < nout)
+        def _():
+            for k in range(terms):
+                b_copy(o + 1, 1 - bslot, k).start()
+
         acc = None
         for k in range(terms):
-            t = o * terms + k
-            d = jnp.dot(rows_ref[a_ref[t]], cols_ref[b_ref[t]], preferred_element_type=jnp.float32)
-            d = jnp.where(v_ref[t] > 0, d, 0.0)
+            d = jnp.dot(abuf[aslot, k], bbuf[bslot, k], preferred_element_type=jnp.float32)
+            d = jnp.where(v_ref[o * terms + k] > 0, d, 0.0)
             acc = d if acc is None else acc + d
         p = prev_ref[o]
         prev = jnp.where(p >= 0, owned_ref[jnp.maximum(p, 0)], 0.0)
-        out_ref[o] = jnp.where(take_product, acc, 2.0 * prev - acc)
+        res = jnp.where(take_product, acc, 2.0 * prev - acc)
+        out_ref[o] = res
+        outb_ref[o] = res.astype(outb_ref.dtype)
         return carry
 
     lax.fori_loop(0, nout, body, 0)
@@ -31,15 +68,26 @@
 def run_product(a_t, b_t, v_t, prev_t, misc, rows, cols, owned):
     nout, edge, _ = owned.shape
     max_terms = a_t.shape[0]
+    terms = max_terms // nout
     smem = pl.BlockSpec(memory_space=pltpu.SMEM)
     vmem = pl.BlockSpec(memory_space=pltpu.VMEM)
+    hbm = pl.BlockSpec(memory_space=pl.ANY)
     flops = 2 * edge * edge * edge * max_terms
-    nbytes = (rows.size + cols.size) * 2 + 2 * owned.size * 4
+    nbytes = (max_terms + max_terms // 2) * edge * edge * 2 + 2 * owned.size * 4
     return pl.pallas_call(
         product_kernel,
-        in_specs=[smem] * 5 + [vmem] * 3,
-        out_specs=vmem,
-        out_shape=jax.ShapeDtypeStruct(owned.shape, jnp.float32),
+        in_specs=[smem] * 5 + [hbm, hbm, vmem],
+        out_specs=(vmem, vmem),
+        out_shape=(
+            jax.ShapeDtypeStruct(owned.shape, jnp.float32),
+            jax.ShapeDtypeStruct(owned.shape, jnp.bfloat16),
+        ),
+        scratch_shapes=[
+            pltpu.VMEM((2, terms, edge, edge), rows.dtype),
+            pltpu.VMEM((2, terms, edge, edge), cols.dtype),
+            pltpu.SemaphoreType.DMA((2, terms)),
+            pltpu.SemaphoreType.DMA((2, terms)),
+        ],
         cost_estimate=pl.CostEstimate(flops=flops, transcendentals=0, bytes_accessed=nbytes),
         compiler_params=pltpu.CompilerParams(vmem_limit_bytes=48 * 1024 * 1024),
     )(a_t, b_t, v_t, prev_t, misc, rows, cols, owned)
@@ -69,7 +117,7 @@
     return offs % grid_cols
 
 
-def purify_section(owned, cur_list, next_list, trace_now, grid_rows, grid_cols, row_index, col_index):
+def purify_section(owned, panels, cur_list, next_list, trace_now, grid_rows, grid_cols, row_index, col_index):
     block_rows = owned.shape[0]
     slot_pairs = owned.shape[2]
     edge = owned.shape[4]
@@ -77,7 +125,7 @@
     slot_count = cur_list.shape[1]
     occupied = total_rows * edge / 2.0
     owned4 = owned.reshape(block_rows, slot_pairs, edge, edge)
-    panels = owned4.astype(jnp.bfloat16)
+    panels = panels.reshape(block_rows, slot_pairs, edge, edge)
 
     cols = lax.all_gather(panels, "row", axis=0, tiled=False)
     cols = cols.reshape(total_rows * slot_pairs, edge, edge)
@@ -115,8 +163,8 @@
     ).reshape(-1)
     misc = (trace_now > occupied).astype(jnp.int32).reshape(1)
 
-    updated = run_product(a_t, b_t, v_t, prev_t, misc, rows, cols, owned4.reshape(nout, edge, edge))
-    return updated.reshape(block_rows, 1, slot_pairs, 1, edge, edge)
+    updated, rounded = run_product(a_t, b_t, v_t, prev_t, misc, rows, cols, owned4.reshape(nout, edge, edge))
+    return updated.reshape(owned.shape), rounded.reshape(owned.shape)
 
 
 def local_trace(owned, cur_list, grid_rows, grid_cols, row_index, col_index):
@@ -137,11 +185,12 @@
     col_index = lax.axis_index("col")
     all_lists = (pattern_in, pattern_mid, pattern_out)
     current = density_blocks
+    rounded = density_blocks.astype(jnp.bfloat16)
     for iteration in range(ITERS):
         diag_term = local_trace(current, all_lists[iteration], grid_rows, grid_cols, row_index, col_index)
         trace_now = lax.psum(lax.psum(diag_term, "col"), "row")
-        current = purify_section(
-            current, all_lists[iteration], all_lists[iteration + 1], trace_now,
+        current, rounded = purify_section(
+            current, rounded, all_lists[iteration], all_lists[iteration + 1], trace_now,
             grid_rows, grid_cols, row_index, col_index,
         )
     return current

time: 279 us -> 287 us (1.029)
  Pallas kernels: 29.2 us -> 34.6 us
  waiting for transfers between devices: 26.3 us -> 30.4 us
  blocking collectives: 134 us -> 130 us
  local copies, waits for them, and re-layouts: 41.1 us -> 45 us
    pallas_call x2, Pallas kernels: 29.2 us -> 34.6 us  [run_product(): pl.pallas_call(product_kernel, in_specs=[smem] * 5 + [hbm, hbm, vmem], ou...]
    all_gather x2, waiting for transfers between devices: 4.19 us -> 9.03 us  [purify_section(): cols = lax.all_gather(panels, 'row', axis=0, tiled=False)]
    psum x4, blocking collectives: 134 us -> 130 us  [shards(): trace_now = lax.psum(lax.psum(diag_term, 'col'), 'row')]
    convert_element_type x2 -> x0, other arithmetic: 4.07 us -> none  [purify_section(): panels = owned4.astype(jnp.bfloat16)]
    unnamed x36 -> x26, local copies, waits for them, and re-layouts: 25.9 us -> 28.1 us
where the time goes in v4:
time: 287 us; the launch traced here: 284 us
  blocking collectives  130 us (45%)
  local copies, waits for them, and re-layouts  45 us (16%)
  Pallas kernels  34.6 us (12%)
  waiting for transfers between devices  30.4 us (11%)
  between operations  14.9 us (5%)
  starting transfers between devices  14.3 us (5%)
  other arithmetic  14.3 us (5%)
    psum x4, blocking collectives, shards(): trace_now = lax.psum(lax.psum(diag_term, 'col'), 'row')  130 us
    pallas_call x2, Pallas kernels, run_product(): pl.pallas_call(product_kernel, in_specs=[smem] * 5 + [hbm, hbm, vmem], ou...  34.6 us
    unnamed x26, local copies, waits for them, and re-layouts  28.1 us
    ppermute x2, waiting for transfers between devices, col_gather(): from_minus = lax.ppermute(x, 'col', plus2)  21.3 us
    all_gather x2, waiting for transfers between devices, purify_section(): cols = lax.all_gather(panels, 'row', axis=0, tiled=False)  9.03 us
  transfers between devices with their start and end apart: 16, of which 3 were waited for; matrix products, arithmetic and copies ran while one was open for 19% of the time, Pallas kernels for 0%

profile of v4, /device:TPU:0, one launch (start us, length us, event | category | flops | bytes accessed | tf_op | source)
XLA Modules:
  0.0 283.9 jit_solution(14429314615675251721)
XLA Ops:
  6.5 3.2 %bitcast_dynamic-update-slice_fusion.6 = (bf16[8,4,2,256,256]{4,3,2,1,0:T(8,128)(2,1)}, bf16[4,1,2,1,256,256]{5,4,3,2,1,0:T(8,128)(2,1)}) fusion(f32[4,1,2,1,256,256]{5,4,3,2,1,0:T(8,128)} %param.7), kind=kLoop, calls=%fused_computation.18 | loop fusion | flops 524287 | bytes 4194304
  9.8 2.1 collective-permute-start
  11.9 2.2 collective-permute-start.1
  14.1 0.8 copy.72
  15.5 0.8 copy.83
  17.2 0.8 copy.76
  18.9 0.7 constant_dynamic-slice_fusion.1
  19.8 1.9 fusion
  21.7 0.7 select_reduce_fusion.1
  23.0 25.1 %psum.28 = f32[]{:T(128)} all-reduce(f32[]{:T(128)} %select_reduce_fusion.1), channel_id=1, replica_groups=mesh['row'=16,'col'=8] {'col'}, use_global_device_ids=true, to_apply=%region_11.12 | all-reduce | flops 1 | bytes 8 | tf_op jit(solution)/shard_map/psum | solution.py:191
  50.8 0.7 compare_reduce_fusion.1
  51.5 1.6 pad_maximum_fusion
  53.2 0.8 slice.34
  54.0 0.8 slice.35
  54.8 3.2 %collective-permute-start.3 = (bf16[2,2,256,256]{3,2,1,0:T(8,128)(2,1)}, bf16[2,2,256,256]{3,2,1,0:T(8,128)(2,1)}, u32[]{:S(2)}, u32[]{:S(2)}) collective-permute-start(bf16[2,2,256,256]{3,2,1,0:T(8,128)(2,1)} %slice.35), channel_id=1, source_target_pairs={{0,6},{1,7},{2,0},{3,1},{4,2},{5,3},{6,4},{7,5},{8,14},{9,15},{10,... | collective-permute-start | bytes 1572872 | tf_op jit(solution)/shard_map/ppermute | solution.py:105
  58.1 42.4 %psum.29 = f32[]{:T(128)} all-reduce(f32[]{:T(128)} %psum.28), channel_id=1, replica_groups=mesh['row'=16,'col'=8] {'row'}, use_global_device_ids=true, to_apply=%region_12.13 | all-reduce | flops 1 | bytes 8 | tf_op jit(solution)/shard_map/psum | solution.py:191
  101.8 1.2 constant_dynamic-update-slice_fusion.1
  103.0 1.1 constant_dynamic-update-slice_fusion
  104.2 1.1 constant_dynamic-update-slice_fusion.4
  105.3 2.3 constant_dynamic-update-slice_fusion.3
  107.6 1.1 bitcast_dynamic-update-slice_fusion.5
  108.6 2.3 bitcast_dynamic-update-slice_fusion.4
  110.9 3.1 %constant_dynamic-update-slice_fusion.2 = bf16[8,4,2,256,256]{4,3,2,1,0:T(8,128)(2,1)} fusion(bf16[8,4,2,256,256]{4,3,2,1,0:T(8,128)(2,1)} %bitcast_dynamic-update-slice_fusion.4, bf16[2,4,2,256,256]{4,3,2,1,0:T(8,128)(2,1)} %collective-permute-done.5), kind=kLoop, calls=%fused_computation.22 | loop fusion | bytes 4194304
  114.1 1.0 bitcast_dynamic-update-slice_fusion.3
  115.1 9.0 %all-gather.6.cloned.1.call-done = bf16[64,1,2,1,256,256]{5,4,3,2,1,0:T(8,128)(2,1)} async-done(((bf16[4,1,2,1,256,256]{5,4,3,2,1,0:T(8,128)(2,1)}), bf16[64,1,2,1,256,256]{5,4,3,2,1,0:T(8,128)(2,1)}) %all-gather.6.cloned.1.call-update) | async-done | bytes 16777232 | tf_op jit(solution)/shard_map/all_gather | solution.py:130
  124.1 16.9 %shard_map.46 = (f32[8,256,256]{2,1,0:T(8,128)S(1)}, bf16[8,256,256]{2,1,0:T(8,128)(2,1)}) custom-call(s32[128]{0:T(128)S(1)} %reshape.624.a_ref, s32[128]{0:T(128)S(1)} %reshape.631.b_ref, s32[128]{0:T(128)S(1)} %reshape.645.v_ref, s32[8]{0:T(128)S(1)} %reshape.633.prev_ref, s32[1]{0:T(128)} %bitcast.23.misc_ref, bf16[64,256,256]{2,1,0:T(8,128)(2,1)} %bitcast.83, ...), custom_call_target="tpu_custom_call" | custom-call | flops 4294967296 | bytes 29360128 | tf_op jit(solution)/shard_map/pallas_call | solution.py:77
  141.1 1.3 copy-done.1
  142.4 1.6 collective-permute-start.7
  144.0 1.7 collective-permute-start.8
  146.8 0.7 compare_reduce_fusion.3
  147.5 21.3 %collective-permute-done.7 = bf16[4,2,256,256]{3,2,1,0:T(8,128)(2,1)} collective-permute-done((bf16[4,2,256,256]{3,2,1,0:T(8,128)(2,1)}, bf16[4,2,256,256]{3,2,1,0:T(8,128)(2,1)}, u32[]{:S(2)}, u32[]{:S(2)}) %collective-permute-start.7) | collective-permute-done | bytes 1048608 | tf_op jit(solution)/shard_map/ppermute | solution.py:101
  168.8 3.1 %pad_maximum_fusion.1 = bf16[2,4,2,256,256]{4,3,2,1,0:T(8,128)(2,1)} fusion(bf16[1,4,2,256,256]{4,3,2,1,0:T(8,128)(2,1)} %bitcast.38, bf16[1,4,2,256,256]{4,3,2,1,0:T(8,128)(2,1)} %bitcast.37), kind=kLoop, calls=%fused_computation.8 | loop fusion | flops 1048576 | bytes 4194304 | tf_op jit(solution)/shard_map/stack | solution.py:107
  172.0 1.9 slice.36
  173.9 1.6 collective-permute-start.9
  175.5 1.9 slice.37
  177.4 1.7 collective-permute-start.10
  179.5 0.7 fusion.1
  180.3 21.9 %psum.30 = f32[]{:T(128)} all-reduce(f32[]{:T(128)} %fusion.1), channel_id=1, replica_groups=mesh['row'=16,'col'=8] {'col'}, use_global_device_ids=true, to_apply=%region_15.16 | all-reduce | flops 1 | bytes 8 | tf_op jit(solution)/shard_map/psum | solution.py:191
  202.2 40.9 %psum.31 = f32[]{:T(128)} all-reduce(f32[]{:T(128)} %psum.30), channel_id=1, replica_groups=mesh['row'=16,'col'=8] {'row'}, use_global_device_ids=true, to_apply=%region_16.17 | all-reduce | flops 1 | bytes 8 | tf_op jit(solution)/shard_map/psum | solution.py:191
  243.7 2.3 constant_dynamic-update-slice_fusion.10
  246.1 1.1 constant_dynamic-update-slice_fusion.5
  247.2 2.3 constant_dynamic-update-slice_fusion.9
  249.6 2.3 constant_dynamic-update-slice_fusion.8
  251.8 1.1 bitcast_dynamic-update-slice_fusion.2
  252.9 2.3 bitcast_dynamic-update-slice_fusion.1
  255.2 3.1 %constant_dynamic-update-slice_fusion.7 = bf16[8,4,2,256,256]{4,3,2,1,0:T(8,128)(2,1)} fusion(bf16[8,4,2,256,256]{4,3,2,1,0:T(8,128)(2,1)} %bitcast_dynamic-update-slice_fusion.1, bf16[2,4,2,256,256]{4,3,2,1,0:T(8,128)(2,1)} %collective-permute-done.12), kind=kLoop, calls=%fused_computation.27 | loop fusion | bytes 4194304
  258.3 1.0 bitcast_dynamic-update-slice_fusion
  259.4 17.6 %shard_map.47 = (f32[8,256,256]{2,1,0:T(8,128)}, bf16[8,256,256]{2,1,0:T(8,128)(2,1)}) custom-call(s32[128]{0:T(128)S(1)} %reshape.624.a_ref, s32[128]{0:T(128)S(1)} %reshape.627.b_ref, s32[128]{0:T(128)S(1)} %reshape.644.v_ref, s32[8]{0:T(128)S(1)} %reshape.629.prev_ref, s32[1]{0:T(128)} %bitcast.34.misc_ref, bf16[64,256,256]{2,1,0:T(8,128)(2,1)} %bitcast.42.rows_hbm, ...), custom_call_target="tpu_custom_call" | custom-call | flops 4294967296 | bytes 29360128 | tf_op jit(solution)/shard_map/pallas_call | solution.py:77
  (99 shorter events, 8.7 us)
Async XLA Ops:
  6.5 117.6 %all-gather.6.cloned.1.call-start = ((), (), s32[]{:S(2)}) async-start(), calls=%async_computation.1 | async-start | bytes 17825792 | tf_op jit(solution)/shard_map/all_gather | solution.py:130
  9.7 249.6 %all-gather.4.cloned.1.call-start = ((), (), s32[]{:S(2)}) async-start(), calls=%async_computation | async-start | bytes 17825792 | tf_op jit(solution)/shard_map/all_gather | solution.py:130
  9.8 41.8 %collective-permute-start = (bf16[4,2,256,256]{3,2,1,0:T(8,128)(2,1)}, bf16[4,2,256,256]{3,2,1,0:T(8,128)(2,1)S(1)}, u32[]{:S(2)}, u32[]{:S(2)}) collective-permute-start(bf16[4,2,256,256]{3,2,1,0:T(8,128)(2,1)} %bitcast.86), channel_id=1, source_target_pairs={{0,2},{1,3},{2,4},{3,5},{4,6},{5,7},{6,0},{7,1},{8,10},{9,11},{10,... | collective-permute-start | bytes 3145736 | tf_op jit(solution)/shard_map/ppermute | solution.py:101
  11.9 39.7 %collective-permute-start.1 = (bf16[4,2,256,256]{3,2,1,0:T(8,128)(2,1)}, bf16[4,2,256,256]{3,2,1,0:T(8,128)(2,1)S(1)}, u32[]{:S(2)}, u32[]{:S(2)}) collective-permute-start(bf16[4,2,256,256]{3,2,1,0:T(8,128)(2,1)} %bitcast.87), channel_id=1, source_target_pairs={{0,6},{1,7},{2,0},{3,1},{4,2},{5,3},{6,4},{7,5},{8,14},{9,15},{10,... | collective-permute-start | bytes 3145736 | tf_op jit(solution)/shard_map/ppermute | solution.py:102
  14.1 94.6 %collective-permute-start.4 = (bf16[4,2,256,256]{3,2,1,0:T(8,128)(2,1)}, bf16[4,2,256,256]{3,2,1,0:T(8,128)(2,1)}, u32[]{:S(2)}, u32[]{:S(2)}) collective-permute-start(bf16[4,2,256,256]{3,2,1,0:T(8,128)(2,1)} %bitcast.88), channel_id=1, source_target_pairs={{0,1},{1,0},{2,3},{3,2},{4,5},{5,4},{6,7},{7,6},{8,9},{9,8},{10,11... | collective-permute-start | bytes 3145736 | tf_op jit(solution)/shard_map/ppermute | solution.py:103
  51.5 49.0 %copy-start.3 = (bf16[4,2,256,256]{3,2,1,0:T(8,128)(2,1)}, bf16[4,2,256,256]{3,2,1,0:T(8,128)(2,1)S(1)}, u32[]{:S(2)}) copy-start(bf16[4,2,256,256]{3,2,1,0:T(8,128)(2,1)S(1)} %collective-permute-done.1) | copy-start | bytes 3145732
  53.2 57.8 %collective-permute-start.5 = (bf16[2,4,2,256,256]{4,3,2,1,0:T(8,128)(2,1)}, bf16[2,4,2,256,256]{4,3,2,1,0:T(8,128)(2,1)}, u32[]{:S(2)}, u32[]{:S(2)}) collective-permute-start(bf16[2,4,2,256,256]{4,3,2,1,0:T(8,128)(2,1)} %pad_maximum_fusion), channel_id=1, source_target_pairs={{0,1},{1,0},{2,3},{3,2},{4,5},{5,4},{6,7},{7,6},{8,9},{9,8},{10,11... | collective-permute-start | bytes 6291464 | tf_op jit(solution)/shard_map/ppermute | solution.py:107
  54.0 47.8 %collective-permute-start.2 = (bf16[2,2,256,256]{3,2,1,0:T(8,128)(2,1)}, bf16[2,2,256,256]{3,2,1,0:T(8,128)(2,1)}, u32[]{:S(2)}, u32[]{:S(2)}) collective-permute-start(bf16[2,2,256,256]{3,2,1,0:T(8,128)(2,1)} %slice.34), channel_id=1, source_target_pairs={{0,2},{1,3},{2,4},{3,5},{4,6},{5,7},{6,0},{7,1},{8,10},{9,11},{10,... | collective-permute-start | bytes 1572872 | tf_op jit(solution)/shard_map/ppermute | solution.py:104
  54.8 48.2 %collective-permute-start.3 = (bf16[2,2,256,256]{3,2,1,0:T(8,128)(2,1)}, bf16[2,2,256,256]{3,2,1,0:T(8,128)(2,1)}, u32[]{:S(2)}, u32[]{:S(2)}) collective-permute-start(bf16[2,2,256,256]{3,2,1,0:T(8,128)(2,1)} %slice.35), channel_id=1, source_target_pairs={{0,6},{1,7},{2,0},{3,1},{4,2},{5,3},{6,4},{7,5},{8,14},{9,15},{10,... | collective-permute-start | bytes 1572872 | tf_op jit(solution)/shard_map/ppermute | solution.py:105
  101.7 22.4 %copy-start = (f32[4,1,2,1,256,256]{5,4,3,2,1,0:T(8,128)S(1)}, f32[4,1,2,1,256,256]{5,4,3,2,1,0:T(8,128)}, u32[]{:S(2)}) copy-start(f32[4,1,2,1,256,256]{5,4,3,2,1,0:T(8,128)} %param.7) | copy-start | bytes 6291460
  104.1 9.9 %collective-permute-start.6 = (bf16[4,2,256,256]{3,2,1,0:T(8,128)(2,1)S(1)}, bf16[4,2,256,256]{3,2,1,0:T(8,128)(2,1)S(1)}, u32[]{:S(2)}, u32[]{:S(2)}) collective-permute-start(bf16[4,2,256,256]{3,2,1,0:T(8,128)(2,1)S(1)} %constant_dynamic-update-slice_fusion), channel_id=1, source_target_pairs={{0,1},{1,0},{2,3},{3,2},{4,5},{5,4},{6,7},{7,6},{8,9},{9,8},{10,11... | collective-permute-start | bytes 3145736 | tf_op jit(solution)/shard_map/ppermute | solution.py:108
  141.1 1.3 copy-start.1
  142.4 36.7 %copy-start.2 = (f32[8,256,256]{2,1,0:T(8,128)S(1)}, f32[8,256,256]{2,1,0:T(8,128)}, u32[]{:S(2)}) copy-start(f32[8,256,256]{2,1,0:T(8,128)} %copy-done.1) | copy-start | bytes 6291460
  142.4 26.3 %collective-permute-start.7 = (bf16[4,2,256,256]{3,2,1,0:T(8,128)(2,1)}, bf16[4,2,256,256]{3,2,1,0:T(8,128)(2,1)}, u32[]{:S(2)}, u32[]{:S(2)}) collective-permute-start(bf16[4,2,256,256]{3,2,1,0:T(8,128)(2,1)} %bitcast.36), channel_id=1, source_target_pairs={{0,2},{1,3},{2,4},{3,5},{4,6},{5,7},{6,0},{7,1},{8,10},{9,11},{10,... | collective-permute-start | bytes 3145736 | tf_op jit(solution)/shard_map/ppermute | solution.py:101
  144.0 24.8 %collective-permute-start.8 = (bf16[4,2,256,256]{3,2,1,0:T(8,128)(2,1)}, bf16[4,2,256,256]{3,2,1,0:T(8,128)(2,1)}, u32[]{:S(2)}, u32[]{:S(2)}) collective-permute-start(bf16[4,2,256,256]{3,2,1,0:T(8,128)(2,1)} %bitcast.36), channel_id=1, source_target_pairs={{0,6},{1,7},{2,0},{3,1},{4,2},{5,3},{6,4},{7,5},{8,14},{9,15},{10,... | collective-permute-start | bytes 3145736 | tf_op jit(solution)/shard_map/ppermute | solution.py:102
  171.9 83.3 %collective-permute-start.12 = (bf16[2,4,2,256,256]{4,3,2,1,0:T(8,128)(2,1)}, bf16[2,4,2,256,256]{4,3,2,1,0:T(8,128)(2,1)}, u32[]{:S(2)}, u32[]{:S(2)}) collective-permute-start(bf16[2,4,2,256,256]{4,3,2,1,0:T(8,128)(2,1)} %pad_maximum_fusion.1), channel_id=1, source_target_pairs={{0,1},{1,0},{2,3},{3,2},{4,5},{5,4},{6,7},{7,6},{8,9},{9,8},{10,11... | collective-permute-start | bytes 6291464 | tf_op jit(solution)/shard_map/ppermute | solution.py:107
  173.9 72.1 %collective-permute-start.9 = (bf16[2,2,256,256]{3,2,1,0:T(8,128)(2,1)}, bf16[2,2,256,256]{3,2,1,0:T(8,128)(2,1)S(1)}, u32[]{:S(2)}, u32[]{:S(2)}) collective-permute-start(bf16[2,2,256,256]{3,2,1,0:T(8,128)(2,1)} %slice.36), channel_id=1, source_target_pairs={{0,2},{1,3},{2,4},{3,5},{4,6},{5,7},{6,0},{7,1},{8,10},{9,11},{10,... | collective-permute-start | bytes 1572872 | tf_op jit(solution)/shard_map/ppermute | solution.py:104
  177.4 68.7 %collective-permute-start.10 = (bf16[2,2,256,256]{3,2,1,0:T(8,128)(2,1)}, bf16[2,2,256,256]{3,2,1,0:T(8,128)(2,1)}, u32[]{:S(2)}, u32[]{:S(2)}) collective-permute-start(bf16[2,2,256,256]{3,2,1,0:T(8,128)(2,1)} %slice.37), channel_id=1, source_target_pairs={{0,6},{1,7},{2,0},{3,1},{4,2},{5,3},{6,4},{7,5},{8,14},{9,15},{10,... | collective-permute-start | bytes 1572872 | tf_op jit(solution)/shard_map/ppermute | solution.py:105
  202.2 50.7 %collective-permute-start.11 = (bf16[4,2,256,256]{3,2,1,0:T(8,128)(2,1)}, bf16[4,2,256,256]{3,2,1,0:T(8,128)(2,1)}, u32[]{:S(2)}, u32[]{:S(2)}) collective-permute-start(bf16[4,2,256,256]{3,2,1,0:T(8,128)(2,1)} %bitcast.36), channel_id=1, source_target_pairs={{0,1},{1,0},{2,3},{3,2},{4,5},{5,4},{6,7},{7,6},{8,9},{9,8},{10,11... | collective-permute-start | bytes 3145736 | tf_op jit(solution)/shard_map/ppermute | solution.py:103
  247.1 11.2 %collective-permute-start.13 = (bf16[4,2,256,256]{3,2,1,0:T(8,128)(2,1)S(1)}, bf16[4,2,256,256]{3,2,1,0:T(8,128)(2,1)S(1)}, u32[]{:S(2)}, u32[]{:S(2)}) collective-permute-start(bf16[4,2,256,256]{3,2,1,0:T(8,128)(2,1)S(1)} %constant_dynamic-update-slice_fusion.5), channel_id=1, source_target_pairs={{0,1},{1,0},{2,3},{3,2},{4,5},{5,4},{6,7},{7,6},{8,9},{9,8},{10,11... | collective-permute-start | bytes 3145736 | tf_op jit(solution)/shard_map/ppermute | solution.py:108
Sparse Core Ops, SparseCore 0:
  9.8 114.2 all-gather.5
  142.5 111.3 all-gather.3

commit v5 on v3

--- a/solution.py
+++ b/solution.py
@@ -8,7 +8,7 @@
 ITERS = 2
 
 
-def product_kernel(a_ref, b_ref, v_ref, prev_ref, misc_ref, rows_ref, cols_ref, owned_ref, out_ref):
+def product_kernel(a_ref, b_ref, v_ref, prev_ref, misc_ref, rows_ref, cols_ref, owned_ref, out_ref, outb_ref):
     nout = out_ref.shape[0]
     terms = a_ref.shape[0] // nout
     take_product = misc_ref[0] > 0
@@ -22,7 +22,9 @@
             acc = d if acc is None else acc + d
         p = prev_ref[o]
         prev = jnp.where(p >= 0, owned_ref[jnp.maximum(p, 0)], 0.0)
-        out_ref[o] = jnp.where(take_product, acc, 2.0 * prev - acc)
+        res = jnp.where(take_product, acc, 2.0 * prev - acc)
+        out_ref[o] = res
+        outb_ref[o] = res.astype(outb_ref.dtype)
         return carry
 
     lax.fori_loop(0, nout, body, 0)
@@ -38,8 +40,11 @@
     return pl.pallas_call(
         product_kernel,
         in_specs=[smem] * 5 + [vmem] * 3,
-        out_specs=vmem,
-        out_shape=jax.ShapeDtypeStruct(owned.shape, jnp.float32),
+        out_specs=(vmem, vmem),
+        out_shape=(
+            jax.ShapeDtypeStruct(owned.shape, jnp.float32),
+            jax.ShapeDtypeStruct(owned.shape, jnp.bfloat16),
+        ),
         cost_estimate=pl.CostEstimate(flops=flops, transcendentals=0, bytes_accessed=nbytes),
         compiler_params=pltpu.CompilerParams(vmem_limit_bytes=48 * 1024 * 1024),
     )(a_t, b_t, v_t, prev_t, misc, rows, cols, owned)
@@ -69,7 +74,7 @@
     return offs % grid_cols
 
 
-def purify_section(owned, cur_list, next_list, trace_now, grid_rows, grid_cols, row_index, col_index):
+def purify_section(owned, panels, cur_list, next_list, trace_now, grid_rows, grid_cols, row_index, col_index):
     block_rows = owned.shape[0]
     slot_pairs = owned.shape[2]
     edge = owned.shape[4]
@@ -77,7 +82,7 @@
     slot_count = cur_list.shape[1]
     occupied = total_rows * edge / 2.0
     owned4 = owned.reshape(block_rows, slot_pairs, edge, edge)
-    panels = owned4.astype(jnp.bfloat16)
+    panels = panels.reshape(block_rows, slot_pairs, edge, edge)
 
     cols = lax.all_gather(panels, "row", axis=0, tiled=False)
     cols = cols.reshape(total_rows * slot_pairs, edge, edge)
@@ -115,8 +120,8 @@
     ).reshape(-1)
     misc = (trace_now > occupied).astype(jnp.int32).reshape(1)
 
-    updated = run_product(a_t, b_t, v_t, prev_t, misc, rows, cols, owned4.reshape(nout, edge, edge))
-    return updated.reshape(block_rows, 1, slot_pairs, 1, edge, edge)
+    updated, rounded = run_product(a_t, b_t, v_t, prev_t, misc, rows, cols, owned4.reshape(nout, edge, edge))
+    return updated.reshape(owned.shape), rounded.reshape(owned.shape)
 
 
 def local_trace(owned, cur_list, grid_rows, grid_cols, row_index, col_index):
@@ -137,11 +142,18 @@
     col_index = lax.axis_index("col")
     all_lists = (pattern_in, pattern_mid, pattern_out)
     current = density_blocks
+    rounded = density_blocks.astype(jnp.bfloat16)
+    occupied = pattern_in.shape[0] * density_blocks.shape[-1] / 2.0
+    diag_term = local_trace(current, pattern_in, grid_rows, grid_cols, row_index, col_index)
+    wide = rounded.astype(jnp.float32)
+    square_term = jnp.sum(wide * wide)
+    totals = lax.psum(lax.psum(jnp.stack([diag_term, square_term]), "col"), "row")
+    first_trace = totals[0]
+    second_trace = jnp.where(first_trace > occupied, totals[1], 2.0 * first_trace - totals[1])
+    traces = (first_trace, second_trace)
     for iteration in range(ITERS):
-        diag_term = local_trace(current, all_lists[iteration], grid_rows, grid_cols, row_index, col_index)
-        trace_now = lax.psum(lax.psum(diag_term, "col"), "row")
-        current = purify_section(
-            current, all_lists[iteration], all_lists[iteration + 1], trace_now,
+        current, rounded = purify_section(
+            current, rounded, all_lists[iteration], all_lists[iteration + 1], traces[iteration],
             grid_rows, grid_cols, row_index, col_index,
         )
     return current

time: 279 us -> 275 us (0.986)
  blocking collectives: 134 us -> 57.9 us
  waiting for transfers between devices: 26.3 us -> 96.6 us
    psum x4 -> x2, blocking collectives: 134 us -> 57.9 us  [the longest x1 42.4 us: shards(): lax.psum(lax.psum(jnp.stack([diag_term, square_term]), 'col'), 'row')]
    all_gather x2, waiting for transfers between devices: 4.19 us -> 53.4 us  [purify_section(): cols = lax.all_gather(panels, 'row', axis=0, tiled=False)]
    ppermute x2, waiting for transfers between devices: 22 us -> 30.1 us  [col_gather(): from_minus = lax.ppermute(x, 'col', plus2)]
    ppermute x2, waiting for transfers between devices: 0.01 us -> 6.67 us  [col_gather(): far_b = lax.ppermute(from_plus[half:], 'col', minus2)]
    ppermute x2, waiting for transfers between devices: 0.01 us -> 6.36 us  [col_gather(): far_a = lax.ppermute(from_minus[:half], 'col', plus2)]
    convert_element_type x2 -> x0, other arithmetic: 4.07 us -> none  [purify_section(): panels = owned4.astype(jnp.bfloat16)]
    unnamed x36 -> x30, local copies, waits for them, and re-layouts: 25.9 us -> 28.2 us
  transfers between devices with their start and end apart: 16 -> 16, of which waited for: 3 -> 7; matrix products, arithmetic and copies ran while one was open for 19% -> 20% of each run, Pallas kernels for 0% -> 0%
where the time goes in v5:
time: 275 us; the launch traced here: 274 us
  waiting for transfers between devices  96.6 us (35%)
  blocking collectives  57.9 us (21%)
  local copies, waits for them, and re-layouts  42.5 us (15%)
  Pallas kernels  30.6 us (11%)
  between operations  16.3 us (6%)
  other arithmetic  15.5 us (6%)
  starting transfers between devices  14.3 us (5%)
    all_gather x2, waiting for transfers between devices, purify_section(): cols = lax.all_gather(panels, 'row', axis=0, tiled=False)  53.4 us
    psum x1, blocking collectives, shards(): lax.psum(lax.psum(jnp.stack([diag_term, square_term]), 'col'), 'row')  42.4 us
    pallas_call x2, Pallas kernels, run_product(): pl.pallas_call(product_kernel, in_specs=[smem] * 5 + [vmem] * 3, out_spec...  30.6 us
    ppermute x2, waiting for transfers between devices, col_gather(): from_minus = lax.ppermute(x, 'col', plus2)  30.1 us
    unnamed x30, local copies, waits for them, and re-layouts  28.2 us
    psum x1, blocking collectives, shards(): lax.psum(jnp.stack([diag_term, square_term]), 'col')  15.5 us
    ppermute x2, waiting for transfers between devices, col_gather(): far_b = lax.ppermute(from_plus[half:], 'col', minus2)  6.67 us
    ppermute x2, waiting for transfers between devices, col_gather(): far_a = lax.ppermute(from_minus[:half], 'col', plus2)  6.36 us
  transfers between devices with their start and end apart: 16, of which 7 were waited for; matrix products, arithmetic and copies ran while one was open for 20% of the time, Pallas kernels for 0%

profile of v5, /device:TPU:0, one launch (start us, length us, event | category | flops | bytes accessed | tf_op | source)
XLA Modules:
  0.0 273.9 jit_solution(15273576021162384632)
XLA Ops:
  6.5 3.2 %bitcast_dynamic-update-slice_fusion.6 = (bf16[8,4,2,256,256]{4,3,2,1,0:T(8,128)(2,1)}, bf16[4,1,2,1,256,256]{5,4,3,2,1,0:T(8,128)(2,1)}) fusion(f32[4,1,2,1,256,256]{5,4,3,2,1,0:T(8,128)} %param.7), kind=kLoop, calls=%fused_computation.18 | loop fusion | flops 524287 | bytes 4194304
  9.8 2.1 collective-permute-start
  11.9 2.2 collective-permute-start.1
  14.1 0.8 copy.69
  15.5 0.8 copy.80
  17.2 0.8 copy.73
  19.8 1.9 fusion
  22.4 2.5 multiply_reduce_fusion
  25.4 1.3 pad_maximum_fusion.2
  30.1 7.2 %collective-permute-done = bf16[4,2,256,256]{3,2,1,0:T(8,128)(2,1)S(1)} collective-permute-done((bf16[4,2,256,256]{3,2,1,0:T(8,128)(2,1)}, bf16[4,2,256,256]{3,2,1,0:T(8,128)(2,1)S(1)}, u32[]{:S(2)}, u32[]{:S(2)}) %collective-permute-start) | collective-permute-done | bytes 1048608 | tf_op jit(solution)/shard_map/ppermute | solution.py:58
  37.4 1.6 pad_maximum_fusion
  39.0 15.5 %psum.14 = f32[2]{0:T(128)S(1)} all-reduce(f32[2]{0:T(128)S(1)} %pad_maximum_fusion.2), channel_id=1, replica_groups=mesh['row'=16,'col'=8] {'col'}, use_global_device_ids=true, to_apply=%region_8.9 | all-reduce | flops 2 | bytes 16 | tf_op jit(solution)/shard_map/psum | solution.py:150
  54.5 0.8 slice.43
  55.4 42.4 %psum.15 = f32[2]{0:T(128)S(1)} all-reduce(f32[2]{0:T(128)S(1)} %psum.14), channel_id=1, replica_groups=mesh['row'=16,'col'=8] {'row'}, use_global_device_ids=true, to_apply=%region_9.10 | all-reduce | flops 2 | bytes 16 | tf_op jit(solution)/shard_map/psum | solution.py:150
  98.1 0.9 slice.44
  98.9 3.2 %collective-permute-start.3 = (bf16[2,2,256,256]{3,2,1,0:T(8,128)(2,1)}, bf16[2,2,256,256]{3,2,1,0:T(8,128)(2,1)}, u32[]{:S(2)}, u32[]{:S(2)}) collective-permute-start(bf16[2,2,256,256]{3,2,1,0:T(8,128)(2,1)} %slice.44), channel_id=1, source_target_pairs={{0,6},{1,7},{2,0},{3,1},{4,2},{5,3},{6,4},{7,5},{8,14},{9,15},{10,... | collective-permute-start | bytes 1572872 | tf_op jit(solution)/shard_map/ppermute | solution.py:62
  103.7 1.2 constant_dynamic-update-slice_fusion.1
  105.0 4.1 %collective-permute-done.3 = bf16[2,2,256,256]{3,2,1,0:T(8,128)(2,1)} collective-permute-done((bf16[2,2,256,256]{3,2,1,0:T(8,128)(2,1)}, bf16[2,2,256,256]{3,2,1,0:T(8,128)(2,1)}, u32[]{:S(2)}, u32[]{:S(2)}) %collective-permute-start.3) | collective-permute-done | bytes 524320 | tf_op jit(solution)/shard_map/ppermute | solution.py:62
  109.1 1.1 constant_dynamic-update-slice_fusion
  110.3 1.1 constant_dynamic-update-slice_fusion.4
  111.4 2.3 constant_dynamic-update-slice_fusion.3
  113.7 1.1 bitcast_dynamic-update-slice_fusion.5
  114.7 2.3 bitcast_dynamic-update-slice_fusion.4
  117.0 3.1 %constant_dynamic-update-slice_fusion.2 = bf16[8,4,2,256,256]{4,3,2,1,0:T(8,128)(2,1)} fusion(bf16[8,4,2,256,256]{4,3,2,1,0:T(8,128)(2,1)} %bitcast_dynamic-update-slice_fusion.4, bf16[2,4,2,256,256]{4,3,2,1,0:T(8,128)(2,1)} %collective-permute-done.5), kind=kLoop, calls=%fused_computation.22 | loop fusion | bytes 4194304
  120.1 1.0 bitcast_dynamic-update-slice_fusion.3
  121.2 3.0 %all-gather.6.cloned.1.call-done = bf16[64,1,2,1,256,256]{5,4,3,2,1,0:T(8,128)(2,1)} async-done(((bf16[4,1,2,1,256,256]{5,4,3,2,1,0:T(8,128)(2,1)}), bf16[64,1,2,1,256,256]{5,4,3,2,1,0:T(8,128)(2,1)}) %all-gather.6.cloned.1.call-update) | async-done | bytes 16777232 | tf_op jit(solution)/shard_map/all_gather | solution.py:87
  124.1 15.0 %shard_map.46 = (f32[8,256,256]{2,1,0:T(8,128)S(1)}, bf16[8,256,256]{2,1,0:T(8,128)(2,1)}) custom-call(s32[128]{0:T(128)S(1)} %reshape.618.a_ref, s32[128]{0:T(128)S(1)} %reshape.628.b_ref, s32[128]{0:T(128)S(1)} %reshape.640.v_ref, s32[8]{0:T(128)S(1)} %reshape.629.prev_ref, s32[1]{0:T(128)S(6)} %reshape.630.misc_ref, bf16[64,256,256]{2,1,0:T(8,128)(2,1)} %bitcast.87, ...), custom_call_target="tpu_custom_call" | custom-call | flops 4294967296 | bytes 29360128 | tf_op jit(solution)/shard_map/pallas_call | solution.py:40
  139.1 1.4 copy-done.1
  140.5 1.6 collective-permute-start.7
  142.1 1.7 collective-permute-start.8
  143.9 22.9 %collective-permute-done.7 = bf16[4,2,256,256]{3,2,1,0:T(8,128)(2,1)S(1)} collective-permute-done((bf16[4,2,256,256]{3,2,1,0:T(8,128)(2,1)}, bf16[4,2,256,256]{3,2,1,0:T(8,128)(2,1)S(1)}, u32[]{:S(2)}, u32[]{:S(2)}) %collective-permute-start.7) | collective-permute-done | bytes 1048608 | tf_op jit(solution)/shard_map/ppermute | solution.py:58
  166.8 1.6 pad_maximum_fusion.1
  169.2 0.8 slice.45
  170.0 1.6 collective-permute-start.9
  174.6 0.8 slice.46
  175.4 1.6 collective-permute-start.10
  177.4 2.3 constant_dynamic-update-slice_fusion.10
  179.7 6.4 %collective-permute-done.9 = bf16[2,2,256,256]{3,2,1,0:T(8,128)(2,1)} collective-permute-done((bf16[2,2,256,256]{3,2,1,0:T(8,128)(2,1)}, bf16[2,2,256,256]{3,2,1,0:T(8,128)(2,1)}, u32[]{:S(2)}, u32[]{:S(2)}) %collective-permute-start.9) | collective-permute-done | bytes 524320 | tf_op jit(solution)/shard_map/ppermute | solution.py:61
  186.0 1.1 constant_dynamic-update-slice_fusion.6
  187.1 2.6 collective-permute-done.10
  189.8 2.4 constant_dynamic-update-slice_fusion.9
  192.2 2.3 constant_dynamic-update-slice_fusion.8
  194.5 1.1 bitcast_dynamic-update-slice_fusion.2
  195.6 1.0 bitcast_dynamic-update-slice_fusion.1
  196.6 3.2 %constant_dynamic-update-slice_fusion.7 = bf16[8,4,2,256,256]{4,3,2,1,0:T(8,128)(2,1)} fusion(bf16[8,4,2,256,256]{4,3,2,1,0:T(8,128)(2,1)} %bitcast_dynamic-update-slice_fusion.1, bf16[2,4,2,256,256]{4,3,2,1,0:T(8,128)(2,1)} %collective-permute-done.12), kind=kLoop, calls=%fused_computation.27 | loop fusion | bytes 4194304
  199.8 1.0 bitcast_dynamic-update-slice_fusion
  200.9 50.5 %all-gather.4.cloned.1.call-done = bf16[16,4,2,256,256]{4,3,2,1,0:T(8,128)(2,1)} async-done(((bf16[1,4,2,256,256]{4,3,2,1,0:T(8,128)(2,1)}), bf16[16,4,2,256,256]{4,3,2,1,0:T(8,128)(2,1)}) %all-gather.4.cloned.1.call-update) | async-done | bytes 16777232 | tf_op jit(solution)/shard_map/all_gather | solution.py:87
  251.4 15.7 %shard_map.47 = (f32[8,256,256]{2,1,0:T(8,128)}, bf16[8,256,256]{2,1,0:T(8,128)(2,1)}) custom-call(s32[128]{0:T(128)S(1)} %reshape.618.a_ref, s32[128]{0:T(128)S(1)} %reshape.621.b_ref, s32[128]{0:T(128)S(1)} %reshape.637.v_ref, s32[8]{0:T(128)S(1)} %reshape.623.prev_ref, s32[1]{0:T(128)} %bitcast.24.misc_ref, bf16[64,256,256]{2,1,0:T(8,128)(2,1)} %bitcast.46.rows_ref, ...), custom_call_target="tpu_custom_call" | custom-call | flops 4294967296 | bytes 29360128 | tf_op jit(solution)/shard_map/pallas_call | solution.py:40
  (101 shorter events, 11.6 us)
Async XLA Ops:
  6.5 117.6 %all-gather.6.cloned.1.call-start = ((), (), s32[]{:S(2)}) async-start(), calls=%async_computation.1 | async-start | bytes 17825792 | tf_op jit(solution)/shard_map/all_gather | solution.py:87
  9.7 241.6 %all-gather.4.cloned.1.call-start = ((), (), s32[]{:S(2)}) async-start(), calls=%async_computation | async-start | bytes 17825792 | tf_op jit(solution)/shard_map/all_gather | solution.py:87
  9.8 27.6 %collective-permute-start = (bf16[4,2,256,256]{3,2,1,0:T(8,128)(2,1)}, bf16[4,2,256,256]{3,2,1,0:T(8,128)(2,1)S(1)}, u32[]{:S(2)}, u32[]{:S(2)}) collective-permute-start(bf16[4,2,256,256]{3,2,1,0:T(8,128)(2,1)} %bitcast.88), channel_id=1, source_target_pairs={{0,2},{1,3},{2,4},{3,5},{4,6},{5,7},{6,0},{7,1},{8,10},{9,11},{10,... | collective-permute-start | bytes 3145736 | tf_op jit(solution)/shard_map/ppermute | solution.py:58
  11.9 25.5 %collective-permute-start.1 = (bf16[4,2,256,256]{3,2,1,0:T(8,128)(2,1)}, bf16[4,2,256,256]{3,2,1,0:T(8,128)(2,1)S(1)}, u32[]{:S(2)}, u32[]{:S(2)}) collective-permute-start(bf16[4,2,256,256]{3,2,1,0:T(8,128)(2,1)} %bitcast.89), channel_id=1, source_target_pairs={{0,6},{1,7},{2,0},{3,1},{4,2},{5,3},{6,4},{7,5},{8,14},{9,15},{10,... | collective-permute-start | bytes 3145736 | tf_op jit(solution)/shard_map/ppermute | solution.py:59
  14.1 100.6 %collective-permute-start.4 = (bf16[4,2,256,256]{3,2,1,0:T(8,128)(2,1)}, bf16[4,2,256,256]{3,2,1,0:T(8,128)(2,1)}, u32[]{:S(2)}, u32[]{:S(2)}) collective-permute-start(bf16[4,2,256,256]{3,2,1,0:T(8,128)(2,1)} %bitcast.90), channel_id=1, source_target_pairs={{0,1},{1,0},{2,3},{3,2},{4,5},{5,4},{6,7},{7,6},{8,9},{9,8},{10,11... | collective-permute-start | bytes 3145736 | tf_op jit(solution)/shard_map/ppermute | solution.py:60
  37.4 64.7 %copy-start.3 = (bf16[4,2,256,256]{3,2,1,0:T(8,128)(2,1)}, bf16[4,2,256,256]{3,2,1,0:T(8,128)(2,1)S(1)}, u32[]{:S(2)}) copy-start(bf16[4,2,256,256]{3,2,1,0:T(8,128)(2,1)S(1)} %collective-permute-done.1) | copy-start | bytes 3145732
  39.0 78.0 %collective-permute-start.5 = (bf16[2,4,2,256,256]{4,3,2,1,0:T(8,128)(2,1)}, bf16[2,4,2,256,256]{4,3,2,1,0:T(8,128)(2,1)}, u32[]{:S(2)}, u32[]{:S(2)}) collective-permute-start(bf16[2,4,2,256,256]{4,3,2,1,0:T(8,128)(2,1)} %pad_maximum_fusion), channel_id=1, source_target_pairs={{0,1},{1,0},{2,3},{3,2},{4,5},{5,4},{6,7},{7,6},{8,9},{9,8},{10,11... | collective-permute-start | bytes 6291464 | tf_op jit(solution)/shard_map/ppermute | solution.py:64
  55.4 48.4 %collective-permute-start.2 = (bf16[2,2,256,256]{3,2,1,0:T(8,128)(2,1)}, bf16[2,2,256,256]{3,2,1,0:T(8,128)(2,1)}, u32[]{:S(2)}, u32[]{:S(2)}) collective-permute-start(bf16[2,2,256,256]{3,2,1,0:T(8,128)(2,1)} %slice.43), channel_id=1, source_target_pairs={{0,2},{1,3},{2,4},{3,5},{4,6},{5,7},{6,0},{7,1},{8,10},{9,11},{10,... | collective-permute-start | bytes 1572872 | tf_op jit(solution)/shard_map/ppermute | solution.py:61
  98.9 10.2 %collective-permute-start.3 = (bf16[2,2,256,256]{3,2,1,0:T(8,128)(2,1)}, bf16[2,2,256,256]{3,2,1,0:T(8,128)(2,1)}, u32[]{:S(2)}, u32[]{:S(2)}) collective-permute-start(bf16[2,2,256,256]{3,2,1,0:T(8,128)(2,1)} %slice.44), channel_id=1, source_target_pairs={{0,6},{1,7},{2,0},{3,1},{4,2},{5,3},{6,4},{7,5},{8,14},{9,15},{10,... | collective-permute-start | bytes 1572872 | tf_op jit(solution)/shard_map/ppermute | solution.py:62
  103.7 20.4 %copy-start = (f32[4,1,2,1,256,256]{5,4,3,2,1,0:T(8,128)S(1)}, f32[4,1,2,1,256,256]{5,4,3,2,1,0:T(8,128)}, u32[]{:S(2)}) copy-start(f32[4,1,2,1,256,256]{5,4,3,2,1,0:T(8,128)} %param.7) | copy-start | bytes 6291460
  110.2 9.9 %collective-permute-start.6 = (bf16[4,2,256,256]{3,2,1,0:T(8,128)(2,1)S(1)}, bf16[4,2,256,256]{3,2,1,0:T(8,128)(2,1)S(1)}, u32[]{:S(2)}, u32[]{:S(2)}) collective-permute-start(bf16[4,2,256,256]{3,2,1,0:T(8,128)(2,1)S(1)} %constant_dynamic-update-slice_fusion), channel_id=1, source_target_pairs={{0,1},{1,0},{2,3},{3,2},{4,5},{5,4},{6,7},{7,6},{8,9},{9,8},{10,11... | collective-permute-start | bytes 3145736 | tf_op jit(solution)/shard_map/ppermute | solution.py:65
  139.1 1.4 copy-start.1
  140.5 26.3 %collective-permute-start.7 = (bf16[4,2,256,256]{3,2,1,0:T(8,128)(2,1)}, bf16[4,2,256,256]{3,2,1,0:T(8,128)(2,1)S(1)}, u32[]{:S(2)}, u32[]{:S(2)}) collective-permute-start(bf16[4,2,256,256]{3,2,1,0:T(8,128)(2,1)} %bitcast.40), channel_id=1, source_target_pairs={{0,2},{1,3},{2,4},{3,5},{4,6},{5,7},{6,0},{7,1},{8,10},{9,11},{10,... | collective-permute-start | bytes 3145736 | tf_op jit(solution)/shard_map/ppermute | solution.py:58
  142.1 24.7 %collective-permute-start.8 = (bf16[4,2,256,256]{3,2,1,0:T(8,128)(2,1)}, bf16[4,2,256,256]{3,2,1,0:T(8,128)(2,1)S(1)}, u32[]{:S(2)}, u32[]{:S(2)}) collective-permute-start(bf16[4,2,256,256]{3,2,1,0:T(8,128)(2,1)} %bitcast.40), channel_id=1, source_target_pairs={{0,6},{1,7},{2,0},{3,1},{4,2},{5,3},{6,4},{7,5},{8,14},{9,15},{10,... | collective-permute-start | bytes 3145736 | tf_op jit(solution)/shard_map/ppermute | solution.py:59
  166.8 5.6 %copy-start.4 = (bf16[4,2,256,256]{3,2,1,0:T(8,128)(2,1)}, bf16[4,2,256,256]{3,2,1,0:T(8,128)(2,1)S(1)}, u32[]{:S(2)}) copy-start(bf16[4,2,256,256]{3,2,1,0:T(8,128)(2,1)S(1)} %collective-permute-done.7) | copy-start | bytes 3145732
  166.8 10.6 %copy-start.5 = (bf16[4,2,256,256]{3,2,1,0:T(8,128)(2,1)}, bf16[4,2,256,256]{3,2,1,0:T(8,128)(2,1)S(1)}, u32[]{:S(2)}) copy-start(bf16[4,2,256,256]{3,2,1,0:T(8,128)(2,1)S(1)} %collective-permute-done.8) | copy-start | bytes 3145732
  168.4 28.2 %collective-permute-start.12 = (bf16[2,4,2,256,256]{4,3,2,1,0:T(8,128)(2,1)}, bf16[2,4,2,256,256]{4,3,2,1,0:T(8,128)(2,1)}, u32[]{:S(2)}, u32[]{:S(2)}) collective-permute-start(bf16[2,4,2,256,256]{4,3,2,1,0:T(8,128)(2,1)} %pad_maximum_fusion.1), channel_id=1, source_target_pairs={{0,1},{1,0},{2,3},{3,2},{4,5},{5,4},{6,7},{7,6},{8,9},{9,8},{10,11... | collective-permute-start | bytes 6291464 | tf_op jit(solution)/shard_map/ppermute | solution.py:64
  170.0 16.0 %collective-permute-start.9 = (bf16[2,2,256,256]{3,2,1,0:T(8,128)(2,1)}, bf16[2,2,256,256]{3,2,1,0:T(8,128)(2,1)}, u32[]{:S(2)}, u32[]{:S(2)}) collective-permute-start(bf16[2,2,256,256]{3,2,1,0:T(8,128)(2,1)} %slice.45), channel_id=1, source_target_pairs={{0,2},{1,3},{2,4},{3,5},{4,6},{5,7},{6,0},{7,1},{8,10},{9,11},{10,... | collective-permute-start | bytes 1572872 | tf_op jit(solution)/shard_map/ppermute | solution.py:61
  175.4 14.3 %collective-permute-start.10 = (bf16[2,2,256,256]{3,2,1,0:T(8,128)(2,1)}, bf16[2,2,256,256]{3,2,1,0:T(8,128)(2,1)S(1)}, u32[]{:S(2)}, u32[]{:S(2)}) collective-permute-start(bf16[2,2,256,256]{3,2,1,0:T(8,128)(2,1)} %slice.46), channel_id=1, source_target_pairs={{0,6},{1,7},{2,0},{3,1},{4,2},{5,3},{6,4},{7,5},{8,14},{9,15},{10,... | collective-permute-start | bytes 1572872 | tf_op jit(solution)/shard_map/ppermute | solution.py:62
  177.3 18.2 %collective-permute-start.11 = (bf16[4,2,256,256]{3,2,1,0:T(8,128)(2,1)}, bf16[4,2,256,256]{3,2,1,0:T(8,128)(2,1)S(1)}, u32[]{:S(2)}, u32[]{:S(2)}) collective-permute-start(bf16[4,2,256,256]{3,2,1,0:T(8,128)(2,1)} %bitcast.40), channel_id=1, source_target_pairs={{0,1},{1,0},{2,3},{3,2},{4,5},{5,4},{6,7},{7,6},{8,9},{9,8},{10,11... | collective-permute-start | bytes 3145736 | tf_op jit(solution)/shard_map/ppermute | solution.py:60
  179.7 71.7 %copy-start.2 = (f32[8,256,256]{2,1,0:T(8,128)S(1)}, f32[8,256,256]{2,1,0:T(8,128)}, u32[]{:S(2)}) copy-start(f32[8,256,256]{2,1,0:T(8,128)} %copy-done.1) | copy-start | bytes 6291460
  189.7 10.1 %collective-permute-start.13 = (bf16[4,2,256,256]{3,2,1,0:T(8,128)(2,1)S(1)}, bf16[4,2,256,256]{3,2,1,0:T(8,128)(2,1)S(1)}, u32[]{:S(2)}, u32[]{:S(2)}) collective-permute-start(bf16[4,2,256,256]{3,2,1,0:T(8,128)(2,1)S(1)} %constant_dynamic-update-slice_fusion.5), channel_id=1, source_target_pairs={{0,1},{1,0},{2,3},{3,2},{4,5},{5,4},{6,7},{7,6},{8,9},{9,8},{10,11... | collective-permute-start | bytes 3145736 | tf_op jit(solution)/shard_map/ppermute | solution.py:65
Sparse Core Ops, SparseCore 0:
  9.8 114.2 all-gather.5
  140.6 110.6 all-gather.3

commit v6 on v5

--- a/solution.py
+++ b/solution.py
@@ -18,7 +18,6 @@
         for k in range(terms):
             t = o * terms + k
             d = jnp.dot(rows_ref[a_ref[t]], cols_ref[b_ref[t]], preferred_element_type=jnp.float32)
-            d = jnp.where(v_ref[t] > 0, d, 0.0)
             acc = d if acc is None else acc + d
         p = prev_ref[o]
         prev = jnp.where(p >= 0, owned_ref[jnp.maximum(p, 0)], 0.0)
@@ -64,7 +63,7 @@
     sib_near = lax.ppermute(jnp.stack([from_minus, from_plus]), "col", sib)
     sib_far = lax.ppermute(far, "col", sib)
     pieces = jnp.stack([x, from_minus, from_plus, far, sib_own, sib_near[0], sib_near[1], sib_far])
-    return pieces
+    return pieces.reshape((-1,) + x.shape[2:])
 
 
 def piece_classes(col_index, grid_cols):
@@ -87,7 +86,8 @@
     cols = lax.all_gather(panels, "row", axis=0, tiled=False)
     cols = cols.reshape(total_rows * slot_pairs, edge, edge)
     pieces = col_gather(panels, grid_cols)
-    rows = pieces.reshape(grid_cols * block_rows * slot_pairs, edge, edge)
+    zero_slot = pieces.shape[0]
+    rows = jnp.concatenate([pieces, jnp.zeros((1, edge, edge), pieces.dtype)])
 
     cls = piece_classes(col_index, grid_cols)
     piece_of = jnp.zeros((grid_cols,), jnp.int32).at[cls].set(jnp.arange(grid_cols, dtype=jnp.int32))
@@ -108,7 +108,7 @@
     lsel = jnp.argmax(match, axis=-1).astype(jnp.int32)
     b_idx = ((inner % grid_rows) * block_rows + inner // grid_rows)[:, None, :] * slot_pairs + lsel
     nout = block_rows * slot_pairs
-    a_t = jnp.broadcast_to(a_idx[:, None, :], valid.shape).reshape(-1)
+    a_t = jnp.where(valid, a_idx[:, None, :], zero_slot).reshape(-1)
     b_t = b_idx.reshape(-1)
     v_t = valid.astype(jnp.int32).reshape(-1)
 

time: 275 us -> 275 us (level)
  waiting for transfers between devices: 96.6 us -> 88.3 us
  local copies, waits for them, and re-layouts: 42.5 us -> 48.2 us
  blocking collectives: 57.9 us -> 60.7 us
    concatenate x0 -> x2, local copies, waits for them, and re-layouts: none -> 16.2 us  [purify_section(): rows = jnp.concatenate([pieces, jnp.zeros((1, edge, edge), pieces.dtype)])]
    unnamed x30 -> x26, local copies, waits for them, and re-layouts: 28.2 us -> 18.7 us
    ppermute x2, waiting for transfers between devices: 30.1 us -> 22.9 us  [col_gather(): from_minus = lax.ppermute(x, 'col', plus2)]
    ppermute x2, waiting for transfers between devices: 6.67 us -> 0.87 us  [col_gather(): far_b = lax.ppermute(from_plus[half:], 'col', minus2)]
    psum x1, blocking collectives: 15.5 us -> 18.8 us  [shards(): lax.psum(jnp.stack([diag_term, square_term]), 'col')]
    all_gather x2, waiting for transfers between devices: 53.4 us -> 56.6 us  [purify_section(): cols = lax.all_gather(panels, 'row', axis=0, tiled=False)]
where the time goes in v6:
time: 275 us; the launch traced here: 274 us
  waiting for transfers between devices  88.3 us (32%)
  blocking collectives  60.7 us (22%)
  local copies, waits for them, and re-layouts  48.2 us (18%)
  Pallas kernels  30.5 us (11%)
  between operations  16.3 us (6%)
  other arithmetic  15.5 us (6%)
  starting transfers between devices  14.3 us (5%)
    all_gather x2, waiting for transfers between devices, purify_section(): cols = lax.all_gather(panels, 'row', axis=0, tiled=False)  56.6 us
    psum x1, blocking collectives, shards(): lax.psum(lax.psum(jnp.stack([diag_term, square_term]), 'col'), 'row')  41.9 us
    pallas_call x2, Pallas kernels, run_product(): pl.pallas_call(product_kernel, in_specs=[smem] * 5 + [vmem] * 3, out_spec...  30.5 us
    ppermute x2, waiting for transfers between devices, col_gather(): from_minus = lax.ppermute(x, 'col', plus2)  22.9 us
    psum x1, blocking collectives, shards(): lax.psum(jnp.stack([diag_term, square_term]), 'col')  18.8 us
    unnamed x26, local copies, waits for them, and re-layouts  18.7 us
    concatenate x2, local copies, waits for them, and re-layouts, purify_section(): rows = jnp.concatenate([pieces, jnp.zeros((1, edge, edge), pieces.dtype)])  16.2 us
    ppermute x2, waiting for transfers between devices, col_gather(): far_a = lax.ppermute(from_minus[:half], 'col', plus2)  7.3 us
  transfers between devices with their start and end apart: 16, of which 7 were waited for; matrix products, arithmetic and copies ran while one was open for 20% of the time, Pallas kernels for 0%

profile of v6, /device:TPU:0, one launch (start us, length us, event | category | flops | bytes accessed | tf_op | source)
XLA Modules:
  0.0 273.8 jit_solution(9225502474420531411)
XLA Ops:
  6.5 3.2 %bitcast_dynamic-update-slice_fusion.6 = (bf16[8,4,2,256,256]{4,3,2,1,0:T(8,128)(2,1)}, bf16[4,1,2,1,256,256]{5,4,3,2,1,0:T(8,128)(2,1)}) fusion(f32[4,1,2,1,256,256]{5,4,3,2,1,0:T(8,128)} %param.7), kind=kLoop, calls=%fused_computation.18 | loop fusion | flops 524287 | bytes 4194304
  9.8 2.1 collective-permute-start
  11.9 2.2 collective-permute-start.1
  14.1 0.8 copy.70
  15.6 0.8 copy.81
  17.3 0.8 copy.73
  18.9 0.7 constant_dynamic-slice_fusion
  21.4 0.7 gather_fusion.3
  22.1 2.2 fusion
  24.3 0.7 select_reduce_fusion
  25.0 2.4 multiply_reduce_fusion
  27.3 1.3 pad_maximum_fusion.2
  28.8 18.8 %psum.14 = f32[2]{0:T(128)S(1)} all-reduce(f32[2]{0:T(128)S(1)} %pad_maximum_fusion.2), channel_id=1, replica_groups=mesh['row'=16,'col'=8] {'col'}, use_global_device_ids=true, to_apply=%region_8.9 | all-reduce | flops 2 | bytes 16 | tf_op jit(solution)/shard_map/psum | solution.py:150
  49.0 0.7 compare_reduce_fusion
  49.7 1.5 pad_maximum_fusion
  51.8 0.8 slice.43
  52.6 0.8 slice.44
  53.4 3.2 %collective-permute-start.3 = (bf16[2,2,256,256]{3,2,1,0:T(8,128)(2,1)}, bf16[2,2,256,256]{3,2,1,0:T(8,128)(2,1)}, u32[]{:S(2)}, u32[]{:S(2)}) collective-permute-start(bf16[2,2,256,256]{3,2,1,0:T(8,128)(2,1)} %slice.44), channel_id=1, source_target_pairs={{0,6},{1,7},{2,0},{3,1},{4,2},{5,3},{6,4},{7,5},{8,14},{9,15},{10,... | collective-permute-start | bytes 1572872 | tf_op jit(solution)/shard_map/ppermute | solution.py:61
  56.7 41.9 %psum.15 = f32[2]{0:T(128)S(1)} all-reduce(f32[2]{0:T(128)S(1)} %psum.14), channel_id=1, replica_groups=mesh['row'=16,'col'=8] {'row'}, use_global_device_ids=true, to_apply=%region_9.10 | all-reduce | flops 2 | bytes 16 | tf_op jit(solution)/shard_map/psum | solution.py:150
  100.3 1.1 constant_dynamic-update-slice_fusion.1
  101.4 1.1 constant_dynamic-update-slice_fusion
  102.6 1.0 constant_dynamic-update-slice_fusion.4
  103.6 1.1 constant_dynamic-update-slice_fusion.3
  104.6 1.1 bitcast_dynamic-update-slice_fusion.5
  105.7 1.1 bitcast_dynamic-update-slice_fusion.4
  106.8 3.1 %constant_dynamic-update-slice_fusion.2 = bf16[8,4,2,256,256]{4,3,2,1,0:T(8,128)(2,1)} fusion(bf16[8,4,2,256,256]{4,3,2,1,0:T(8,128)(2,1)} %bitcast_dynamic-update-slice_fusion.4, bf16[2,4,2,256,256]{4,3,2,1,0:T(8,128)(2,1)} %collective-permute-done.5), kind=kLoop, calls=%fused_computation.22 | loop fusion | bytes 4194304
  109.9 1.0 bitcast_dynamic-update-slice_fusion.3
  111.0 8.0 %concatenate.32.rows_ref = bf16[65,256,256]{2,1,0:T(8,128)(2,1)} pad(bf16[64,256,256]{2,1,0:T(8,128)(2,1)} %bitcast.88, bf16[]{:T(256)} %constant.146.clone.1), padding=0_1x0_0x0_0 | pad | bytes 16908290 | tf_op jit(solution)/shard_map/concatenate | solution.py:90
  119.0 5.2 %all-gather.6.cloned.1.call-done = bf16[64,1,2,1,256,256]{5,4,3,2,1,0:T(8,128)(2,1)} async-done(((bf16[4,1,2,1,256,256]{5,4,3,2,1,0:T(8,128)(2,1)}), bf16[64,1,2,1,256,256]{5,4,3,2,1,0:T(8,128)(2,1)}) %all-gather.6.cloned.1.call-update) | async-done | bytes 16777232 | tf_op jit(solution)/shard_map/all_gather | solution.py:86
  124.2 14.9 %shard_map.46 = (f32[8,256,256]{2,1,0:T(8,128)S(1)}, bf16[8,256,256]{2,1,0:T(8,128)(2,1)}) custom-call(s32[128]{0:T(128)S(1)} %select_n.205.a_ref, s32[128]{0:T(128)S(1)} %reshape.633.b_ref, s32[128]{0:T(128)S(1)} %reshape.645.v_ref, s32[8]{0:T(128)S(1)} %reshape.634.prev_ref, s32[1]{0:T(128)S(6)} %reshape.635.misc_ref, ...), custom_call_target="tpu_custom_call" | custom-call | flops 4294967296 | bytes 29491200 | tf_op jit(solution)/shard_map/pallas_call | solution.py:39
  139.1 1.3 copy-done.1
  140.5 1.6 collective-permute-start.7
  142.1 1.7 collective-permute-start.8
  143.8 22.9 %collective-permute-done.7 = bf16[4,2,256,256]{3,2,1,0:T(8,128)(2,1)S(1)} collective-permute-done((bf16[4,2,256,256]{3,2,1,0:T(8,128)(2,1)}, bf16[4,2,256,256]{3,2,1,0:T(8,128)(2,1)S(1)}, u32[]{:S(2)}, u32[]{:S(2)}) %collective-permute-start.7) | collective-permute-done | bytes 1048608 | tf_op jit(solution)/shard_map/ppermute | solution.py:57
  166.8 1.5 pad_maximum_fusion.1
  168.3 0.8 slice.45
  169.1 1.6 collective-permute-start.9
  170.6 0.9 slice.46
  171.5 1.7 collective-permute-start.10
  173.2 0.6 compare_reduce_fusion.2
  176.3 1.3 constant_dynamic-update-slice_fusion.10
  177.6 7.3 %collective-permute-done.9 = bf16[2,2,256,256]{3,2,1,0:T(8,128)(2,1)S(1)} collective-permute-done((bf16[2,2,256,256]{3,2,1,0:T(8,128)(2,1)}, bf16[2,2,256,256]{3,2,1,0:T(8,128)(2,1)S(1)}, u32[]{:S(2)}, u32[]{:S(2)}) %collective-permute-start.9) | collective-permute-done | bytes 524320 | tf_op jit(solution)/shard_map/ppermute | solution.py:60
  184.9 0.9 collective-permute-done.10
  186.2 1.7 constant_dynamic-update-slice_fusion.7
  188.6 3.2 %copy-done.3 = bf16[8,4,2,256,256]{4,3,2,1,0:T(8,128)(2,1)} copy-done((bf16[8,4,2,256,256]{4,3,2,1,0:T(8,128)(2,1)}, bf16[8,4,2,256,256]{4,3,2,1,0:T(8,128)(2,1)S(1)}, u32[]{:S(2)}) %copy-start.3) | copy-done | bytes 8388632
  191.8 8.1 %concatenate.34.rows_ref = bf16[65,256,256]{2,1,0:T(8,128)(2,1)} pad(bf16[64,256,256]{2,1,0:T(8,128)(2,1)} %bitcast.87, bf16[]{:T(256)} %constant.146.clone.1), padding=0_1x0_0x0_0 | pad | bytes 16908290 | tf_op jit(solution)/shard_map/concatenate | solution.py:90
  200.0 51.4 %all-gather.4.cloned.1.call-done = bf16[16,4,2,256,256]{4,3,2,1,0:T(8,128)(2,1)} async-done(((bf16[1,4,2,256,256]{4,3,2,1,0:T(8,128)(2,1)}), bf16[16,4,2,256,256]{4,3,2,1,0:T(8,128)(2,1)}) %all-gather.4.cloned.1.call-update) | async-done | bytes 16777232 | tf_op jit(solution)/shard_map/all_gather | solution.py:86
  251.3 15.6 %shard_map.47 = (f32[8,256,256]{2,1,0:T(8,128)}, bf16[8,256,256]{2,1,0:T(8,128)(2,1)}) custom-call(s32[128]{0:T(128)S(1)} %select_n.196.a_ref, s32[128]{0:T(128)S(1)} %reshape.626.b_ref, s32[128]{0:T(128)S(1)} %reshape.642.v_ref, s32[8]{0:T(128)S(1)} %reshape.628.prev_ref, s32[1]{0:T(128)} %bitcast.24.misc_ref, bf16[65,256,256]{2,1,0:T(8,128)(2,1)} %concatenate.34.rows_ref, ...), custom_call_target="tpu_custom_call" | custom-call | flops 4294967296 | bytes 29491200 | tf_op jit(solution)/shard_map/pallas_call | solution.py:39
  (102 shorter events, 9.2 us)
Async XLA Ops:
  6.5 117.7 %all-gather.6.cloned.1.call-start = ((), (), s32[]{:S(2)}) async-start(), calls=%async_computation.1 | async-start | bytes 17825792 | tf_op jit(solution)/shard_map/all_gather | solution.py:86
  9.8 241.5 %all-gather.4.cloned.1.call-start = ((), (), s32[]{:S(2)}) async-start(), calls=%async_computation | async-start | bytes 17825792 | tf_op jit(solution)/shard_map/all_gather | solution.py:86
  9.8 39.9 %collective-permute-start = (bf16[4,2,256,256]{3,2,1,0:T(8,128)(2,1)}, bf16[4,2,256,256]{3,2,1,0:T(8,128)(2,1)S(1)}, u32[]{:S(2)}, u32[]{:S(2)}) collective-permute-start(bf16[4,2,256,256]{3,2,1,0:T(8,128)(2,1)} %bitcast.89), channel_id=1, source_target_pairs={{0,2},{1,3},{2,4},{3,5},{4,6},{5,7},{6,0},{7,1},{8,10},{9,11},{10,... | collective-permute-start | bytes 3145736 | tf_op jit(solution)/shard_map/ppermute | solution.py:57
  11.9 37.8 %collective-permute-start.1 = (bf16[4,2,256,256]{3,2,1,0:T(8,128)(2,1)}, bf16[4,2,256,256]{3,2,1,0:T(8,128)(2,1)S(1)}, u32[]{:S(2)}, u32[]{:S(2)}) collective-permute-start(bf16[4,2,256,256]{3,2,1,0:T(8,128)(2,1)} %bitcast.90), channel_id=1, source_target_pairs={{0,6},{1,7},{2,0},{3,1},{4,2},{5,3},{6,4},{7,5},{8,14},{9,15},{10,... | collective-permute-start | bytes 3145736 | tf_op jit(solution)/shard_map/ppermute | solution.py:58
  14.1 91.6 %collective-permute-start.4 = (bf16[4,2,256,256]{3,2,1,0:T(8,128)(2,1)}, bf16[4,2,256,256]{3,2,1,0:T(8,128)(2,1)S(1)}, u32[]{:S(2)}, u32[]{:S(2)}) collective-permute-start(bf16[4,2,256,256]{3,2,1,0:T(8,128)(2,1)} %bitcast.91), channel_id=1, source_target_pairs={{0,1},{1,0},{2,3},{3,2},{4,5},{5,4},{6,7},{7,6},{8,9},{9,8},{10,11... | collective-permute-start | bytes 3145736 | tf_op jit(solution)/shard_map/ppermute | solution.py:59
  51.2 55.6 %collective-permute-start.5 = (bf16[2,4,2,256,256]{4,3,2,1,0:T(8,128)(2,1)}, bf16[2,4,2,256,256]{4,3,2,1,0:T(8,128)(2,1)}, u32[]{:S(2)}, u32[]{:S(2)}) collective-permute-start(bf16[2,4,2,256,256]{4,3,2,1,0:T(8,128)(2,1)} %pad_maximum_fusion), channel_id=1, source_target_pairs={{0,1},{1,0},{2,3},{3,2},{4,5},{5,4},{6,7},{7,6},{8,9},{9,8},{10,11... | collective-permute-start | bytes 6291464 | tf_op jit(solution)/shard_map/ppermute | solution.py:63
  52.6 47.7 %collective-permute-start.2 = (bf16[2,2,256,256]{3,2,1,0:T(8,128)(2,1)}, bf16[2,2,256,256]{3,2,1,0:T(8,128)(2,1)}, u32[]{:S(2)}, u32[]{:S(2)}) collective-permute-start(bf16[2,2,256,256]{3,2,1,0:T(8,128)(2,1)} %slice.43), channel_id=1, source_target_pairs={{0,2},{1,3},{2,4},{3,5},{4,6},{5,7},{6,0},{7,1},{8,10},{9,11},{10,... | collective-permute-start | bytes 1572872 | tf_op jit(solution)/shard_map/ppermute | solution.py:60
  53.4 48.0 %collective-permute-start.3 = (bf16[2,2,256,256]{3,2,1,0:T(8,128)(2,1)}, bf16[2,2,256,256]{3,2,1,0:T(8,128)(2,1)}, u32[]{:S(2)}, u32[]{:S(2)}) collective-permute-start(bf16[2,2,256,256]{3,2,1,0:T(8,128)(2,1)} %slice.44), channel_id=1, source_target_pairs={{0,6},{1,7},{2,0},{3,1},{4,2},{5,3},{6,4},{7,5},{8,14},{9,15},{10,... | collective-permute-start | bytes 1572872 | tf_op jit(solution)/shard_map/ppermute | solution.py:61
  102.5 7.4 %collective-permute-start.6 = (bf16[4,2,256,256]{3,2,1,0:T(8,128)(2,1)S(1)}, bf16[4,2,256,256]{3,2,1,0:T(8,128)(2,1)S(1)}, u32[]{:S(2)}, u32[]{:S(2)}) collective-permute-start(bf16[4,2,256,256]{3,2,1,0:T(8,128)(2,1)S(1)} %constant_dynamic-update-slice_fusion), channel_id=1, source_target_pairs={{0,1},{1,0},{2,3},{3,2},{4,5},{5,4},{6,7},{7,6},{8,9},{9,8},{10,11... | collective-permute-start | bytes 3145736 | tf_op jit(solution)/shard_map/ppermute | solution.py:64
  111.0 13.3 %copy-start = (f32[4,1,2,1,256,256]{5,4,3,2,1,0:T(8,128)S(1)}, f32[4,1,2,1,256,256]{5,4,3,2,1,0:T(8,128)}, u32[]{:S(2)}) copy-start(f32[4,1,2,1,256,256]{5,4,3,2,1,0:T(8,128)} %param.7) | copy-start | bytes 6291460
  139.1 1.3 copy-start.1
  140.5 26.2 %collective-permute-start.7 = (bf16[4,2,256,256]{3,2,1,0:T(8,128)(2,1)}, bf16[4,2,256,256]{3,2,1,0:T(8,128)(2,1)S(1)}, u32[]{:S(2)}, u32[]{:S(2)}) collective-permute-start(bf16[4,2,256,256]{3,2,1,0:T(8,128)(2,1)} %bitcast.40), channel_id=1, source_target_pairs={{0,2},{1,3},{2,4},{3,5},{4,6},{5,7},{6,0},{7,1},{8,10},{9,11},{10,... | collective-permute-start | bytes 3145736 | tf_op jit(solution)/shard_map/ppermute | solution.py:57
  142.1 24.7 %collective-permute-start.8 = (bf16[4,2,256,256]{3,2,1,0:T(8,128)(2,1)}, bf16[4,2,256,256]{3,2,1,0:T(8,128)(2,1)S(1)}, u32[]{:S(2)}, u32[]{:S(2)}) collective-permute-start(bf16[4,2,256,256]{3,2,1,0:T(8,128)(2,1)} %bitcast.40), channel_id=1, source_target_pairs={{0,6},{1,7},{2,0},{3,1},{4,2},{5,3},{6,4},{7,5},{8,14},{9,15},{10,... | collective-permute-start | bytes 3145736 | tf_op jit(solution)/shard_map/ppermute | solution.py:58
  168.3 18.0 %collective-permute-start.12 = (bf16[2,4,2,256,256]{4,3,2,1,0:T(8,128)(2,1)}, bf16[2,4,2,256,256]{4,3,2,1,0:T(8,128)(2,1)}, u32[]{:S(2)}, u32[]{:S(2)}) collective-permute-start(bf16[2,4,2,256,256]{4,3,2,1,0:T(8,128)(2,1)} %pad_maximum_fusion.1), channel_id=1, source_target_pairs={{0,1},{1,0},{2,3},{3,2},{4,5},{5,4},{6,7},{7,6},{8,9},{9,8},{10,11... | collective-permute-start | bytes 6291464 | tf_op jit(solution)/shard_map/ppermute | solution.py:63
  169.1 15.8 %collective-permute-start.9 = (bf16[2,2,256,256]{3,2,1,0:T(8,128)(2,1)}, bf16[2,2,256,256]{3,2,1,0:T(8,128)(2,1)S(1)}, u32[]{:S(2)}, u32[]{:S(2)}) collective-permute-start(bf16[2,2,256,256]{3,2,1,0:T(8,128)(2,1)} %slice.45), channel_id=1, source_target_pairs={{0,2},{1,3},{2,4},{3,5},{4,6},{5,7},{6,0},{7,1},{8,10},{9,11},{10,... | collective-permute-start | bytes 1572872 | tf_op jit(solution)/shard_map/ppermute | solution.py:60
  171.5 14.3 %collective-permute-start.10 = (bf16[2,2,256,256]{3,2,1,0:T(8,128)(2,1)}, bf16[2,2,256,256]{3,2,1,0:T(8,128)(2,1)S(1)}, u32[]{:S(2)}, u32[]{:S(2)}) collective-permute-start(bf16[2,2,256,256]{3,2,1,0:T(8,128)(2,1)} %slice.46), channel_id=1, source_target_pairs={{0,6},{1,7},{2,0},{3,1},{4,2},{5,3},{6,4},{7,5},{8,14},{9,15},{10,... | collective-permute-start | bytes 1572872 | tf_op jit(solution)/shard_map/ppermute | solution.py:61
  176.2 9.9 %collective-permute-start.11 = (bf16[4,2,256,256]{3,2,1,0:T(8,128)(2,1)}, bf16[4,2,256,256]{3,2,1,0:T(8,128)(2,1)S(1)}, u32[]{:S(2)}, u32[]{:S(2)}) collective-permute-start(bf16[4,2,256,256]{3,2,1,0:T(8,128)(2,1)} %bitcast.40), channel_id=1, source_target_pairs={{0,1},{1,0},{2,3},{3,2},{4,5},{5,4},{6,7},{7,6},{8,9},{9,8},{10,11... | collective-permute-start | bytes 3145736 | tf_op jit(solution)/shard_map/ppermute | solution.py:59
  185.8 2.7 %collective-permute-start.13 = (bf16[4,2,256,256]{3,2,1,0:T(8,128)(2,1)S(1)}, bf16[4,2,256,256]{3,2,1,0:T(8,128)(2,1)S(1)}, u32[]{:S(2)}, u32[]{:S(2)}) collective-permute-start(bf16[4,2,256,256]{3,2,1,0:T(8,128)(2,1)S(1)} %constant_dynamic-update-slice_fusion.5), channel_id=1, source_target_pairs={{0,1},{1,0},{2,3},{3,2},{4,5},{5,4},{6,7},{7,6},{8,9},{9,8},{10,11... | collective-permute-start | bytes 3145736 | tf_op jit(solution)/shard_map/ppermute | solution.py:64
  188.6 3.2 %copy-start.3 = (bf16[8,4,2,256,256]{4,3,2,1,0:T(8,128)(2,1)}, bf16[8,4,2,256,256]{4,3,2,1,0:T(8,128)(2,1)S(1)}, u32[]{:S(2)}) copy-start(bf16[8,4,2,256,256]{4,3,2,1,0:T(8,128)(2,1)S(1)} %bitcast_dynamic-update-slice_fusion) | copy-start | bytes 25165828
  191.8 59.5 %copy-start.2 = (f32[8,256,256]{2,1,0:T(8,128)S(1)}, f32[8,256,256]{2,1,0:T(8,128)}, u32[]{:S(2)}) copy-start(f32[8,256,256]{2,1,0:T(8,128)} %copy-done.1) | copy-start | bytes 6291460
Sparse Core Ops, SparseCore 0:
  9.9 114.3 all-gather.5
  140.6 110.6 all-gather.3

commit v7 on v5

--- a/solution.py
+++ b/solution.py
@@ -8,10 +8,21 @@
 ITERS = 2
 
 
-def product_kernel(a_ref, b_ref, v_ref, prev_ref, misc_ref, rows_ref, cols_ref, owned_ref, out_ref, outb_ref):
+def product_kernel(a_ref, b_ref, v_ref, prev_ref, misc_ref, rows_hbm, cols_hbm, owned_ref, out_ref, outb_ref,
+                   rows_ref, cols_ref, sem):
     nout = out_ref.shape[0]
     terms = a_ref.shape[0] // nout
     take_product = misc_ref[0] > 0
+    parts = sem.shape[0] - 1
+    step = cols_ref.shape[0] // parts
+    copies = [pltpu.make_async_copy(rows_hbm, rows_ref, sem.at[0])]
+    for q in range(parts):
+        piece = pl.ds(q * step, step)
+        copies.append(pltpu.make_async_copy(cols_hbm.at[piece], cols_ref.at[piece], sem.at[q + 1]))
+    for c in copies:
+        c.start()
+    for c in copies:
+        c.wait()
 
     def body(o, carry):
         acc = None
@@ -35,11 +46,17 @@
     max_terms = a_t.shape[0]
     smem = pl.BlockSpec(memory_space=pltpu.SMEM)
     vmem = pl.BlockSpec(memory_space=pltpu.VMEM)
+    hbm = pl.BlockSpec(memory_space=pl.ANY)
     flops = 2 * edge * edge * edge * max_terms
     nbytes = (rows.size + cols.size) * 2 + 2 * owned.size * 4
     return pl.pallas_call(
         product_kernel,
-        in_specs=[smem] * 5 + [vmem] * 3,
+        in_specs=[smem] * 5 + [hbm, hbm, vmem],
+        scratch_shapes=[
+            pltpu.VMEM(rows.shape, rows.dtype),
+            pltpu.VMEM(cols.shape, cols.dtype),
+            pltpu.SemaphoreType.DMA((5,)),
+        ],
         out_specs=(vmem, vmem),
         out_shape=(
             jax.ShapeDtypeStruct(owned.shape, jnp.float32),

time: 275 us -> 276 us (level)
  transfers between devices with their start and end apart: 16 -> 16, of which waited for: 7 -> 8; matrix products, arithmetic and copies ran while one was open for 20% -> 19% of each run, Pallas kernels for 0% -> 0%
where the time goes in v7:
time: 276 us; the launch traced here: 275 us
  waiting for transfers between devices  96.6 us (35%)
  blocking collectives  57.9 us (21%)
  local copies, waits for them, and re-layouts  42.5 us (15%)
  Pallas kernels  31.8 us (12%)
  between operations  16.3 us (6%)
  other arithmetic  15.6 us (6%)
  starting transfers between devices  14.3 us (5%)
    all_gather x2, waiting for transfers between devices, purify_section(): cols = lax.all_gather(panels, 'row', axis=0, tiled=False)  53.5 us
    psum x1, blocking collectives, shards(): lax.psum(lax.psum(jnp.stack([diag_term, square_term]), 'col'), 'row')  42.4 us
    pallas_call x2, Pallas kernels, run_product(): pl.pallas_call(product_kernel, in_specs=[smem] * 5 + [hbm, hbm, vmem], sc...  31.8 us
    ppermute x2, waiting for transfers between devices, col_gather(): from_minus = lax.ppermute(x, 'col', plus2)  30.1 us
    unnamed x30, local copies, waits for them, and re-layouts  28.2 us
    psum x1, blocking collectives, shards(): lax.psum(jnp.stack([diag_term, square_term]), 'col')  15.5 us
    ppermute x2, waiting for transfers between devices, col_gather(): far_b = lax.ppermute(from_plus[half:], 'col', minus2)  6.68 us
    ppermute x2, waiting for transfers between devices, col_gather(): far_a = lax.ppermute(from_minus[:half], 'col', plus2)  6.28 us
  transfers between devices with their start and end apart: 16, of which 8 were waited for; matrix products, arithmetic and copies ran while one was open for 19% of the time, Pallas kernels for 0%

profile of v7, /device:TPU:0, one launch (start us, length us, event | category | flops | bytes accessed | tf_op | source)
XLA Modules:
  0.0 275.1 jit_solution(12344725787906495629)
XLA Ops:
  6.5 3.2 %bitcast_dynamic-update-slice_fusion.6 = (bf16[8,4,2,256,256]{4,3,2,1,0:T(8,128)(2,1)}, bf16[4,1,2,1,256,256]{5,4,3,2,1,0:T(8,128)(2,1)}) fusion(f32[4,1,2,1,256,256]{5,4,3,2,1,0:T(8,128)} %param.7), kind=kLoop, calls=%fused_computation.18 | loop fusion | flops 524287 | bytes 4194304
  9.8 2.1 collective-permute-start
  11.9 2.2 collective-permute-start.1
  14.1 0.8 copy.69
  15.5 0.8 copy.80
  17.2 0.8 copy.73
  19.8 1.9 fusion
  22.4 2.5 multiply_reduce_fusion
  25.4 1.3 pad_maximum_fusion.2
  30.1 7.2 %collective-permute-done = bf16[4,2,256,256]{3,2,1,0:T(8,128)(2,1)S(1)} collective-permute-done((bf16[4,2,256,256]{3,2,1,0:T(8,128)(2,1)}, bf16[4,2,256,256]{3,2,1,0:T(8,128)(2,1)S(1)}, u32[]{:S(2)}, u32[]{:S(2)}) %collective-permute-start) | collective-permute-done | bytes 1048608 | tf_op jit(solution)/shard_map/ppermute | solution.py:75
  37.4 1.6 pad_maximum_fusion
  39.0 15.5 %psum.14 = f32[2]{0:T(128)S(1)} all-reduce(f32[2]{0:T(128)S(1)} %pad_maximum_fusion.2), channel_id=1, replica_groups=mesh['row'=16,'col'=8] {'col'}, use_global_device_ids=true, to_apply=%region_8.9 | all-reduce | flops 2 | bytes 16 | tf_op jit(solution)/shard_map/psum | solution.py:167
  54.5 0.8 slice.43
  55.4 42.4 %psum.15 = f32[2]{0:T(128)S(1)} all-reduce(f32[2]{0:T(128)S(1)} %psum.14), channel_id=1, replica_groups=mesh['row'=16,'col'=8] {'row'}, use_global_device_ids=true, to_apply=%region_9.10 | all-reduce | flops 2 | bytes 16 | tf_op jit(solution)/shard_map/psum | solution.py:167
  98.1 0.9 slice.44
  98.9 3.2 %collective-permute-start.3 = (bf16[2,2,256,256]{3,2,1,0:T(8,128)(2,1)}, bf16[2,2,256,256]{3,2,1,0:T(8,128)(2,1)}, u32[]{:S(2)}, u32[]{:S(2)}) collective-permute-start(bf16[2,2,256,256]{3,2,1,0:T(8,128)(2,1)} %slice.44), channel_id=1, source_target_pairs={{0,6},{1,7},{2,0},{3,1},{4,2},{5,3},{6,4},{7,5},{8,14},{9,15},{10,... | collective-permute-start | bytes 1572872 | tf_op jit(solution)/shard_map/ppermute | solution.py:79
  103.7 1.2 constant_dynamic-update-slice_fusion.1
  105.0 4.1 %collective-permute-done.3 = bf16[2,2,256,256]{3,2,1,0:T(8,128)(2,1)} collective-permute-done((bf16[2,2,256,256]{3,2,1,0:T(8,128)(2,1)}, bf16[2,2,256,256]{3,2,1,0:T(8,128)(2,1)}, u32[]{:S(2)}, u32[]{:S(2)}) %collective-permute-start.3) | collective-permute-done | bytes 524320 | tf_op jit(solution)/shard_map/ppermute | solution.py:79
  109.1 1.1 constant_dynamic-update-slice_fusion
  110.3 1.1 constant_dynamic-update-slice_fusion.4
  111.4 2.3 constant_dynamic-update-slice_fusion.3
  113.7 1.1 bitcast_dynamic-update-slice_fusion.5
  114.7 2.3 bitcast_dynamic-update-slice_fusion.4
  117.0 3.1 %constant_dynamic-update-slice_fusion.2 = bf16[8,4,2,256,256]{4,3,2,1,0:T(8,128)(2,1)} fusion(bf16[8,4,2,256,256]{4,3,2,1,0:T(8,128)(2,1)} %bitcast_dynamic-update-slice_fusion.4, bf16[2,4,2,256,256]{4,3,2,1,0:T(8,128)(2,1)} %collective-permute-done.5), kind=kLoop, calls=%fused_computation.22 | loop fusion | bytes 4194304
  120.1 1.0 bitcast_dynamic-update-slice_fusion.3
  121.2 3.0 %all-gather.6.cloned.1.call-done = bf16[64,1,2,1,256,256]{5,4,3,2,1,0:T(8,128)(2,1)} async-done(((bf16[4,1,2,1,256,256]{5,4,3,2,1,0:T(8,128)(2,1)}), bf16[64,1,2,1,256,256]{5,4,3,2,1,0:T(8,128)(2,1)}) %all-gather.6.cloned.1.call-update) | async-done | bytes 16777232 | tf_op jit(solution)/shard_map/all_gather | solution.py:104
  124.1 15.5 %shard_map.46 = (f32[8,256,256]{2,1,0:T(8,128)S(1)}, bf16[8,256,256]{2,1,0:T(8,128)(2,1)}) custom-call(s32[128]{0:T(128)S(1)} %reshape.618.a_ref, s32[128]{0:T(128)S(1)} %reshape.628.b_ref, s32[128]{0:T(128)S(1)} %reshape.640.v_ref, s32[8]{0:T(128)S(1)} %reshape.629.prev_ref, s32[1]{0:T(128)S(6)} %reshape.630.misc_ref, bf16[64,256,256]{2,1,0:T(8,128)(2,1)} %bitcast.87, ...), custom_call_target="tpu_custom_call" | custom-call | flops 4294967296 | bytes 29360128 | tf_op jit(solution)/shard_map/pallas_call | solution.py:52
  139.7 1.4 copy-done.1
  141.1 1.6 collective-permute-start.7
  142.7 1.7 collective-permute-start.8
  144.5 22.8 %collective-permute-done.7 = bf16[4,2,256,256]{3,2,1,0:T(8,128)(2,1)S(1)} collective-permute-done((bf16[4,2,256,256]{3,2,1,0:T(8,128)(2,1)}, bf16[4,2,256,256]{3,2,1,0:T(8,128)(2,1)S(1)}, u32[]{:S(2)}, u32[]{:S(2)}) %collective-permute-start.7) | collective-permute-done | bytes 1048608 | tf_op jit(solution)/shard_map/ppermute | solution.py:75
  167.4 1.7 pad_maximum_fusion.1
  169.9 0.8 slice.45
  170.7 1.5 collective-permute-start.9
  175.1 0.8 slice.46
  176.0 1.7 collective-permute-start.10
  178.0 2.3 constant_dynamic-update-slice_fusion.10
  180.3 6.3 %collective-permute-done.9 = bf16[2,2,256,256]{3,2,1,0:T(8,128)(2,1)} collective-permute-done((bf16[2,2,256,256]{3,2,1,0:T(8,128)(2,1)}, bf16[2,2,256,256]{3,2,1,0:T(8,128)(2,1)}, u32[]{:S(2)}, u32[]{:S(2)}) %collective-permute-start.9) | collective-permute-done | bytes 524320 | tf_op jit(solution)/shard_map/ppermute | solution.py:78
  186.6 1.1 constant_dynamic-update-slice_fusion.6
  187.7 2.6 collective-permute-done.10
  190.4 2.4 constant_dynamic-update-slice_fusion.9
  192.7 2.3 constant_dynamic-update-slice_fusion.8
  195.1 1.1 bitcast_dynamic-update-slice_fusion.2
  196.1 1.0 bitcast_dynamic-update-slice_fusion.1
  197.2 3.2 %constant_dynamic-update-slice_fusion.7 = bf16[8,4,2,256,256]{4,3,2,1,0:T(8,128)(2,1)} fusion(bf16[8,4,2,256,256]{4,3,2,1,0:T(8,128)(2,1)} %bitcast_dynamic-update-slice_fusion.1, bf16[2,4,2,256,256]{4,3,2,1,0:T(8,128)(2,1)} %collective-permute-done.12), kind=kLoop, calls=%fused_computation.27 | loop fusion | bytes 4194304
  200.4 1.0 bitcast_dynamic-update-slice_fusion
  201.4 50.5 %all-gather.4.cloned.1.call-done = bf16[16,4,2,256,256]{4,3,2,1,0:T(8,128)(2,1)} async-done(((bf16[1,4,2,256,256]{4,3,2,1,0:T(8,128)(2,1)}), bf16[16,4,2,256,256]{4,3,2,1,0:T(8,128)(2,1)}) %all-gather.4.cloned.1.call-update) | async-done | bytes 16777232 | tf_op jit(solution)/shard_map/all_gather | solution.py:104
  252.0 16.3 %shard_map.47 = (f32[8,256,256]{2,1,0:T(8,128)}, bf16[8,256,256]{2,1,0:T(8,128)(2,1)}) custom-call(s32[128]{0:T(128)S(1)} %reshape.618.a_ref, s32[128]{0:T(128)S(1)} %reshape.621.b_ref, s32[128]{0:T(128)S(1)} %reshape.637.v_ref, s32[8]{0:T(128)S(1)} %reshape.623.prev_ref, s32[1]{0:T(128)} %bitcast.24.misc_ref, bf16[64,256,256]{2,1,0:T(8,128)(2,1)} %bitcast.46.rows_hbm, ...), custom_call_target="tpu_custom_call" | custom-call | flops 4294967296 | bytes 29360128 | tf_op jit(solution)/shard_map/pallas_call | solution.py:52
  (101 shorter events, 11.6 us)
Async XLA Ops:
  6.5 117.6 %all-gather.6.cloned.1.call-start = ((), (), s32[]{:S(2)}) async-start(), calls=%async_computation.1 | async-start | bytes 17825792 | tf_op jit(solution)/shard_map/all_gather | solution.py:104
  9.7 242.2 %all-gather.4.cloned.1.call-start = ((), (), s32[]{:S(2)}) async-start(), calls=%async_computation | async-start | bytes 17825792 | tf_op jit(solution)/shard_map/all_gather | solution.py:104
  9.8 27.6 %collective-permute-start = (bf16[4,2,256,256]{3,2,1,0:T(8,128)(2,1)}, bf16[4,2,256,256]{3,2,1,0:T(8,128)(2,1)S(1)}, u32[]{:S(2)}, u32[]{:S(2)}) collective-permute-start(bf16[4,2,256,256]{3,2,1,0:T(8,128)(2,1)} %bitcast.88), channel_id=1, source_target_pairs={{0,2},{1,3},{2,4},{3,5},{4,6},{5,7},{6,0},{7,1},{8,10},{9,11},{10,... | collective-permute-start | bytes 3145736 | tf_op jit(solution)/shard_map/ppermute | solution.py:75
  11.9 25.5 %collective-permute-start.1 = (bf16[4,2,256,256]{3,2,1,0:T(8,128)(2,1)}, bf16[4,2,256,256]{3,2,1,0:T(8,128)(2,1)S(1)}, u32[]{:S(2)}, u32[]{:S(2)}) collective-permute-start(bf16[4,2,256,256]{3,2,1,0:T(8,128)(2,1)} %bitcast.89), channel_id=1, source_target_pairs={{0,6},{1,7},{2,0},{3,1},{4,2},{5,3},{6,4},{7,5},{8,14},{9,15},{10,... | collective-permute-start | bytes 3145736 | tf_op jit(solution)/shard_map/ppermute | solution.py:76
  14.1 100.6 %collective-permute-start.4 = (bf16[4,2,256,256]{3,2,1,0:T(8,128)(2,1)}, bf16[4,2,256,256]{3,2,1,0:T(8,128)(2,1)}, u32[]{:S(2)}, u32[]{:S(2)}) collective-permute-start(bf16[4,2,256,256]{3,2,1,0:T(8,128)(2,1)} %bitcast.90), channel_id=1, source_target_pairs={{0,1},{1,0},{2,3},{3,2},{4,5},{5,4},{6,7},{7,6},{8,9},{9,8},{10,11... | collective-permute-start | bytes 3145736 | tf_op jit(solution)/shard_map/ppermute | solution.py:77
  37.4 64.7 %copy-start.3 = (bf16[4,2,256,256]{3,2,1,0:T(8,128)(2,1)}, bf16[4,2,256,256]{3,2,1,0:T(8,128)(2,1)S(1)}, u32[]{:S(2)}) copy-start(bf16[4,2,256,256]{3,2,1,0:T(8,128)(2,1)S(1)} %collective-permute-done.1) | copy-start | bytes 3145732
  39.0 78.0 %collective-permute-start.5 = (bf16[2,4,2,256,256]{4,3,2,1,0:T(8,128)(2,1)}, bf16[2,4,2,256,256]{4,3,2,1,0:T(8,128)(2,1)}, u32[]{:S(2)}, u32[]{:S(2)}) collective-permute-start(bf16[2,4,2,256,256]{4,3,2,1,0:T(8,128)(2,1)} %pad_maximum_fusion), channel_id=1, source_target_pairs={{0,1},{1,0},{2,3},{3,2},{4,5},{5,4},{6,7},{7,6},{8,9},{9,8},{10,11... | collective-permute-start | bytes 6291464 | tf_op jit(solution)/shard_map/ppermute | solution.py:81
  55.4 48.4 %collective-permute-start.2 = (bf16[2,2,256,256]{3,2,1,0:T(8,128)(2,1)}, bf16[2,2,256,256]{3,2,1,0:T(8,128)(2,1)}, u32[]{:S(2)}, u32[]{:S(2)}) collective-permute-start(bf16[2,2,256,256]{3,2,1,0:T(8,128)(2,1)} %slice.43), channel_id=1, source_target_pairs={{0,2},{1,3},{2,4},{3,5},{4,6},{5,7},{6,0},{7,1},{8,10},{9,11},{10,... | collective-permute-start | bytes 1572872 | tf_op jit(solution)/shard_map/ppermute | solution.py:78
  98.9 10.2 %collective-permute-start.3 = (bf16[2,2,256,256]{3,2,1,0:T(8,128)(2,1)}, bf16[2,2,256,256]{3,2,1,0:T(8,128)(2,1)}, u32[]{:S(2)}, u32[]{:S(2)}) collective-permute-start(bf16[2,2,256,256]{3,2,1,0:T(8,128)(2,1)} %slice.44), channel_id=1, source_target_pairs={{0,6},{1,7},{2,0},{3,1},{4,2},{5,3},{6,4},{7,5},{8,14},{9,15},{10,... | collective-permute-start | bytes 1572872 | tf_op jit(solution)/shard_map/ppermute | solution.py:79
  103.7 20.4 %copy-start = (f32[4,1,2,1,256,256]{5,4,3,2,1,0:T(8,128)S(1)}, f32[4,1,2,1,256,256]{5,4,3,2,1,0:T(8,128)}, u32[]{:S(2)}) copy-start(f32[4,1,2,1,256,256]{5,4,3,2,1,0:T(8,128)} %param.7) | copy-start | bytes 6291460
  110.2 9.9 %collective-permute-start.6 = (bf16[4,2,256,256]{3,2,1,0:T(8,128)(2,1)S(1)}, bf16[4,2,256,256]{3,2,1,0:T(8,128)(2,1)S(1)}, u32[]{:S(2)}, u32[]{:S(2)}) collective-permute-start(bf16[4,2,256,256]{3,2,1,0:T(8,128)(2,1)S(1)} %constant_dynamic-update-slice_fusion), channel_id=1, source_target_pairs={{0,1},{1,0},{2,3},{3,2},{4,5},{5,4},{6,7},{7,6},{8,9},{9,8},{10,11... | collective-permute-start | bytes 3145736 | tf_op jit(solution)/shard_map/ppermute | solution.py:82
  139.7 1.4 copy-start.1
  141.1 26.2 %collective-permute-start.7 = (bf16[4,2,256,256]{3,2,1,0:T(8,128)(2,1)}, bf16[4,2,256,256]{3,2,1,0:T(8,128)(2,1)S(1)}, u32[]{:S(2)}, u32[]{:S(2)}) collective-permute-start(bf16[4,2,256,256]{3,2,1,0:T(8,128)(2,1)} %bitcast.40), channel_id=1, source_target_pairs={{0,2},{1,3},{2,4},{3,5},{4,6},{5,7},{6,0},{7,1},{8,10},{9,11},{10,... | collective-permute-start | bytes 3145736 | tf_op jit(solution)/shard_map/ppermute | solution.py:75
  142.7 24.7 %collective-permute-start.8 = (bf16[4,2,256,256]{3,2,1,0:T(8,128)(2,1)}, bf16[4,2,256,256]{3,2,1,0:T(8,128)(2,1)S(1)}, u32[]{:S(2)}, u32[]{:S(2)}) collective-permute-start(bf16[4,2,256,256]{3,2,1,0:T(8,128)(2,1)} %bitcast.40), channel_id=1, source_target_pairs={{0,6},{1,7},{2,0},{3,1},{4,2},{5,3},{6,4},{7,5},{8,14},{9,15},{10,... | collective-permute-start | bytes 3145736 | tf_op jit(solution)/shard_map/ppermute | solution.py:76
  167.3 5.6 %copy-start.4 = (bf16[4,2,256,256]{3,2,1,0:T(8,128)(2,1)}, bf16[4,2,256,256]{3,2,1,0:T(8,128)(2,1)S(1)}, u32[]{:S(2)}) copy-start(bf16[4,2,256,256]{3,2,1,0:T(8,128)(2,1)S(1)} %collective-permute-done.7) | copy-start | bytes 3145732
  167.4 10.6 %copy-start.5 = (bf16[4,2,256,256]{3,2,1,0:T(8,128)(2,1)}, bf16[4,2,256,256]{3,2,1,0:T(8,128)(2,1)S(1)}, u32[]{:S(2)}) copy-start(bf16[4,2,256,256]{3,2,1,0:T(8,128)(2,1)S(1)} %collective-permute-done.8) | copy-start | bytes 3145732
  169.1 28.1 %collective-permute-start.12 = (bf16[2,4,2,256,256]{4,3,2,1,0:T(8,128)(2,1)}, bf16[2,4,2,256,256]{4,3,2,1,0:T(8,128)(2,1)}, u32[]{:S(2)}, u32[]{:S(2)}) collective-permute-start(bf16[2,4,2,256,256]{4,3,2,1,0:T(8,128)(2,1)} %pad_maximum_fusion.1), channel_id=1, source_target_pairs={{0,1},{1,0},{2,3},{3,2},{4,5},{5,4},{6,7},{7,6},{8,9},{9,8},{10,11... | collective-permute-start | bytes 6291464 | tf_op jit(solution)/shard_map/ppermute | solution.py:81
  170.7 15.9 %collective-permute-start.9 = (bf16[2,2,256,256]{3,2,1,0:T(8,128)(2,1)}, bf16[2,2,256,256]{3,2,1,0:T(8,128)(2,1)}, u32[]{:S(2)}, u32[]{:S(2)}) collective-permute-start(bf16[2,2,256,256]{3,2,1,0:T(8,128)(2,1)} %slice.45), channel_id=1, source_target_pairs={{0,2},{1,3},{2,4},{3,5},{4,6},{5,7},{6,0},{7,1},{8,10},{9,11},{10,... | collective-permute-start | bytes 1572872 | tf_op jit(solution)/shard_map/ppermute | solution.py:78
  176.0 14.3 %collective-permute-start.10 = (bf16[2,2,256,256]{3,2,1,0:T(8,128)(2,1)}, bf16[2,2,256,256]{3,2,1,0:T(8,128)(2,1)S(1)}, u32[]{:S(2)}, u32[]{:S(2)}) collective-permute-start(bf16[2,2,256,256]{3,2,1,0:T(8,128)(2,1)} %slice.46), channel_id=1, source_target_pairs={{0,6},{1,7},{2,0},{3,1},{4,2},{5,3},{6,4},{7,5},{8,14},{9,15},{10,... | collective-permute-start | bytes 1572872 | tf_op jit(solution)/shard_map/ppermute | solution.py:79
  178.0 18.1 %collective-permute-start.11 = (bf16[4,2,256,256]{3,2,1,0:T(8,128)(2,1)}, bf16[4,2,256,256]{3,2,1,0:T(8,128)(2,1)S(1)}, u32[]{:S(2)}, u32[]{:S(2)}) collective-permute-start(bf16[4,2,256,256]{3,2,1,0:T(8,128)(2,1)} %bitcast.40), channel_id=1, source_target_pairs={{0,1},{1,0},{2,3},{3,2},{4,5},{5,4},{6,7},{7,6},{8,9},{9,8},{10,11... | collective-permute-start | bytes 3145736 | tf_op jit(solution)/shard_map/ppermute | solution.py:77
  180.3 71.7 %copy-start.2 = (f32[8,256,256]{2,1,0:T(8,128)S(1)}, f32[8,256,256]{2,1,0:T(8,128)}, u32[]{:S(2)}) copy-start(f32[8,256,256]{2,1,0:T(8,128)} %copy-done.1) | copy-start | bytes 6291460
  190.3 10.1 %collective-permute-start.13 = (bf16[4,2,256,256]{3,2,1,0:T(8,128)(2,1)S(1)}, bf16[4,2,256,256]{3,2,1,0:T(8,128)(2,1)S(1)}, u32[]{:S(2)}, u32[]{:S(2)}) collective-permute-start(bf16[4,2,256,256]{3,2,1,0:T(8,128)(2,1)S(1)} %constant_dynamic-update-slice_fusion.5), channel_id=1, source_target_pairs={{0,1},{1,0},{2,3},{3,2},{4,5},{5,4},{6,7},{7,6},{8,9},{9,8},{10,11... | collective-permute-start | bytes 3145736 | tf_op jit(solution)/shard_map/ppermute | solution.py:82
Sparse Core Ops, SparseCore 0:
  9.8 114.2 all-gather.5
  141.2 110.7 all-gather.3

commit v8 on v5

--- a/solution.py
+++ b/solution.py
@@ -8,29 +8,31 @@
 ITERS = 2
 
 
-def product_kernel(a_ref, b_ref, v_ref, prev_ref, misc_ref, rows_ref, cols_ref, owned_ref, out_ref, outb_ref):
+def product_kernel(a_ref, b_ref, v_ref, prev_ref, misc_ref, rows_ref, cols_ref, owned_ref, out_ref, *rest):
     nout = out_ref.shape[0]
     terms = a_ref.shape[0] // nout
     take_product = misc_ref[0] > 0
 
     def body(o, carry):
-        acc = None
+        sums = [None, None]
         for k in range(terms):
             t = o * terms + k
             d = jnp.dot(rows_ref[a_ref[t]], cols_ref[b_ref[t]], preferred_element_type=jnp.float32)
             d = jnp.where(v_ref[t] > 0, d, 0.0)
-            acc = d if acc is None else acc + d
+            sums[k % 2] = d if sums[k % 2] is None else sums[k % 2] + d
+        acc = sums[0] + sums[1]
         p = prev_ref[o]
         prev = jnp.where(p >= 0, owned_ref[jnp.maximum(p, 0)], 0.0)
         res = jnp.where(take_product, acc, 2.0 * prev - acc)
         out_ref[o] = res
-        outb_ref[o] = res.astype(outb_ref.dtype)
+        for outb_ref in rest:
+            outb_ref[o] = res.astype(outb_ref.dtype)
         return carry
 
     lax.fori_loop(0, nout, body, 0)
 
 
-def run_product(a_t, b_t, v_t, prev_t, misc, rows, cols, owned):
+def run_product(a_t, b_t, v_t, prev_t, misc, rows, cols, owned, with_rounded):
     nout, edge, _ = owned.shape
     max_terms = a_t.shape[0]
     smem = pl.BlockSpec(memory_space=pltpu.SMEM)
@@ -40,11 +42,9 @@
     return pl.pallas_call(
         product_kernel,
         in_specs=[smem] * 5 + [vmem] * 3,
-        out_specs=(vmem, vmem),
-        out_shape=(
-            jax.ShapeDtypeStruct(owned.shape, jnp.float32),
-            jax.ShapeDtypeStruct(owned.shape, jnp.bfloat16),
-        ),
+        out_specs=(vmem,) * (1 + with_rounded),
+        out_shape=(jax.ShapeDtypeStruct(owned.shape, jnp.float32),)
+        + (jax.ShapeDtypeStruct(owned.shape, jnp.bfloat16),) * with_rounded,
         cost_estimate=pl.CostEstimate(flops=flops, transcendentals=0, bytes_accessed=nbytes),
         compiler_params=pltpu.CompilerParams(vmem_limit_bytes=48 * 1024 * 1024),
     )(a_t, b_t, v_t, prev_t, misc, rows, cols, owned)
@@ -74,7 +74,7 @@
     return offs % grid_cols
 
 
-def purify_section(owned, panels, cur_list, next_list, trace_now, grid_rows, grid_cols, row_index, col_index):
+def purify_section(owned, panels, cur_list, next_list, trace_now, grid_rows, grid_cols, row_index, col_index, last):
     block_rows = owned.shape[0]
     slot_pairs = owned.shape[2]
     edge = owned.shape[4]
@@ -120,8 +120,10 @@
     ).reshape(-1)
     misc = (trace_now > occupied).astype(jnp.int32).reshape(1)
 
-    updated, rounded = run_product(a_t, b_t, v_t, prev_t, misc, rows, cols, owned4.reshape(nout, edge, edge))
-    return updated.reshape(owned.shape), rounded.reshape(owned.shape)
+    results = run_product(a_t, b_t, v_t, prev_t, misc, rows, cols, owned4.reshape(nout, edge, edge), int(not last))
+    if last:
+        return results[0].reshape(owned.shape), None
+    return results[0].reshape(owned.shape), results[1].reshape(owned.shape)
 
 
 def local_trace(owned, cur_list, grid_rows, grid_cols, row_index, col_index):
@@ -154,7 +156,7 @@
     for iteration in range(ITERS):
         current, rounded = purify_section(
             current, rounded, all_lists[iteration], all_lists[iteration + 1], traces[iteration],
-            grid_rows, grid_cols, row_index, col_index,
+            grid_rows, grid_cols, row_index, col_index, iteration == ITERS - 1,
         )
     return current
 

time: 275 us -> 275 us (level)
  no operation moved by 1% of the time
where the time goes in v8:
time: 275 us; the launch traced here: 274 us
  waiting for transfers between devices  96.6 us (35%)
  blocking collectives  57.9 us (21%)
  local copies, waits for them, and re-layouts  42.5 us (15%)
  Pallas kernels  30.3 us (11%)
  between operations  16.3 us (6%)
  other arithmetic  15.5 us (6%)
  starting transfers between devices  14.3 us (5%)
    all_gather x2, waiting for transfers between devices, purify_section(): cols = lax.all_gather(panels, 'row', axis=0, tiled=False)  53.4 us
    psum x1, blocking collectives, shards(): lax.psum(lax.psum(jnp.stack([diag_term, square_term]), 'col'), 'row')  42.4 us
    pallas_call x2, Pallas kernels, run_product(): pl.pallas_call(product_kernel, in_specs=[smem] * 5 + [vmem] * 3, out_spec...  30.3 us
    ppermute x2, waiting for transfers between devices, col_gather(): from_minus = lax.ppermute(x, 'col', plus2)  30.1 us
    unnamed x30, local copies, waits for them, and re-layouts  28.2 us
    psum x1, blocking collectives, shards(): lax.psum(jnp.stack([diag_term, square_term]), 'col')  15.5 us
    ppermute x2, waiting for transfers between devices, col_gather(): far_b = lax.ppermute(from_plus[half:], 'col', minus2)  6.67 us
    ppermute x2, waiting for transfers between devices, col_gather(): far_a = lax.ppermute(from_minus[:half], 'col', plus2)  6.36 us
  transfers between devices with their start and end apart: 16, of which 7 were waited for; matrix products, arithmetic and copies ran while one was open for 20% of the time, Pallas kernels for 0%

profile of v8, /device:TPU:0, one launch (start us, length us, event | category | flops | bytes accessed | tf_op | source)
XLA Modules:
  0.0 273.6 jit_solution(17963423405983052176)
XLA Ops:
  6.5 3.2 %bitcast_dynamic-update-slice_fusion.6 = (bf16[8,4,2,256,256]{4,3,2,1,0:T(8,128)(2,1)}, bf16[4,1,2,1,256,256]{5,4,3,2,1,0:T(8,128)(2,1)}) fusion(f32[4,1,2,1,256,256]{5,4,3,2,1,0:T(8,128)} %param.7), kind=kLoop, calls=%fused_computation.18 | loop fusion | flops 524287 | bytes 4194304
  9.8 2.1 collective-permute-start
  11.9 2.2 collective-permute-start.1
  14.1 0.8 copy.69
  15.5 0.8 copy.80
  17.2 0.8 copy.73
  19.8 1.9 fusion
  22.4 2.5 multiply_reduce_fusion
  25.4 1.3 pad_maximum_fusion.2
  30.1 7.2 %collective-permute-done = bf16[4,2,256,256]{3,2,1,0:T(8,128)(2,1)S(1)} collective-permute-done((bf16[4,2,256,256]{3,2,1,0:T(8,128)(2,1)}, bf16[4,2,256,256]{3,2,1,0:T(8,128)(2,1)S(1)}, u32[]{:S(2)}, u32[]{:S(2)}) %collective-permute-start) | collective-permute-done | bytes 1048608 | tf_op jit(solution)/shard_map/ppermute | solution.py:58
  37.4 1.6 pad_maximum_fusion
  39.0 15.5 %psum.14 = f32[2]{0:T(128)S(1)} all-reduce(f32[2]{0:T(128)S(1)} %pad_maximum_fusion.2), channel_id=1, replica_groups=mesh['row'=16,'col'=8] {'col'}, use_global_device_ids=true, to_apply=%region_8.9 | all-reduce | flops 2 | bytes 16 | tf_op jit(solution)/shard_map/psum | solution.py:152
  54.5 0.8 slice.43
  55.4 42.4 %psum.15 = f32[2]{0:T(128)S(1)} all-reduce(f32[2]{0:T(128)S(1)} %psum.14), channel_id=1, replica_groups=mesh['row'=16,'col'=8] {'row'}, use_global_device_ids=true, to_apply=%region_9.10 | all-reduce | flops 2 | bytes 16 | tf_op jit(solution)/shard_map/psum | solution.py:152
  98.1 0.9 slice.44
  98.9 3.2 %collective-permute-start.3 = (bf16[2,2,256,256]{3,2,1,0:T(8,128)(2,1)}, bf16[2,2,256,256]{3,2,1,0:T(8,128)(2,1)}, u32[]{:S(2)}, u32[]{:S(2)}) collective-permute-start(bf16[2,2,256,256]{3,2,1,0:T(8,128)(2,1)} %slice.44), channel_id=1, source_target_pairs={{0,6},{1,7},{2,0},{3,1},{4,2},{5,3},{6,4},{7,5},{8,14},{9,15},{10,... | collective-permute-start | bytes 1572872 | tf_op jit(solution)/shard_map/ppermute | solution.py:62
  103.7 1.2 constant_dynamic-update-slice_fusion.1
  105.0 4.1 %collective-permute-done.3 = bf16[2,2,256,256]{3,2,1,0:T(8,128)(2,1)} collective-permute-done((bf16[2,2,256,256]{3,2,1,0:T(8,128)(2,1)}, bf16[2,2,256,256]{3,2,1,0:T(8,128)(2,1)}, u32[]{:S(2)}, u32[]{:S(2)}) %collective-permute-start.3) | collective-permute-done | bytes 524320 | tf_op jit(solution)/shard_map/ppermute | solution.py:62
  109.1 1.1 constant_dynamic-update-slice_fusion
  110.3 1.1 constant_dynamic-update-slice_fusion.4
  111.4 2.3 constant_dynamic-update-slice_fusion.3
  113.7 1.1 bitcast_dynamic-update-slice_fusion.5
  114.7 2.3 bitcast_dynamic-update-slice_fusion.4
  117.0 3.1 %constant_dynamic-update-slice_fusion.2 = bf16[8,4,2,256,256]{4,3,2,1,0:T(8,128)(2,1)} fusion(bf16[8,4,2,256,256]{4,3,2,1,0:T(8,128)(2,1)} %bitcast_dynamic-update-slice_fusion.4, bf16[2,4,2,256,256]{4,3,2,1,0:T(8,128)(2,1)} %collective-permute-done.5), kind=kLoop, calls=%fused_computation.22 | loop fusion | bytes 4194304
  120.1 1.0 bitcast_dynamic-update-slice_fusion.3
  121.2 3.0 %all-gather.6.cloned.1.call-done = bf16[64,1,2,1,256,256]{5,4,3,2,1,0:T(8,128)(2,1)} async-done(((bf16[4,1,2,1,256,256]{5,4,3,2,1,0:T(8,128)(2,1)}), bf16[64,1,2,1,256,256]{5,4,3,2,1,0:T(8,128)(2,1)}) %all-gather.6.cloned.1.call-update) | async-done | bytes 16777232 | tf_op jit(solution)/shard_map/all_gather | solution.py:87
  124.1 15.0 %shard_map.46 = (f32[8,256,256]{2,1,0:T(8,128)S(1)}, bf16[8,256,256]{2,1,0:T(8,128)(2,1)}) custom-call(s32[128]{0:T(128)S(1)} %reshape.618.a_ref, s32[128]{0:T(128)S(1)} %reshape.628.b_ref, s32[128]{0:T(128)S(1)} %reshape.640.v_ref, s32[8]{0:T(128)S(1)} %reshape.629.prev_ref, s32[1]{0:T(128)S(6)} %reshape.630.misc_ref, bf16[64,256,256]{2,1,0:T(8,128)(2,1)} %bitcast.87, ...), custom_call_target="tpu_custom_call" | custom-call | flops 4294967296 | bytes 29360128 | tf_op jit(solution)/shard_map/pallas_call | solution.py:42
  139.2 1.4 copy-done.1
  140.6 1.6 collective-permute-start.7
  142.2 1.7 collective-permute-start.8
  144.0 22.9 %collective-permute-done.7 = bf16[4,2,256,256]{3,2,1,0:T(8,128)(2,1)S(1)} collective-permute-done((bf16[4,2,256,256]{3,2,1,0:T(8,128)(2,1)}, bf16[4,2,256,256]{3,2,1,0:T(8,128)(2,1)S(1)}, u32[]{:S(2)}, u32[]{:S(2)}) %collective-permute-start.7) | collective-permute-done | bytes 1048608 | tf_op jit(solution)/shard_map/ppermute | solution.py:58
  166.9 1.6 pad_maximum_fusion.1
  169.3 0.8 slice.45
  170.1 1.6 collective-permute-start.9
  174.6 0.8 slice.46
  175.5 1.6 collective-permute-start.10
  177.5 2.3 constant_dynamic-update-slice_fusion.10
  179.7 6.4 %collective-permute-done.9 = bf16[2,2,256,256]{3,2,1,0:T(8,128)(2,1)} collective-permute-done((bf16[2,2,256,256]{3,2,1,0:T(8,128)(2,1)}, bf16[2,2,256,256]{3,2,1,0:T(8,128)(2,1)}, u32[]{:S(2)}, u32[]{:S(2)}) %collective-permute-start.9) | collective-permute-done | bytes 524320 | tf_op jit(solution)/shard_map/ppermute | solution.py:61
  186.1 1.1 constant_dynamic-update-slice_fusion.6
  187.2 2.6 collective-permute-done.10
  189.9 2.4 constant_dynamic-update-slice_fusion.9
  192.2 2.3 constant_dynamic-update-slice_fusion.8
  194.6 1.1 bitcast_dynamic-update-slice_fusion.2
  195.6 1.0 bitcast_dynamic-update-slice_fusion.1
  196.7 3.2 %constant_dynamic-update-slice_fusion.7 = bf16[8,4,2,256,256]{4,3,2,1,0:T(8,128)(2,1)} fusion(bf16[8,4,2,256,256]{4,3,2,1,0:T(8,128)(2,1)} %bitcast_dynamic-update-slice_fusion.1, bf16[2,4,2,256,256]{4,3,2,1,0:T(8,128)(2,1)} %collective-permute-done.12), kind=kLoop, calls=%fused_computation.27 | loop fusion | bytes 4194304
  199.9 1.0 bitcast_dynamic-update-slice_fusion
  201.0 50.5 %all-gather.4.cloned.1.call-done = bf16[16,4,2,256,256]{4,3,2,1,0:T(8,128)(2,1)} async-done(((bf16[1,4,2,256,256]{4,3,2,1,0:T(8,128)(2,1)}), bf16[16,4,2,256,256]{4,3,2,1,0:T(8,128)(2,1)}) %all-gather.4.cloned.1.call-update) | async-done | bytes 16777232 | tf_op jit(solution)/shard_map/all_gather | solution.py:87
  251.4 15.3 %shard_map.47 = f32[8,256,256]{2,1,0:T(8,128)} custom-call(s32[128]{0:T(128)S(1)} %reshape.618.a_ref, s32[128]{0:T(128)S(1)} %reshape.621.b_ref, s32[128]{0:T(128)S(1)} %reshape.637.v_ref, s32[8]{0:T(128)S(1)} %reshape.623.prev_ref, s32[1]{0:T(128)} %bitcast.24.misc_ref, bf16[64,256,256]{2,1,0:T(8,128)(2,1)} %bitcast.46.rows_ref, ...), custom_call_target="tpu_custom_call" | custom-call | flops 4294967296 | bytes 29360128 | tf_op jit(solution)/shard_map/pallas_call | solution.py:42
  (101 shorter events, 11.6 us)
Async XLA Ops:
  6.5 117.6 %all-gather.6.cloned.1.call-start = ((), (), s32[]{:S(2)}) async-start(), calls=%async_computation.1 | async-start | bytes 17825792 | tf_op jit(solution)/shard_map/all_gather | solution.py:87
  9.7 241.7 %all-gather.4.cloned.1.call-start = ((), (), s32[]{:S(2)}) async-start(), calls=%async_computation | async-start | bytes 17825792 | tf_op jit(solution)/shard_map/all_gather | solution.py:87
  9.8 27.6 %collective-permute-start = (bf16[4,2,256,256]{3,2,1,0:T(8,128)(2,1)}, bf16[4,2,256,256]{3,2,1,0:T(8,128)(2,1)S(1)}, u32[]{:S(2)}, u32[]{:S(2)}) collective-permute-start(bf16[4,2,256,256]{3,2,1,0:T(8,128)(2,1)} %bitcast.88), channel_id=1, source_target_pairs={{0,2},{1,3},{2,4},{3,5},{4,6},{5,7},{6,0},{7,1},{8,10},{9,11},{10,... | collective-permute-start | bytes 3145736 | tf_op jit(solution)/shard_map/ppermute | solution.py:58
  11.9 25.5 %collective-permute-start.1 = (bf16[4,2,256,256]{3,2,1,0:T(8,128)(2,1)}, bf16[4,2,256,256]{3,2,1,0:T(8,128)(2,1)S(1)}, u32[]{:S(2)}, u32[]{:S(2)}) collective-permute-start(bf16[4,2,256,256]{3,2,1,0:T(8,128)(2,1)} %bitcast.89), channel_id=1, source_target_pairs={{0,6},{1,7},{2,0},{3,1},{4,2},{5,3},{6,4},{7,5},{8,14},{9,15},{10,... | collective-permute-start | bytes 3145736 | tf_op jit(solution)/shard_map/ppermute | solution.py:59
  14.1 100.6 %collective-permute-start.4 = (bf16[4,2,256,256]{3,2,1,0:T(8,128)(2,1)}, bf16[4,2,256,256]{3,2,1,0:T(8,128)(2,1)}, u32[]{:S(2)}, u32[]{:S(2)}) collective-permute-start(bf16[4,2,256,256]{3,2,1,0:T(8,128)(2,1)} %bitcast.90), channel_id=1, source_target_pairs={{0,1},{1,0},{2,3},{3,2},{4,5},{5,4},{6,7},{7,6},{8,9},{9,8},{10,11... | collective-permute-start | bytes 3145736 | tf_op jit(solution)/shard_map/ppermute | solution.py:60
  37.4 64.7 %copy-start.3 = (bf16[4,2,256,256]{3,2,1,0:T(8,128)(2,1)}, bf16[4,2,256,256]{3,2,1,0:T(8,128)(2,1)S(1)}, u32[]{:S(2)}) copy-start(bf16[4,2,256,256]{3,2,1,0:T(8,128)(2,1)S(1)} %collective-permute-done.1) | copy-start | bytes 3145732
  39.0 78.0 %collective-permute-start.5 = (bf16[2,4,2,256,256]{4,3,2,1,0:T(8,128)(2,1)}, bf16[2,4,2,256,256]{4,3,2,1,0:T(8,128)(2,1)}, u32[]{:S(2)}, u32[]{:S(2)}) collective-permute-start(bf16[2,4,2,256,256]{4,3,2,1,0:T(8,128)(2,1)} %pad_maximum_fusion), channel_id=1, source_target_pairs={{0,1},{1,0},{2,3},{3,2},{4,5},{5,4},{6,7},{7,6},{8,9},{9,8},{10,11... | collective-permute-start | bytes 6291464 | tf_op jit(solution)/shard_map/ppermute | solution.py:64
  55.4 48.4 %collective-permute-start.2 = (bf16[2,2,256,256]{3,2,1,0:T(8,128)(2,1)}, bf16[2,2,256,256]{3,2,1,0:T(8,128)(2,1)}, u32[]{:S(2)}, u32[]{:S(2)}) collective-permute-start(bf16[2,2,256,256]{3,2,1,0:T(8,128)(2,1)} %slice.43), channel_id=1, source_target_pairs={{0,2},{1,3},{2,4},{3,5},{4,6},{5,7},{6,0},{7,1},{8,10},{9,11},{10,... | collective-permute-start | bytes 1572872 | tf_op jit(solution)/shard_map/ppermute | solution.py:61
  98.9 10.2 %collective-permute-start.3 = (bf16[2,2,256,256]{3,2,1,0:T(8,128)(2,1)}, bf16[2,2,256,256]{3,2,1,0:T(8,128)(2,1)}, u32[]{:S(2)}, u32[]{:S(2)}) collective-permute-start(bf16[2,2,256,256]{3,2,1,0:T(8,128)(2,1)} %slice.44), channel_id=1, source_target_pairs={{0,6},{1,7},{2,0},{3,1},{4,2},{5,3},{6,4},{7,5},{8,14},{9,15},{10,... | collective-permute-start | bytes 1572872 | tf_op jit(solution)/shard_map/ppermute | solution.py:62
  103.7 20.4 %copy-start = (f32[4,1,2,1,256,256]{5,4,3,2,1,0:T(8,128)S(1)}, f32[4,1,2,1,256,256]{5,4,3,2,1,0:T(8,128)}, u32[]{:S(2)}) copy-start(f32[4,1,2,1,256,256]{5,4,3,2,1,0:T(8,128)} %param.7) | copy-start | bytes 6291460
  110.2 9.9 %collective-permute-start.6 = (bf16[4,2,256,256]{3,2,1,0:T(8,128)(2,1)S(1)}, bf16[4,2,256,256]{3,2,1,0:T(8,128)(2,1)S(1)}, u32[]{:S(2)}, u32[]{:S(2)}) collective-permute-start(bf16[4,2,256,256]{3,2,1,0:T(8,128)(2,1)S(1)} %constant_dynamic-update-slice_fusion), channel_id=1, source_target_pairs={{0,1},{1,0},{2,3},{3,2},{4,5},{5,4},{6,7},{7,6},{8,9},{9,8},{10,11... | collective-permute-start | bytes 3145736 | tf_op jit(solution)/shard_map/ppermute | solution.py:65
  139.2 1.4 copy-start.1
  140.6 26.3 %collective-permute-start.7 = (bf16[4,2,256,256]{3,2,1,0:T(8,128)(2,1)}, bf16[4,2,256,256]{3,2,1,0:T(8,128)(2,1)S(1)}, u32[]{:S(2)}, u32[]{:S(2)}) collective-permute-start(bf16[4,2,256,256]{3,2,1,0:T(8,128)(2,1)} %bitcast.40), channel_id=1, source_target_pairs={{0,2},{1,3},{2,4},{3,5},{4,6},{5,7},{6,0},{7,1},{8,10},{9,11},{10,... | collective-permute-start | bytes 3145736 | tf_op jit(solution)/shard_map/ppermute | solution.py:58
  142.2 24.7 %collective-permute-start.8 = (bf16[4,2,256,256]{3,2,1,0:T(8,128)(2,1)}, bf16[4,2,256,256]{3,2,1,0:T(8,128)(2,1)S(1)}, u32[]{:S(2)}, u32[]{:S(2)}) collective-permute-start(bf16[4,2,256,256]{3,2,1,0:T(8,128)(2,1)} %bitcast.40), channel_id=1, source_target_pairs={{0,6},{1,7},{2,0},{3,1},{4,2},{5,3},{6,4},{7,5},{8,14},{9,15},{10,... | collective-permute-start | bytes 3145736 | tf_op jit(solution)/shard_map/ppermute | solution.py:59
  166.8 5.6 %copy-start.4 = (bf16[4,2,256,256]{3,2,1,0:T(8,128)(2,1)}, bf16[4,2,256,256]{3,2,1,0:T(8,128)(2,1)S(1)}, u32[]{:S(2)}) copy-start(bf16[4,2,256,256]{3,2,1,0:T(8,128)(2,1)S(1)} %collective-permute-done.7) | copy-start | bytes 3145732
  166.9 10.6 %copy-start.5 = (bf16[4,2,256,256]{3,2,1,0:T(8,128)(2,1)}, bf16[4,2,256,256]{3,2,1,0:T(8,128)(2,1)S(1)}, u32[]{:S(2)}) copy-start(bf16[4,2,256,256]{3,2,1,0:T(8,128)(2,1)S(1)} %collective-permute-done.8) | copy-start | bytes 3145732
  168.5 28.2 %collective-permute-start.12 = (bf16[2,4,2,256,256]{4,3,2,1,0:T(8,128)(2,1)}, bf16[2,4,2,256,256]{4,3,2,1,0:T(8,128)(2,1)}, u32[]{:S(2)}, u32[]{:S(2)}) collective-permute-start(bf16[2,4,2,256,256]{4,3,2,1,0:T(8,128)(2,1)} %pad_maximum_fusion.1), channel_id=1, source_target_pairs={{0,1},{1,0},{2,3},{3,2},{4,5},{5,4},{6,7},{7,6},{8,9},{9,8},{10,11... | collective-permute-start | bytes 6291464 | tf_op jit(solution)/shard_map/ppermute | solution.py:64
  170.1 16.0 %collective-permute-start.9 = (bf16[2,2,256,256]{3,2,1,0:T(8,128)(2,1)}, bf16[2,2,256,256]{3,2,1,0:T(8,128)(2,1)}, u32[]{:S(2)}, u32[]{:S(2)}) collective-permute-start(bf16[2,2,256,256]{3,2,1,0:T(8,128)(2,1)} %slice.45), channel_id=1, source_target_pairs={{0,2},{1,3},{2,4},{3,5},{4,6},{5,7},{6,0},{7,1},{8,10},{9,11},{10,... | collective-permute-start | bytes 1572872 | tf_op jit(solution)/shard_map/ppermute | solution.py:61
  175.5 14.3 %collective-permute-start.10 = (bf16[2,2,256,256]{3,2,1,0:T(8,128)(2,1)}, bf16[2,2,256,256]{3,2,1,0:T(8,128)(2,1)S(1)}, u32[]{:S(2)}, u32[]{:S(2)}) collective-permute-start(bf16[2,2,256,256]{3,2,1,0:T(8,128)(2,1)} %slice.46), channel_id=1, source_target_pairs={{0,6},{1,7},{2,0},{3,1},{4,2},{5,3},{6,4},{7,5},{8,14},{9,15},{10,... | collective-permute-start | bytes 1572872 | tf_op jit(solution)/shard_map/ppermute | solution.py:62
  177.4 18.2 %collective-permute-start.11 = (bf16[4,2,256,256]{3,2,1,0:T(8,128)(2,1)}, bf16[4,2,256,256]{3,2,1,0:T(8,128)(2,1)S(1)}, u32[]{:S(2)}, u32[]{:S(2)}) collective-permute-start(bf16[4,2,256,256]{3,2,1,0:T(8,128)(2,1)} %bitcast.40), channel_id=1, source_target_pairs={{0,1},{1,0},{2,3},{3,2},{4,5},{5,4},{6,7},{7,6},{8,9},{9,8},{10,11... | collective-permute-start | bytes 3145736 | tf_op jit(solution)/shard_map/ppermute | solution.py:60
  179.7 71.7 %copy-start.2 = (f32[8,256,256]{2,1,0:T(8,128)S(1)}, f32[8,256,256]{2,1,0:T(8,128)}, u32[]{:S(2)}) copy-start(f32[8,256,256]{2,1,0:T(8,128)} %copy-done.1) | copy-start | bytes 6291460
  189.8 10.1 %collective-permute-start.13 = (bf16[4,2,256,256]{3,2,1,0:T(8,128)(2,1)S(1)}, bf16[4,2,256,256]{3,2,1,0:T(8,128)(2,1)S(1)}, u32[]{:S(2)}, u32[]{:S(2)}) collective-permute-start(bf16[4,2,256,256]{3,2,1,0:T(8,128)(2,1)S(1)} %constant_dynamic-update-slice_fusion.5), channel_id=1, source_target_pairs={{0,1},{1,0},{2,3},{3,2},{4,5},{5,4},{6,7},{7,6},{8,9},{9,8},{10,11... | collective-permute-start | bytes 3145736 | tf_op jit(solution)/shard_map/ppermute | solution.py:65
Sparse Core Ops, SparseCore 0:
  9.8 114.2 all-gather.5
  140.7 110.6 all-gather.3

commit v9 on v5

--- a/solution.py
+++ b/solution.py
@@ -27,7 +27,7 @@
         outb_ref[o] = res.astype(outb_ref.dtype)
         return carry
 
-    lax.fori_loop(0, nout, body, 0)
+    lax.fori_loop(0, nout, body, 0, unroll=True)
 
 
 def run_product(a_t, b_t, v_t, prev_t, misc, rows, cols, owned):

time: 275 us -> 273 us (level)
  transfers between devices with their start and end apart: 16 -> 16, of which waited for: 7 -> 8; matrix products, arithmetic and copies ran while one was open for 20% -> 20% of each run, Pallas kernels for 0% -> 0%
where the time goes in v9:
time: 273 us; the launch traced here: 272 us
  waiting for transfers between devices  96.7 us (35%)
  blocking collectives  57.9 us (21%)
  local copies, waits for them, and re-layouts  42.5 us (16%)
  Pallas kernels  28.3 us (10%)
  between operations  16.3 us (6%)
  other arithmetic  15.5 us (6%)
  starting transfers between devices  14.3 us (5%)
    all_gather x2, waiting for transfers between devices, purify_section(): cols = lax.all_gather(panels, 'row', axis=0, tiled=False)  53.5 us
    psum x1, blocking collectives, shards(): lax.psum(lax.psum(jnp.stack([diag_term, square_term]), 'col'), 'row')  42.4 us
    ppermute x2, waiting for transfers between devices, col_gather(): from_minus = lax.ppermute(x, 'col', plus2)  30.1 us
    pallas_call x2, Pallas kernels, run_product(): pl.pallas_call(product_kernel, in_specs=[smem] * 5 + [vmem] * 3, out_spec...  28.3 us
    unnamed x30, local copies, waits for them, and re-layouts  28.2 us
    psum x1, blocking collectives, shards(): lax.psum(jnp.stack([diag_term, square_term]), 'col')  15.5 us
    ppermute x2, waiting for transfers between devices, col_gather(): far_b = lax.ppermute(from_plus[half:], 'col', minus2)  6.68 us
    ppermute x2, waiting for transfers between devices, col_gather(): far_a = lax.ppermute(from_minus[:half], 'col', plus2)  6.28 us
  transfers between devices with their start and end apart: 16, of which 8 were waited for; matrix products, arithmetic and copies ran while one was open for 20% of the time, Pallas kernels for 0%

profile of v9, /device:TPU:0, one launch (start us, length us, event | category | flops | bytes accessed | tf_op | source)
XLA Modules:
  0.0 271.5 jit_solution(3980193052216924136)
XLA Ops:
  6.5 3.2 %bitcast_dynamic-update-slice_fusion.6 = (bf16[8,4,2,256,256]{4,3,2,1,0:T(8,128)(2,1)}, bf16[4,1,2,1,256,256]{5,4,3,2,1,0:T(8,128)(2,1)}) fusion(f32[4,1,2,1,256,256]{5,4,3,2,1,0:T(8,128)} %param.7), kind=kLoop, calls=%fused_computation.18 | loop fusion | flops 524287 | bytes 4194304
  9.8 2.1 collective-permute-start
  11.9 2.2 collective-permute-start.1
  14.1 0.8 copy.69
  15.5 0.8 copy.80
  17.2 0.8 copy.73
  19.8 1.9 fusion
  22.4 2.5 multiply_reduce_fusion
  25.4 1.3 pad_maximum_fusion.2
  30.1 7.2 %collective-permute-done = bf16[4,2,256,256]{3,2,1,0:T(8,128)(2,1)S(1)} collective-permute-done((bf16[4,2,256,256]{3,2,1,0:T(8,128)(2,1)}, bf16[4,2,256,256]{3,2,1,0:T(8,128)(2,1)S(1)}, u32[]{:S(2)}, u32[]{:S(2)}) %collective-permute-start) | collective-permute-done | bytes 1048608 | tf_op jit(solution)/shard_map/ppermute | solution.py:58
  37.4 1.6 pad_maximum_fusion
  39.0 15.5 %psum.14 = f32[2]{0:T(128)S(1)} all-reduce(f32[2]{0:T(128)S(1)} %pad_maximum_fusion.2), channel_id=1, replica_groups=mesh['row'=16,'col'=8] {'col'}, use_global_device_ids=true, to_apply=%region_8.9 | all-reduce | flops 2 | bytes 16 | tf_op jit(solution)/shard_map/psum | solution.py:150
  54.5 0.8 slice.43
  55.3 42.4 %psum.15 = f32[2]{0:T(128)S(1)} all-reduce(f32[2]{0:T(128)S(1)} %psum.14), channel_id=1, replica_groups=mesh['row'=16,'col'=8] {'row'}, use_global_device_ids=true, to_apply=%region_9.10 | all-reduce | flops 2 | bytes 16 | tf_op jit(solution)/shard_map/psum | solution.py:150
  98.0 0.9 slice.44
  98.9 3.2 %collective-permute-start.3 = (bf16[2,2,256,256]{3,2,1,0:T(8,128)(2,1)}, bf16[2,2,256,256]{3,2,1,0:T(8,128)(2,1)}, u32[]{:S(2)}, u32[]{:S(2)}) collective-permute-start(bf16[2,2,256,256]{3,2,1,0:T(8,128)(2,1)} %slice.44), channel_id=1, source_target_pairs={{0,6},{1,7},{2,0},{3,1},{4,2},{5,3},{6,4},{7,5},{8,14},{9,15},{10,... | collective-permute-start | bytes 1572872 | tf_op jit(solution)/shard_map/ppermute | solution.py:62
  103.7 1.2 constant_dynamic-update-slice_fusion.1
  105.0 4.1 %collective-permute-done.3 = bf16[2,2,256,256]{3,2,1,0:T(8,128)(2,1)} collective-permute-done((bf16[2,2,256,256]{3,2,1,0:T(8,128)(2,1)}, bf16[2,2,256,256]{3,2,1,0:T(8,128)(2,1)}, u32[]{:S(2)}, u32[]{:S(2)}) %collective-permute-start.3) | collective-permute-done | bytes 524320 | tf_op jit(solution)/shard_map/ppermute | solution.py:62
  109.1 1.1 constant_dynamic-update-slice_fusion
  110.2 1.1 constant_dynamic-update-slice_fusion.4
  111.3 2.3 constant_dynamic-update-slice_fusion.3
  113.6 1.1 bitcast_dynamic-update-slice_fusion.5
  114.7 2.3 bitcast_dynamic-update-slice_fusion.4
  117.0 3.1 %constant_dynamic-update-slice_fusion.2 = bf16[8,4,2,256,256]{4,3,2,1,0:T(8,128)(2,1)} fusion(bf16[8,4,2,256,256]{4,3,2,1,0:T(8,128)(2,1)} %bitcast_dynamic-update-slice_fusion.4, bf16[2,4,2,256,256]{4,3,2,1,0:T(8,128)(2,1)} %collective-permute-done.5), kind=kLoop, calls=%fused_computation.22 | loop fusion | bytes 4194304
  120.1 1.0 bitcast_dynamic-update-slice_fusion.3
  121.1 3.0 %all-gather.6.cloned.1.call-done = bf16[64,1,2,1,256,256]{5,4,3,2,1,0:T(8,128)(2,1)} async-done(((bf16[4,1,2,1,256,256]{5,4,3,2,1,0:T(8,128)(2,1)}), bf16[64,1,2,1,256,256]{5,4,3,2,1,0:T(8,128)(2,1)}) %all-gather.6.cloned.1.call-update) | async-done | bytes 16777232 | tf_op jit(solution)/shard_map/all_gather | solution.py:87
  124.1 13.8 %shard_map.46 = (f32[8,256,256]{2,1,0:T(8,128)S(1)}, bf16[8,256,256]{2,1,0:T(8,128)(2,1)}) custom-call(s32[128]{0:T(128)S(1)} %reshape.618.a_ref, s32[128]{0:T(128)S(1)} %reshape.628.b_ref, s32[128]{0:T(128)S(1)} %reshape.640.v_ref, s32[8]{0:T(128)S(1)} %reshape.629.prev_ref, s32[1]{0:T(128)S(6)} %reshape.630.misc_ref, bf16[64,256,256]{2,1,0:T(8,128)(2,1)} %bitcast.87, ...), custom_call_target="tpu_custom_call" | custom-call | flops 4294967296 | bytes 29360128 | tf_op jit(solution)/shard_map/pallas_call | solution.py:40
  137.9 1.4 copy-done.1
  139.3 1.6 collective-permute-start.7
  140.9 1.7 collective-permute-start.8
  142.7 22.8 %collective-permute-done.7 = bf16[4,2,256,256]{3,2,1,0:T(8,128)(2,1)S(1)} collective-permute-done((bf16[4,2,256,256]{3,2,1,0:T(8,128)(2,1)}, bf16[4,2,256,256]{3,2,1,0:T(8,128)(2,1)S(1)}, u32[]{:S(2)}, u32[]{:S(2)}) %collective-permute-start.7) | collective-permute-done | bytes 1048608 | tf_op jit(solution)/shard_map/ppermute | solution.py:58
  165.6 1.7 pad_maximum_fusion.1
  168.1 0.8 slice.45
  168.9 1.5 collective-permute-start.9
  173.3 0.8 slice.46
  174.2 1.7 collective-permute-start.10
  176.2 2.3 constant_dynamic-update-slice_fusion.10
  178.5 6.3 %collective-permute-done.9 = bf16[2,2,256,256]{3,2,1,0:T(8,128)(2,1)} collective-permute-done((bf16[2,2,256,256]{3,2,1,0:T(8,128)(2,1)}, bf16[2,2,256,256]{3,2,1,0:T(8,128)(2,1)}, u32[]{:S(2)}, u32[]{:S(2)}) %collective-permute-start.9) | collective-permute-done | bytes 524320 | tf_op jit(solution)/shard_map/ppermute | solution.py:61
  184.8 1.1 constant_dynamic-update-slice_fusion.6
  185.8 2.6 collective-permute-done.10
  188.5 2.4 constant_dynamic-update-slice_fusion.9
  190.9 2.3 constant_dynamic-update-slice_fusion.8
  193.2 1.1 bitcast_dynamic-update-slice_fusion.2
  194.3 1.0 bitcast_dynamic-update-slice_fusion.1
  195.3 3.2 %constant_dynamic-update-slice_fusion.7 = bf16[8,4,2,256,256]{4,3,2,1,0:T(8,128)(2,1)} fusion(bf16[8,4,2,256,256]{4,3,2,1,0:T(8,128)(2,1)} %bitcast_dynamic-update-slice_fusion.1, bf16[2,4,2,256,256]{4,3,2,1,0:T(8,128)(2,1)} %collective-permute-done.12), kind=kLoop, calls=%fused_computation.27 | loop fusion | bytes 4194304
  198.6 1.0 bitcast_dynamic-update-slice_fusion
  199.6 50.6 %all-gather.4.cloned.1.call-done = bf16[16,4,2,256,256]{4,3,2,1,0:T(8,128)(2,1)} async-done(((bf16[1,4,2,256,256]{4,3,2,1,0:T(8,128)(2,1)}), bf16[16,4,2,256,256]{4,3,2,1,0:T(8,128)(2,1)}) %all-gather.4.cloned.1.call-update) | async-done | bytes 16777232 | tf_op jit(solution)/shard_map/all_gather | solution.py:87
  250.2 14.5 %shard_map.47 = (f32[8,256,256]{2,1,0:T(8,128)}, bf16[8,256,256]{2,1,0:T(8,128)(2,1)}) custom-call(s32[128]{0:T(128)S(1)} %reshape.618.a_ref, s32[128]{0:T(128)S(1)} %reshape.621.b_ref, s32[128]{0:T(128)S(1)} %reshape.637.v_ref, s32[8]{0:T(128)S(1)} %reshape.623.prev_ref, s32[1]{0:T(128)} %bitcast.24.misc_ref, bf16[64,256,256]{2,1,0:T(8,128)(2,1)} %bitcast.46.rows_ref, ...), custom_call_target="tpu_custom_call" | custom-call | flops 4294967296 | bytes 29360128 | tf_op jit(solution)/shard_map/pallas_call | solution.py:40
  (101 shorter events, 11.6 us)
Async XLA Ops:
  6.5 117.6 %all-gather.6.cloned.1.call-start = ((), (), s32[]{:S(2)}) async-start(), calls=%async_computation.1 | async-start | bytes 17825792 | tf_op jit(solution)/shard_map/all_gather | solution.py:87
  9.7 240.4 %all-gather.4.cloned.1.call-start = ((), (), s32[]{:S(2)}) async-start(), calls=%async_computation | async-start | bytes 17825792 | tf_op jit(solution)/shard_map/all_gather | solution.py:87
  9.8 27.6 %collective-permute-start = (bf16[4,2,256,256]{3,2,1,0:T(8,128)(2,1)}, bf16[4,2,256,256]{3,2,1,0:T(8,128)(2,1)S(1)}, u32[]{:S(2)}, u32[]{:S(2)}) collective-permute-start(bf16[4,2,256,256]{3,2,1,0:T(8,128)(2,1)} %bitcast.88), channel_id=1, source_target_pairs={{0,2},{1,3},{2,4},{3,5},{4,6},{5,7},{6,0},{7,1},{8,10},{9,11},{10,... | collective-permute-start | bytes 3145736 | tf_op jit(solution)/shard_map/ppermute | solution.py:58
  11.9 25.5 %collective-permute-start.1 = (bf16[4,2,256,256]{3,2,1,0:T(8,128)(2,1)}, bf16[4,2,256,256]{3,2,1,0:T(8,128)(2,1)S(1)}, u32[]{:S(2)}, u32[]{:S(2)}) collective-permute-start(bf16[4,2,256,256]{3,2,1,0:T(8,128)(2,1)} %bitcast.89), channel_id=1, source_target_pairs={{0,6},{1,7},{2,0},{3,1},{4,2},{5,3},{6,4},{7,5},{8,14},{9,15},{10,... | collective-permute-start | bytes 3145736 | tf_op jit(solution)/shard_map/ppermute | solution.py:59
  14.1 100.6 %collective-permute-start.4 = (bf16[4,2,256,256]{3,2,1,0:T(8,128)(2,1)}, bf16[4,2,256,256]{3,2,1,0:T(8,128)(2,1)}, u32[]{:S(2)}, u32[]{:S(2)}) collective-permute-start(bf16[4,2,256,256]{3,2,1,0:T(8,128)(2,1)} %bitcast.90), channel_id=1, source_target_pairs={{0,1},{1,0},{2,3},{3,2},{4,5},{5,4},{6,7},{7,6},{8,9},{9,8},{10,11... | collective-permute-start | bytes 3145736 | tf_op jit(solution)/shard_map/ppermute | solution.py:60
  37.4 64.7 %copy-start.3 = (bf16[4,2,256,256]{3,2,1,0:T(8,128)(2,1)}, bf16[4,2,256,256]{3,2,1,0:T(8,128)(2,1)S(1)}, u32[]{:S(2)}) copy-start(bf16[4,2,256,256]{3,2,1,0:T(8,128)(2,1)S(1)} %collective-permute-done.1) | copy-start | bytes 3145732
  39.0 78.0 %collective-permute-start.5 = (bf16[2,4,2,256,256]{4,3,2,1,0:T(8,128)(2,1)}, bf16[2,4,2,256,256]{4,3,2,1,0:T(8,128)(2,1)}, u32[]{:S(2)}, u32[]{:S(2)}) collective-permute-start(bf16[2,4,2,256,256]{4,3,2,1,0:T(8,128)(2,1)} %pad_maximum_fusion), channel_id=1, source_target_pairs={{0,1},{1,0},{2,3},{3,2},{4,5},{5,4},{6,7},{7,6},{8,9},{9,8},{10,11... | collective-permute-start | bytes 6291464 | tf_op jit(solution)/shard_map/ppermute | solution.py:64
  55.3 48.4 %collective-permute-start.2 = (bf16[2,2,256,256]{3,2,1,0:T(8,128)(2,1)}, bf16[2,2,256,256]{3,2,1,0:T(8,128)(2,1)}, u32[]{:S(2)}, u32[]{:S(2)}) collective-permute-start(bf16[2,2,256,256]{3,2,1,0:T(8,128)(2,1)} %slice.43), channel_id=1, source_target_pairs={{0,2},{1,3},{2,4},{3,5},{4,6},{5,7},{6,0},{7,1},{8,10},{9,11},{10,... | collective-permute-start | bytes 1572872 | tf_op jit(solution)/shard_map/ppermute | solution.py:61
  98.9 10.2 %collective-permute-start.3 = (bf16[2,2,256,256]{3,2,1,0:T(8,128)(2,1)}, bf16[2,2,256,256]{3,2,1,0:T(8,128)(2,1)}, u32[]{:S(2)}, u32[]{:S(2)}) collective-permute-start(bf16[2,2,256,256]{3,2,1,0:T(8,128)(2,1)} %slice.44), channel_id=1, source_target_pairs={{0,6},{1,7},{2,0},{3,1},{4,2},{5,3},{6,4},{7,5},{8,14},{9,15},{10,... | collective-permute-start | bytes 1572872 | tf_op jit(solution)/shard_map/ppermute | solution.py:62
  103.7 20.4 %copy-start = (f32[4,1,2,1,256,256]{5,4,3,2,1,0:T(8,128)S(1)}, f32[4,1,2,1,256,256]{5,4,3,2,1,0:T(8,128)}, u32[]{:S(2)}) copy-start(f32[4,1,2,1,256,256]{5,4,3,2,1,0:T(8,128)} %param.7) | copy-start | bytes 6291460
  110.1 9.9 %collective-permute-start.6 = (bf16[4,2,256,256]{3,2,1,0:T(8,128)(2,1)S(1)}, bf16[4,2,256,256]{3,2,1,0:T(8,128)(2,1)S(1)}, u32[]{:S(2)}, u32[]{:S(2)}) collective-permute-start(bf16[4,2,256,256]{3,2,1,0:T(8,128)(2,1)S(1)} %constant_dynamic-update-slice_fusion), channel_id=1, source_target_pairs={{0,1},{1,0},{2,3},{3,2},{4,5},{5,4},{6,7},{7,6},{8,9},{9,8},{10,11... | collective-permute-start | bytes 3145736 | tf_op jit(solution)/shard_map/ppermute | solution.py:65
  137.9 1.4 copy-start.1
  139.3 26.2 %collective-permute-start.7 = (bf16[4,2,256,256]{3,2,1,0:T(8,128)(2,1)}, bf16[4,2,256,256]{3,2,1,0:T(8,128)(2,1)S(1)}, u32[]{:S(2)}, u32[]{:S(2)}) collective-permute-start(bf16[4,2,256,256]{3,2,1,0:T(8,128)(2,1)} %bitcast.40), channel_id=1, source_target_pairs={{0,2},{1,3},{2,4},{3,5},{4,6},{5,7},{6,0},{7,1},{8,10},{9,11},{10,... | collective-permute-start | bytes 3145736 | tf_op jit(solution)/shard_map/ppermute | solution.py:58
  140.9 24.7 %collective-permute-start.8 = (bf16[4,2,256,256]{3,2,1,0:T(8,128)(2,1)}, bf16[4,2,256,256]{3,2,1,0:T(8,128)(2,1)S(1)}, u32[]{:S(2)}, u32[]{:S(2)}) collective-permute-start(bf16[4,2,256,256]{3,2,1,0:T(8,128)(2,1)} %bitcast.40), channel_id=1, source_target_pairs={{0,6},{1,7},{2,0},{3,1},{4,2},{5,3},{6,4},{7,5},{8,14},{9,15},{10,... | collective-permute-start | bytes 3145736 | tf_op jit(solution)/shard_map/ppermute | solution.py:59
  165.6 5.5 %copy-start.4 = (bf16[4,2,256,256]{3,2,1,0:T(8,128)(2,1)}, bf16[4,2,256,256]{3,2,1,0:T(8,128)(2,1)S(1)}, u32[]{:S(2)}) copy-start(bf16[4,2,256,256]{3,2,1,0:T(8,128)(2,1)S(1)} %collective-permute-done.7) | copy-start | bytes 3145732
  165.6 10.6 %copy-start.5 = (bf16[4,2,256,256]{3,2,1,0:T(8,128)(2,1)}, bf16[4,2,256,256]{3,2,1,0:T(8,128)(2,1)S(1)}, u32[]{:S(2)}) copy-start(bf16[4,2,256,256]{3,2,1,0:T(8,128)(2,1)S(1)} %collective-permute-done.8) | copy-start | bytes 3145732
  167.3 28.1 %collective-permute-start.12 = (bf16[2,4,2,256,256]{4,3,2,1,0:T(8,128)(2,1)}, bf16[2,4,2,256,256]{4,3,2,1,0:T(8,128)(2,1)}, u32[]{:S(2)}, u32[]{:S(2)}) collective-permute-start(bf16[2,4,2,256,256]{4,3,2,1,0:T(8,128)(2,1)} %pad_maximum_fusion.1), channel_id=1, source_target_pairs={{0,1},{1,0},{2,3},{3,2},{4,5},{5,4},{6,7},{7,6},{8,9},{9,8},{10,11... | collective-permute-start | bytes 6291464 | tf_op jit(solution)/shard_map/ppermute | solution.py:64
  168.9 15.9 %collective-permute-start.9 = (bf16[2,2,256,256]{3,2,1,0:T(8,128)(2,1)}, bf16[2,2,256,256]{3,2,1,0:T(8,128)(2,1)}, u32[]{:S(2)}, u32[]{:S(2)}) collective-permute-start(bf16[2,2,256,256]{3,2,1,0:T(8,128)(2,1)} %slice.45), channel_id=1, source_target_pairs={{0,2},{1,3},{2,4},{3,5},{4,6},{5,7},{6,0},{7,1},{8,10},{9,11},{10,... | collective-permute-start | bytes 1572872 | tf_op jit(solution)/shard_map/ppermute | solution.py:61
  174.2 14.3 %collective-permute-start.10 = (bf16[2,2,256,256]{3,2,1,0:T(8,128)(2,1)}, bf16[2,2,256,256]{3,2,1,0:T(8,128)(2,1)S(1)}, u32[]{:S(2)}, u32[]{:S(2)}) collective-permute-start(bf16[2,2,256,256]{3,2,1,0:T(8,128)(2,1)} %slice.46), channel_id=1, source_target_pairs={{0,6},{1,7},{2,0},{3,1},{4,2},{5,3},{6,4},{7,5},{8,14},{9,15},{10,... | collective-permute-start | bytes 1572872 | tf_op jit(solution)/shard_map/ppermute | solution.py:62
  176.2 18.1 %collective-permute-start.11 = (bf16[4,2,256,256]{3,2,1,0:T(8,128)(2,1)}, bf16[4,2,256,256]{3,2,1,0:T(8,128)(2,1)S(1)}, u32[]{:S(2)}, u32[]{:S(2)}) collective-permute-start(bf16[4,2,256,256]{3,2,1,0:T(8,128)(2,1)} %bitcast.40), channel_id=1, source_target_pairs={{0,1},{1,0},{2,3},{3,2},{4,5},{5,4},{6,7},{7,6},{8,9},{9,8},{10,11... | collective-permute-start | bytes 3145736 | tf_op jit(solution)/shard_map/ppermute | solution.py:60
  178.5 71.7 %copy-start.2 = (f32[8,256,256]{2,1,0:T(8,128)S(1)}, f32[8,256,256]{2,1,0:T(8,128)}, u32[]{:S(2)}) copy-start(f32[8,256,256]{2,1,0:T(8,128)} %copy-done.1) | copy-start | bytes 6291460
  188.5 10.1 %collective-permute-start.13 = (bf16[4,2,256,256]{3,2,1,0:T(8,128)(2,1)S(1)}, bf16[4,2,256,256]{3,2,1,0:T(8,128)(2,1)S(1)}, u32[]{:S(2)}, u32[]{:S(2)}) collective-permute-start(bf16[4,2,256,256]{3,2,1,0:T(8,128)(2,1)S(1)} %constant_dynamic-update-slice_fusion.5), channel_id=1, source_target_pairs={{0,1},{1,0},{2,3},{3,2},{4,5},{5,4},{6,7},{7,6},{8,9},{9,8},{10,11... | collective-permute-start | bytes 3145736 | tf_op jit(solution)/shard_map/ppermute | solution.py:65
Sparse Core Ops, SparseCore 0:
  9.8 114.2 all-gather.5
  139.4 110.6 all-gather.3

commit v10 on v8

--- a/solution.py
+++ b/solution.py
@@ -14,13 +14,12 @@
     take_product = misc_ref[0] > 0
 
     def body(o, carry):
-        sums = [None, None]
+        acc = None
         for k in range(terms):
             t = o * terms + k
             d = jnp.dot(rows_ref[a_ref[t]], cols_ref[b_ref[t]], preferred_element_type=jnp.float32)
             d = jnp.where(v_ref[t] > 0, d, 0.0)
-            sums[k % 2] = d if sums[k % 2] is None else sums[k % 2] + d
-        acc = sums[0] + sums[1]
+            acc = d if acc is None else acc + d
         p = prev_ref[o]
         prev = jnp.where(p >= 0, owned_ref[jnp.maximum(p, 0)], 0.0)
         res = jnp.where(take_product, acc, 2.0 * prev - acc)
@@ -29,7 +28,7 @@
             outb_ref[o] = res.astype(outb_ref.dtype)
         return carry
 
-    lax.fori_loop(0, nout, body, 0)
+    lax.fori_loop(0, nout, body, 0, unroll=True)
 
 
 def run_product(a_t, b_t, v_t, prev_t, misc, rows, cols, owned, with_rounded):

time: 275 us -> 272 us (0.989)
  transfers between devices with their start and end apart: 16 -> 16, of which waited for: 7 -> 8; matrix products, arithmetic and copies ran while one was open for 20% -> 20% of each run, Pallas kernels for 0% -> 0%
where the time goes in v10:
time: 272 us; the launch traced here: 271 us
  waiting for transfers between devices  96.7 us (36%)
  blocking collectives  57.9 us (21%)
  local copies, waits for them, and re-layouts  42.5 us (16%)
  Pallas kernels  27.9 us (10%)
  between operations  16.3 us (6%)
  other arithmetic  15.5 us (6%)
  starting transfers between devices  14.3 us (5%)
    all_gather x2, waiting for transfers between devices, purify_section(): cols = lax.all_gather(panels, 'row', axis=0, tiled=False)  53.5 us
    psum x1, blocking collectives, shards(): lax.psum(lax.psum(jnp.stack([diag_term, square_term]), 'col'), 'row')  42.4 us
    ppermute x2, waiting for transfers between devices, col_gather(): from_minus = lax.ppermute(x, 'col', plus2)  30.1 us
    unnamed x30, local copies, waits for them, and re-layouts  28.2 us
    pallas_call x2, Pallas kernels, run_product(): pl.pallas_call(product_kernel, in_specs=[smem] * 5 + [vmem] * 3, out_spec...  27.9 us
    psum x1, blocking collectives, shards(): lax.psum(jnp.stack([diag_term, square_term]), 'col')  15.5 us
    ppermute x2, waiting for transfers between devices, col_gather(): far_b = lax.ppermute(from_plus[half:], 'col', minus2)  6.68 us
    ppermute x2, waiting for transfers between devices, col_gather(): far_a = lax.ppermute(from_minus[:half], 'col', plus2)  6.28 us
  transfers between devices with their start and end apart: 16, of which 8 were waited for; matrix products, arithmetic and copies ran while one was open for 20% of the time, Pallas kernels for 0%

profile of v10, /device:TPU:0, one launch (start us, length us, event | category | flops | bytes accessed | tf_op | source)
XLA Modules:
  0.0 271.1 jit_solution(2662461052252767649)
XLA Ops:
  6.5 3.2 %bitcast_dynamic-update-slice_fusion.6 = (bf16[8,4,2,256,256]{4,3,2,1,0:T(8,128)(2,1)}, bf16[4,1,2,1,256,256]{5,4,3,2,1,0:T(8,128)(2,1)}) fusion(f32[4,1,2,1,256,256]{5,4,3,2,1,0:T(8,128)} %param.7), kind=kLoop, calls=%fused_computation.18 | loop fusion | flops 524287 | bytes 4194304
  9.8 2.1 collective-permute-start
  11.9 2.2 collective-permute-start.1
  14.1 0.8 copy.69
  15.5 0.8 copy.80
  17.2 0.8 copy.73
  19.8 1.9 fusion
  22.4 2.5 multiply_reduce_fusion
  25.4 1.3 pad_maximum_fusion.2
  30.1 7.2 %collective-permute-done = bf16[4,2,256,256]{3,2,1,0:T(8,128)(2,1)S(1)} collective-permute-done((bf16[4,2,256,256]{3,2,1,0:T(8,128)(2,1)}, bf16[4,2,256,256]{3,2,1,0:T(8,128)(2,1)S(1)}, u32[]{:S(2)}, u32[]{:S(2)}) %collective-permute-start) | collective-permute-done | bytes 1048608 | tf_op jit(solution)/shard_map/ppermute | solution.py:57
  37.4 1.6 pad_maximum_fusion
  39.0 15.5 %psum.14 = f32[2]{0:T(128)S(1)} all-reduce(f32[2]{0:T(128)S(1)} %pad_maximum_fusion.2), channel_id=1, replica_groups=mesh['row'=16,'col'=8] {'col'}, use_global_device_ids=true, to_apply=%region_8.9 | all-reduce | flops 2 | bytes 16 | tf_op jit(solution)/shard_map/psum | solution.py:151
  54.5 0.8 slice.43
  55.3 42.4 %psum.15 = f32[2]{0:T(128)S(1)} all-reduce(f32[2]{0:T(128)S(1)} %psum.14), channel_id=1, replica_groups=mesh['row'=16,'col'=8] {'row'}, use_global_device_ids=true, to_apply=%region_9.10 | all-reduce | flops 2 | bytes 16 | tf_op jit(solution)/shard_map/psum | solution.py:151
  98.0 0.9 slice.44
  98.9 3.2 %collective-permute-start.3 = (bf16[2,2,256,256]{3,2,1,0:T(8,128)(2,1)}, bf16[2,2,256,256]{3,2,1,0:T(8,128)(2,1)}, u32[]{:S(2)}, u32[]{:S(2)}) collective-permute-start(bf16[2,2,256,256]{3,2,1,0:T(8,128)(2,1)} %slice.44), channel_id=1, source_target_pairs={{0,6},{1,7},{2,0},{3,1},{4,2},{5,3},{6,4},{7,5},{8,14},{9,15},{10,... | collective-permute-start | bytes 1572872 | tf_op jit(solution)/shard_map/ppermute | solution.py:61
  103.7 1.2 constant_dynamic-update-slice_fusion.1
  105.0 4.1 %collective-permute-done.3 = bf16[2,2,256,256]{3,2,1,0:T(8,128)(2,1)} collective-permute-done((bf16[2,2,256,256]{3,2,1,0:T(8,128)(2,1)}, bf16[2,2,256,256]{3,2,1,0:T(8,128)(2,1)}, u32[]{:S(2)}, u32[]{:S(2)}) %collective-permute-start.3) | collective-permute-done | bytes 524320 | tf_op jit(solution)/shard_map/ppermute | solution.py:61
  109.1 1.1 constant_dynamic-update-slice_fusion
  110.2 1.1 constant_dynamic-update-slice_fusion.4
  111.3 2.3 constant_dynamic-update-slice_fusion.3
  113.6 1.1 bitcast_dynamic-update-slice_fusion.5
  114.7 2.3 bitcast_dynamic-update-slice_fusion.4
  117.0 3.1 %constant_dynamic-update-slice_fusion.2 = bf16[8,4,2,256,256]{4,3,2,1,0:T(8,128)(2,1)} fusion(bf16[8,4,2,256,256]{4,3,2,1,0:T(8,128)(2,1)} %bitcast_dynamic-update-slice_fusion.4, bf16[2,4,2,256,256]{4,3,2,1,0:T(8,128)(2,1)} %collective-permute-done.5), kind=kLoop, calls=%fused_computation.22 | loop fusion | bytes 4194304
  120.1 1.0 bitcast_dynamic-update-slice_fusion.3
  121.1 3.0 %all-gather.6.cloned.1.call-done = bf16[64,1,2,1,256,256]{5,4,3,2,1,0:T(8,128)(2,1)} async-done(((bf16[4,1,2,1,256,256]{5,4,3,2,1,0:T(8,128)(2,1)}), bf16[64,1,2,1,256,256]{5,4,3,2,1,0:T(8,128)(2,1)}) %all-gather.6.cloned.1.call-update) | async-done | bytes 16777232 | tf_op jit(solution)/shard_map/all_gather | solution.py:86
  124.1 13.8 %shard_map.46 = (f32[8,256,256]{2,1,0:T(8,128)S(1)}, bf16[8,256,256]{2,1,0:T(8,128)(2,1)}) custom-call(s32[128]{0:T(128)S(1)} %reshape.618.a_ref, s32[128]{0:T(128)S(1)} %reshape.628.b_ref, s32[128]{0:T(128)S(1)} %reshape.640.v_ref, s32[8]{0:T(128)S(1)} %reshape.629.prev_ref, s32[1]{0:T(128)S(6)} %reshape.630.misc_ref, bf16[64,256,256]{2,1,0:T(8,128)(2,1)} %bitcast.87, ...), custom_call_target="tpu_custom_call" | custom-call | flops 4294967296 | bytes 29360128 | tf_op jit(solution)/shard_map/pallas_call | solution.py:41
  137.9 1.4 copy-done.1
  139.3 1.6 collective-permute-start.7
  140.9 1.7 collective-permute-start.8
  142.7 22.8 %collective-permute-done.7 = bf16[4,2,256,256]{3,2,1,0:T(8,128)(2,1)S(1)} collective-permute-done((bf16[4,2,256,256]{3,2,1,0:T(8,128)(2,1)}, bf16[4,2,256,256]{3,2,1,0:T(8,128)(2,1)S(1)}, u32[]{:S(2)}, u32[]{:S(2)}) %collective-permute-start.7) | collective-permute-done | bytes 1048608 | tf_op jit(solution)/shard_map/ppermute | solution.py:57
  165.6 1.7 pad_maximum_fusion.1
  168.1 0.8 slice.45
  168.9 1.5 collective-permute-start.9
  173.3 0.8 slice.46
  174.2 1.7 collective-permute-start.10
  176.2 2.3 constant_dynamic-update-slice_fusion.10
  178.5 6.3 %collective-permute-done.9 = bf16[2,2,256,256]{3,2,1,0:T(8,128)(2,1)} collective-permute-done((bf16[2,2,256,256]{3,2,1,0:T(8,128)(2,1)}, bf16[2,2,256,256]{3,2,1,0:T(8,128)(2,1)}, u32[]{:S(2)}, u32[]{:S(2)}) %collective-permute-start.9) | collective-permute-done | bytes 524320 | tf_op jit(solution)/shard_map/ppermute | solution.py:60
  184.8 1.1 constant_dynamic-update-slice_fusion.6
  185.8 2.6 collective-permute-done.10
  188.5 2.4 constant_dynamic-update-slice_fusion.9
  190.9 2.3 constant_dynamic-update-slice_fusion.8
  193.2 1.1 bitcast_dynamic-update-slice_fusion.2
  194.3 1.0 bitcast_dynamic-update-slice_fusion.1
  195.3 3.2 %constant_dynamic-update-slice_fusion.7 = bf16[8,4,2,256,256]{4,3,2,1,0:T(8,128)(2,1)} fusion(bf16[8,4,2,256,256]{4,3,2,1,0:T(8,128)(2,1)} %bitcast_dynamic-update-slice_fusion.1, bf16[2,4,2,256,256]{4,3,2,1,0:T(8,128)(2,1)} %collective-permute-done.12), kind=kLoop, calls=%fused_computation.27 | loop fusion | bytes 4194304
  198.6 1.0 bitcast_dynamic-update-slice_fusion
  199.6 50.6 %all-gather.4.cloned.1.call-done = bf16[16,4,2,256,256]{4,3,2,1,0:T(8,128)(2,1)} async-done(((bf16[1,4,2,256,256]{4,3,2,1,0:T(8,128)(2,1)}), bf16[16,4,2,256,256]{4,3,2,1,0:T(8,128)(2,1)}) %all-gather.4.cloned.1.call-update) | async-done | bytes 16777232 | tf_op jit(solution)/shard_map/all_gather | solution.py:86
  250.2 14.1 %shard_map.47 = f32[8,256,256]{2,1,0:T(8,128)} custom-call(s32[128]{0:T(128)S(1)} %reshape.618.a_ref, s32[128]{0:T(128)S(1)} %reshape.621.b_ref, s32[128]{0:T(128)S(1)} %reshape.637.v_ref, s32[8]{0:T(128)S(1)} %reshape.623.prev_ref, s32[1]{0:T(128)} %bitcast.24.misc_ref, bf16[64,256,256]{2,1,0:T(8,128)(2,1)} %bitcast.46.rows_ref, ...), custom_call_target="tpu_custom_call" | custom-call | flops 4294967296 | bytes 29360128 | tf_op jit(solution)/shard_map/pallas_call | solution.py:41
  (101 shorter events, 11.6 us)
Async XLA Ops:
  6.5 117.6 %all-gather.6.cloned.1.call-start = ((), (), s32[]{:S(2)}) async-start(), calls=%async_computation.1 | async-start | bytes 17825792 | tf_op jit(solution)/shard_map/all_gather | solution.py:86
  9.7 240.4 %all-gather.4.cloned.1.call-start = ((), (), s32[]{:S(2)}) async-start(), calls=%async_computation | async-start | bytes 17825792 | tf_op jit(solution)/shard_map/all_gather | solution.py:86
  9.8 27.6 %collective-permute-start = (bf16[4,2,256,256]{3,2,1,0:T(8,128)(2,1)}, bf16[4,2,256,256]{3,2,1,0:T(8,128)(2,1)S(1)}, u32[]{:S(2)}, u32[]{:S(2)}) collective-permute-start(bf16[4,2,256,256]{3,2,1,0:T(8,128)(2,1)} %bitcast.88), channel_id=1, source_target_pairs={{0,2},{1,3},{2,4},{3,5},{4,6},{5,7},{6,0},{7,1},{8,10},{9,11},{10,... | collective-permute-start | bytes 3145736 | tf_op jit(solution)/shard_map/ppermute | solution.py:57
  11.9 25.5 %collective-permute-start.1 = (bf16[4,2,256,256]{3,2,1,0:T(8,128)(2,1)}, bf16[4,2,256,256]{3,2,1,0:T(8,128)(2,1)S(1)}, u32[]{:S(2)}, u32[]{:S(2)}) collective-permute-start(bf16[4,2,256,256]{3,2,1,0:T(8,128)(2,1)} %bitcast.89), channel_id=1, source_target_pairs={{0,6},{1,7},{2,0},{3,1},{4,2},{5,3},{6,4},{7,5},{8,14},{9,15},{10,... | collective-permute-start | bytes 3145736 | tf_op jit(solution)/shard_map/ppermute | solution.py:58
  14.1 100.6 %collective-permute-start.4 = (bf16[4,2,256,256]{3,2,1,0:T(8,128)(2,1)}, bf16[4,2,256,256]{3,2,1,0:T(8,128)(2,1)}, u32[]{:S(2)}, u32[]{:S(2)}) collective-permute-start(bf16[4,2,256,256]{3,2,1,0:T(8,128)(2,1)} %bitcast.90), channel_id=1, source_target_pairs={{0,1},{1,0},{2,3},{3,2},{4,5},{5,4},{6,7},{7,6},{8,9},{9,8},{10,11... | collective-permute-start | bytes 3145736 | tf_op jit(solution)/shard_map/ppermute | solution.py:59
  37.4 64.7 %copy-start.3 = (bf16[4,2,256,256]{3,2,1,0:T(8,128)(2,1)}, bf16[4,2,256,256]{3,2,1,0:T(8,128)(2,1)S(1)}, u32[]{:S(2)}) copy-start(bf16[4,2,256,256]{3,2,1,0:T(8,128)(2,1)S(1)} %collective-permute-done.1) | copy-start | bytes 3145732
  39.0 78.0 %collective-permute-start.5 = (bf16[2,4,2,256,256]{4,3,2,1,0:T(8,128)(2,1)}, bf16[2,4,2,256,256]{4,3,2,1,0:T(8,128)(2,1)}, u32[]{:S(2)}, u32[]{:S(2)}) collective-permute-start(bf16[2,4,2,256,256]{4,3,2,1,0:T(8,128)(2,1)} %pad_maximum_fusion), channel_id=1, source_target_pairs={{0,1},{1,0},{2,3},{3,2},{4,5},{5,4},{6,7},{7,6},{8,9},{9,8},{10,11... | collective-permute-start | bytes 6291464 | tf_op jit(solution)/shard_map/ppermute | solution.py:63
  55.3 48.4 %collective-permute-start.2 = (bf16[2,2,256,256]{3,2,1,0:T(8,128)(2,1)}, bf16[2,2,256,256]{3,2,1,0:T(8,128)(2,1)}, u32[]{:S(2)}, u32[]{:S(2)}) collective-permute-start(bf16[2,2,256,256]{3,2,1,0:T(8,128)(2,1)} %slice.43), channel_id=1, source_target_pairs={{0,2},{1,3},{2,4},{3,5},{4,6},{5,7},{6,0},{7,1},{8,10},{9,11},{10,... | collective-permute-start | bytes 1572872 | tf_op jit(solution)/shard_map/ppermute | solution.py:60
  98.9 10.2 %collective-permute-start.3 = (bf16[2,2,256,256]{3,2,1,0:T(8,128)(2,1)}, bf16[2,2,256,256]{3,2,1,0:T(8,128)(2,1)}, u32[]{:S(2)}, u32[]{:S(2)}) collective-permute-start(bf16[2,2,256,256]{3,2,1,0:T(8,128)(2,1)} %slice.44), channel_id=1, source_target_pairs={{0,6},{1,7},{2,0},{3,1},{4,2},{5,3},{6,4},{7,5},{8,14},{9,15},{10,... | collective-permute-start | bytes 1572872 | tf_op jit(solution)/shard_map/ppermute | solution.py:61
  103.7 20.4 %copy-start = (f32[4,1,2,1,256,256]{5,4,3,2,1,0:T(8,128)S(1)}, f32[4,1,2,1,256,256]{5,4,3,2,1,0:T(8,128)}, u32[]{:S(2)}) copy-start(f32[4,1,2,1,256,256]{5,4,3,2,1,0:T(8,128)} %param.7) | copy-start | bytes 6291460
  110.1 9.9 %collective-permute-start.6 = (bf16[4,2,256,256]{3,2,1,0:T(8,128)(2,1)S(1)}, bf16[4,2,256,256]{3,2,1,0:T(8,128)(2,1)S(1)}, u32[]{:S(2)}, u32[]{:S(2)}) collective-permute-start(bf16[4,2,256,256]{3,2,1,0:T(8,128)(2,1)S(1)} %constant_dynamic-update-slice_fusion), channel_id=1, source_target_pairs={{0,1},{1,0},{2,3},{3,2},{4,5},{5,4},{6,7},{7,6},{8,9},{9,8},{10,11... | collective-permute-start | bytes 3145736 | tf_op jit(solution)/shard_map/ppermute | solution.py:64
  137.9 1.4 copy-start.1
  139.3 26.2 %collective-permute-start.7 = (bf16[4,2,256,256]{3,2,1,0:T(8,128)(2,1)}, bf16[4,2,256,256]{3,2,1,0:T(8,128)(2,1)S(1)}, u32[]{:S(2)}, u32[]{:S(2)}) collective-permute-start(bf16[4,2,256,256]{3,2,1,0:T(8,128)(2,1)} %bitcast.40), channel_id=1, source_target_pairs={{0,2},{1,3},{2,4},{3,5},{4,6},{5,7},{6,0},{7,1},{8,10},{9,11},{10,... | collective-permute-start | bytes 3145736 | tf_op jit(solution)/shard_map/ppermute | solution.py:57
  140.9 24.7 %collective-permute-start.8 = (bf16[4,2,256,256]{3,2,1,0:T(8,128)(2,1)}, bf16[4,2,256,256]{3,2,1,0:T(8,128)(2,1)S(1)}, u32[]{:S(2)}, u32[]{:S(2)}) collective-permute-start(bf16[4,2,256,256]{3,2,1,0:T(8,128)(2,1)} %bitcast.40), channel_id=1, source_target_pairs={{0,6},{1,7},{2,0},{3,1},{4,2},{5,3},{6,4},{7,5},{8,14},{9,15},{10,... | collective-permute-start | bytes 3145736 | tf_op jit(solution)/shard_map/ppermute | solution.py:58
  165.6 5.5 %copy-start.4 = (bf16[4,2,256,256]{3,2,1,0:T(8,128)(2,1)}, bf16[4,2,256,256]{3,2,1,0:T(8,128)(2,1)S(1)}, u32[]{:S(2)}) copy-start(bf16[4,2,256,256]{3,2,1,0:T(8,128)(2,1)S(1)} %collective-permute-done.7) | copy-start | bytes 3145732
  165.6 10.6 %copy-start.5 = (bf16[4,2,256,256]{3,2,1,0:T(8,128)(2,1)}, bf16[4,2,256,256]{3,2,1,0:T(8,128)(2,1)S(1)}, u32[]{:S(2)}) copy-start(bf16[4,2,256,256]{3,2,1,0:T(8,128)(2,1)S(1)} %collective-permute-done.8) | copy-start | bytes 3145732
  167.3 28.1 %collective-permute-start.12 = (bf16[2,4,2,256,256]{4,3,2,1,0:T(8,128)(2,1)}, bf16[2,4,2,256,256]{4,3,2,1,0:T(8,128)(2,1)}, u32[]{:S(2)}, u32[]{:S(2)}) collective-permute-start(bf16[2,4,2,256,256]{4,3,2,1,0:T(8,128)(2,1)} %pad_maximum_fusion.1), channel_id=1, source_target_pairs={{0,1},{1,0},{2,3},{3,2},{4,5},{5,4},{6,7},{7,6},{8,9},{9,8},{10,11... | collective-permute-start | bytes 6291464 | tf_op jit(solution)/shard_map/ppermute | solution.py:63
  168.9 15.9 %collective-permute-start.9 = (bf16[2,2,256,256]{3,2,1,0:T(8,128)(2,1)}, bf16[2,2,256,256]{3,2,1,0:T(8,128)(2,1)}, u32[]{:S(2)}, u32[]{:S(2)}) collective-permute-start(bf16[2,2,256,256]{3,2,1,0:T(8,128)(2,1)} %slice.45), channel_id=1, source_target_pairs={{0,2},{1,3},{2,4},{3,5},{4,6},{5,7},{6,0},{7,1},{8,10},{9,11},{10,... | collective-permute-start | bytes 1572872 | tf_op jit(solution)/shard_map/ppermute | solution.py:60
  174.2 14.3 %collective-permute-start.10 = (bf16[2,2,256,256]{3,2,1,0:T(8,128)(2,1)}, bf16[2,2,256,256]{3,2,1,0:T(8,128)(2,1)S(1)}, u32[]{:S(2)}, u32[]{:S(2)}) collective-permute-start(bf16[2,2,256,256]{3,2,1,0:T(8,128)(2,1)} %slice.46), channel_id=1, source_target_pairs={{0,6},{1,7},{2,0},{3,1},{4,2},{5,3},{6,4},{7,5},{8,14},{9,15},{10,... | collective-permute-start | bytes 1572872 | tf_op jit(solution)/shard_map/ppermute | solution.py:61
  176.2 18.1 %collective-permute-start.11 = (bf16[4,2,256,256]{3,2,1,0:T(8,128)(2,1)}, bf16[4,2,256,256]{3,2,1,0:T(8,128)(2,1)S(1)}, u32[]{:S(2)}, u32[]{:S(2)}) collective-permute-start(bf16[4,2,256,256]{3,2,1,0:T(8,128)(2,1)} %bitcast.40), channel_id=1, source_target_pairs={{0,1},{1,0},{2,3},{3,2},{4,5},{5,4},{6,7},{7,6},{8,9},{9,8},{10,11... | collective-permute-start | bytes 3145736 | tf_op jit(solution)/shard_map/ppermute | solution.py:59
  178.5 71.7 %copy-start.2 = (f32[8,256,256]{2,1,0:T(8,128)S(1)}, f32[8,256,256]{2,1,0:T(8,128)}, u32[]{:S(2)}) copy-start(f32[8,256,256]{2,1,0:T(8,128)} %copy-done.1) | copy-start | bytes 6291460
  188.5 10.1 %collective-permute-start.13 = (bf16[4,2,256,256]{3,2,1,0:T(8,128)(2,1)S(1)}, bf16[4,2,256,256]{3,2,1,0:T(8,128)(2,1)S(1)}, u32[]{:S(2)}, u32[]{:S(2)}) collective-permute-start(bf16[4,2,256,256]{3,2,1,0:T(8,128)(2,1)S(1)} %constant_dynamic-update-slice_fusion.5), channel_id=1, source_target_pairs={{0,1},{1,0},{2,3},{3,2},{4,5},{5,4},{6,7},{7,6},{8,9},{9,8},{10,11... | collective-permute-start | bytes 3145736 | tf_op jit(solution)/shard_map/ppermute | solution.py:64
Sparse Core Ops, SparseCore 0:
  9.8 114.2 all-gather.5
  139.4 110.6 all-gather.3

commit v11 on v10

--- a/solution.py
+++ b/solution.py
@@ -17,8 +17,8 @@
         acc = None
         for k in range(terms):
             t = o * terms + k
-            d = jnp.dot(rows_ref[a_ref[t]], cols_ref[b_ref[t]], preferred_element_type=jnp.float32)
-            d = jnp.where(v_ref[t] > 0, d, 0.0)
+            lhs = jnp.where(v_ref[t] > 0, rows_ref[a_ref[t]], jnp.zeros((), rows_ref.dtype))
+            d = jnp.dot(lhs, cols_ref[b_ref[t]], preferred_element_type=jnp.float32)
             acc = d if acc is None else acc + d
         p = prev_ref[o]
         prev = jnp.where(p >= 0, owned_ref[jnp.maximum(p, 0)], 0.0)

time: 272 us -> 272 us (level)
  no operation moved by 1% of the time
where the time goes in v11:
time: 272 us; the launch traced here: 271 us
  waiting for transfers between devices  96.5 us (35%)
  blocking collectives  57.9 us (21%)
  local copies, waits for them, and re-layouts  42.5 us (16%)
  Pallas kernels  27.8 us (10%)
  between operations  16.3 us (6%)
  other arithmetic  15.5 us (6%)
  starting transfers between devices  14.4 us (5%)
    all_gather x2, waiting for transfers between devices, purify_section(): cols = lax.all_gather(panels, 'row', axis=0, tiled=False)  53.5 us
    psum x1, blocking collectives, shards(): lax.psum(lax.psum(jnp.stack([diag_term, square_term]), 'col'), 'row')  42.4 us
    ppermute x2, waiting for transfers between devices, col_gather(): from_minus = lax.ppermute(x, 'col', plus2)  30.1 us
    unnamed x30, local copies, waits for them, and re-layouts  28.2 us
    pallas_call x2, Pallas kernels, run_product(): pl.pallas_call(product_kernel, in_specs=[smem] * 5 + [vmem] * 3, out_spec...  27.8 us
    psum x1, blocking collectives, shards(): lax.psum(jnp.stack([diag_term, square_term]), 'col')  15.5 us
    ppermute x2, waiting for transfers between devices, col_gather(): far_b = lax.ppermute(from_plus[half:], 'col', minus2)  6.68 us
    ppermute x2, waiting for transfers between devices, col_gather(): far_a = lax.ppermute(from_minus[:half], 'col', plus2)  6.1 us
  transfers between devices with their start and end apart: 16, of which 8 were waited for; matrix products, arithmetic and copies ran while one was open for 20% of the time, Pallas kernels for 0%

profile of v11, /device:TPU:0, one launch (start us, length us, event | category | flops | bytes accessed | tf_op | source)
XLA Modules:
  0.0 271.1 jit_solution(4996035596816733158)
XLA Ops:
  6.5 3.2 %bitcast_dynamic-update-slice_fusion.6 = (bf16[8,4,2,256,256]{4,3,2,1,0:T(8,128)(2,1)}, bf16[4,1,2,1,256,256]{5,4,3,2,1,0:T(8,128)(2,1)}) fusion(f32[4,1,2,1,256,256]{5,4,3,2,1,0:T(8,128)} %param.7), kind=kLoop, calls=%fused_computation.18 | loop fusion | flops 524287 | bytes 4194304
  9.8 2.1 collective-permute-start
  11.9 2.2 collective-permute-start.1
  14.1 0.8 copy.69
  15.5 0.8 copy.80
  17.2 0.8 copy.73
  19.8 1.9 fusion
  22.4 2.5 multiply_reduce_fusion
  25.4 1.3 pad_maximum_fusion.2
  30.1 7.2 %collective-permute-done = bf16[4,2,256,256]{3,2,1,0:T(8,128)(2,1)S(1)} collective-permute-done((bf16[4,2,256,256]{3,2,1,0:T(8,128)(2,1)}, bf16[4,2,256,256]{3,2,1,0:T(8,128)(2,1)S(1)}, u32[]{:S(2)}, u32[]{:S(2)}) %collective-permute-start) | collective-permute-done | bytes 1048608 | tf_op jit(solution)/shard_map/ppermute | solution.py:57
  37.4 1.6 pad_maximum_fusion
  39.0 15.5 %psum.14 = f32[2]{0:T(128)S(1)} all-reduce(f32[2]{0:T(128)S(1)} %pad_maximum_fusion.2), channel_id=1, replica_groups=mesh['row'=16,'col'=8] {'col'}, use_global_device_ids=true, to_apply=%region_8.9 | all-reduce | flops 2 | bytes 16 | tf_op jit(solution)/shard_map/psum | solution.py:151
  54.5 0.8 slice.43
  55.3 42.4 %psum.15 = f32[2]{0:T(128)S(1)} all-reduce(f32[2]{0:T(128)S(1)} %psum.14), channel_id=1, replica_groups=mesh['row'=16,'col'=8] {'row'}, use_global_device_ids=true, to_apply=%region_9.10 | all-reduce | flops 2 | bytes 16 | tf_op jit(solution)/shard_map/psum | solution.py:151
  98.0 0.9 slice.44
  98.9 3.2 %collective-permute-start.3 = (bf16[2,2,256,256]{3,2,1,0:T(8,128)(2,1)}, bf16[2,2,256,256]{3,2,1,0:T(8,128)(2,1)}, u32[]{:S(2)}, u32[]{:S(2)}) collective-permute-start(bf16[2,2,256,256]{3,2,1,0:T(8,128)(2,1)} %slice.44), channel_id=1, source_target_pairs={{0,6},{1,7},{2,0},{3,1},{4,2},{5,3},{6,4},{7,5},{8,14},{9,15},{10,... | collective-permute-start | bytes 1572872 | tf_op jit(solution)/shard_map/ppermute | solution.py:61
  103.7 1.2 constant_dynamic-update-slice_fusion.1
  105.0 4.1 %collective-permute-done.3 = bf16[2,2,256,256]{3,2,1,0:T(8,128)(2,1)} collective-permute-done((bf16[2,2,256,256]{3,2,1,0:T(8,128)(2,1)}, bf16[2,2,256,256]{3,2,1,0:T(8,128)(2,1)}, u32[]{:S(2)}, u32[]{:S(2)}) %collective-permute-start.3) | collective-permute-done | bytes 524320 | tf_op jit(solution)/shard_map/ppermute | solution.py:61
  109.1 1.1 constant_dynamic-update-slice_fusion
  110.2 1.1 constant_dynamic-update-slice_fusion.4
  111.3 2.3 constant_dynamic-update-slice_fusion.3
  113.6 1.1 bitcast_dynamic-update-slice_fusion.5
  114.7 2.3 bitcast_dynamic-update-slice_fusion.4
  117.0 3.1 %constant_dynamic-update-slice_fusion.2 = bf16[8,4,2,256,256]{4,3,2,1,0:T(8,128)(2,1)} fusion(bf16[8,4,2,256,256]{4,3,2,1,0:T(8,128)(2,1)} %bitcast_dynamic-update-slice_fusion.4, bf16[2,4,2,256,256]{4,3,2,1,0:T(8,128)(2,1)} %collective-permute-done.5), kind=kLoop, calls=%fused_computation.22 | loop fusion | bytes 4194304
  120.1 1.0 bitcast_dynamic-update-slice_fusion.3
  121.1 3.0 %all-gather.6.cloned.1.call-done = bf16[64,1,2,1,256,256]{5,4,3,2,1,0:T(8,128)(2,1)} async-done(((bf16[4,1,2,1,256,256]{5,4,3,2,1,0:T(8,128)(2,1)}), bf16[64,1,2,1,256,256]{5,4,3,2,1,0:T(8,128)(2,1)}) %all-gather.6.cloned.1.call-update) | async-done | bytes 16777232 | tf_op jit(solution)/shard_map/all_gather | solution.py:86
  124.1 13.8 %shard_map.46 = (f32[8,256,256]{2,1,0:T(8,128)S(1)}, bf16[8,256,256]{2,1,0:T(8,128)(2,1)}) custom-call(s32[128]{0:T(128)S(1)} %reshape.618.a_ref, s32[128]{0:T(128)S(1)} %reshape.628.b_ref, s32[128]{0:T(128)S(1)} %reshape.640.v_ref, s32[8]{0:T(128)S(1)} %reshape.629.prev_ref, s32[1]{0:T(128)S(6)} %reshape.630.misc_ref, bf16[64,256,256]{2,1,0:T(8,128)(2,1)} %bitcast.87, ...), custom_call_target="tpu_custom_call" | custom-call | flops 4294967296 | bytes 29360128 | tf_op jit(solution)/shard_map/pallas_call | solution.py:41
  137.9 1.4 copy-done.1
  139.3 1.6 collective-permute-start.7
  141.0 1.7 collective-permute-start.8
  142.7 22.8 %collective-permute-done.7 = bf16[4,2,256,256]{3,2,1,0:T(8,128)(2,1)S(1)} collective-permute-done((bf16[4,2,256,256]{3,2,1,0:T(8,128)(2,1)}, bf16[4,2,256,256]{3,2,1,0:T(8,128)(2,1)S(1)}, u32[]{:S(2)}, u32[]{:S(2)}) %collective-permute-start.7) | collective-permute-done | bytes 1048608 | tf_op jit(solution)/shard_map/ppermute | solution.py:57
  165.6 1.7 pad_maximum_fusion.1
  168.1 0.8 slice.45
  168.9 1.5 collective-permute-start.9
  173.3 0.8 slice.46
  174.2 1.7 collective-permute-start.10
  176.4 2.3 constant_dynamic-update-slice_fusion.10
  178.7 6.1 %collective-permute-done.9 = bf16[2,2,256,256]{3,2,1,0:T(8,128)(2,1)} collective-permute-done((bf16[2,2,256,256]{3,2,1,0:T(8,128)(2,1)}, bf16[2,2,256,256]{3,2,1,0:T(8,128)(2,1)}, u32[]{:S(2)}, u32[]{:S(2)}) %collective-permute-start.9) | collective-permute-done | bytes 524320 | tf_op jit(solution)/shard_map/ppermute | solution.py:60
  184.8 1.1 constant_dynamic-update-slice_fusion.6
  185.8 2.6 collective-permute-done.10
  188.6 2.4 constant_dynamic-update-slice_fusion.9
  190.9 2.3 constant_dynamic-update-slice_fusion.8
  193.2 1.1 bitcast_dynamic-update-slice_fusion.2
  194.3 1.0 bitcast_dynamic-update-slice_fusion.1
  195.3 3.2 %constant_dynamic-update-slice_fusion.7 = bf16[8,4,2,256,256]{4,3,2,1,0:T(8,128)(2,1)} fusion(bf16[8,4,2,256,256]{4,3,2,1,0:T(8,128)(2,1)} %bitcast_dynamic-update-slice_fusion.1, bf16[2,4,2,256,256]{4,3,2,1,0:T(8,128)(2,1)} %collective-permute-done.12), kind=kLoop, calls=%fused_computation.27 | loop fusion | bytes 4194304
  198.6 1.0 bitcast_dynamic-update-slice_fusion
  199.6 50.6 %all-gather.4.cloned.1.call-done = bf16[16,4,2,256,256]{4,3,2,1,0:T(8,128)(2,1)} async-done(((bf16[1,4,2,256,256]{4,3,2,1,0:T(8,128)(2,1)}), bf16[16,4,2,256,256]{4,3,2,1,0:T(8,128)(2,1)}) %all-gather.4.cloned.1.call-update) | async-done | bytes 16777232 | tf_op jit(solution)/shard_map/all_gather | solution.py:86
  250.2 14.1 %shard_map.47 = f32[8,256,256]{2,1,0:T(8,128)} custom-call(s32[128]{0:T(128)S(1)} %reshape.618.a_ref, s32[128]{0:T(128)S(1)} %reshape.621.b_ref, s32[128]{0:T(128)S(1)} %reshape.637.v_ref, s32[8]{0:T(128)S(1)} %reshape.623.prev_ref, s32[1]{0:T(128)} %bitcast.24.misc_ref, bf16[64,256,256]{2,1,0:T(8,128)(2,1)} %bitcast.46.rows_ref, ...), custom_call_target="tpu_custom_call" | custom-call | flops 4294967296 | bytes 29360128 | tf_op jit(solution)/shard_map/pallas_call | solution.py:41
  (101 shorter events, 11.8 us)
Async XLA Ops:
  6.5 117.6 %all-gather.6.cloned.1.call-start = ((), (), s32[]{:S(2)}) async-start(), calls=%async_computation.1 | async-start | bytes 17825792 | tf_op jit(solution)/shard_map/all_gather | solution.py:86
  9.7 240.5 %all-gather.4.cloned.1.call-start = ((), (), s32[]{:S(2)}) async-start(), calls=%async_computation | async-start | bytes 17825792 | tf_op jit(solution)/shard_map/all_gather | solution.py:86
  9.8 27.6 %collective-permute-start = (bf16[4,2,256,256]{3,2,1,0:T(8,128)(2,1)}, bf16[4,2,256,256]{3,2,1,0:T(8,128)(2,1)S(1)}, u32[]{:S(2)}, u32[]{:S(2)}) collective-permute-start(bf16[4,2,256,256]{3,2,1,0:T(8,128)(2,1)} %bitcast.88), channel_id=1, source_target_pairs={{0,2},{1,3},{2,4},{3,5},{4,6},{5,7},{6,0},{7,1},{8,10},{9,11},{10,... | collective-permute-start | bytes 3145736 | tf_op jit(solution)/shard_map/ppermute | solution.py:57
  11.9 25.5 %collective-permute-start.1 = (bf16[4,2,256,256]{3,2,1,0:T(8,128)(2,1)}, bf16[4,2,256,256]{3,2,1,0:T(8,128)(2,1)S(1)}, u32[]{:S(2)}, u32[]{:S(2)}) collective-permute-start(bf16[4,2,256,256]{3,2,1,0:T(8,128)(2,1)} %bitcast.89), channel_id=1, source_target_pairs={{0,6},{1,7},{2,0},{3,1},{4,2},{5,3},{6,4},{7,5},{8,14},{9,15},{10,... | collective-permute-start | bytes 3145736 | tf_op jit(solution)/shard_map/ppermute | solution.py:58
  14.1 100.6 %collective-permute-start.4 = (bf16[4,2,256,256]{3,2,1,0:T(8,128)(2,1)}, bf16[4,2,256,256]{3,2,1,0:T(8,128)(2,1)}, u32[]{:S(2)}, u32[]{:S(2)}) collective-permute-start(bf16[4,2,256,256]{3,2,1,0:T(8,128)(2,1)} %bitcast.90), channel_id=1, source_target_pairs={{0,1},{1,0},{2,3},{3,2},{4,5},{5,4},{6,7},{7,6},{8,9},{9,8},{10,11... | collective-permute-start | bytes 3145736 | tf_op jit(solution)/shard_map/ppermute | solution.py:59
  37.4 64.7 %copy-start.3 = (bf16[4,2,256,256]{3,2,1,0:T(8,128)(2,1)}, bf16[4,2,256,256]{3,2,1,0:T(8,128)(2,1)S(1)}, u32[]{:S(2)}) copy-start(bf16[4,2,256,256]{3,2,1,0:T(8,128)(2,1)S(1)} %collective-permute-done.1) | copy-start | bytes 3145732
  39.0 78.0 %collective-permute-start.5 = (bf16[2,4,2,256,256]{4,3,2,1,0:T(8,128)(2,1)}, bf16[2,4,2,256,256]{4,3,2,1,0:T(8,128)(2,1)}, u32[]{:S(2)}, u32[]{:S(2)}) collective-permute-start(bf16[2,4,2,256,256]{4,3,2,1,0:T(8,128)(2,1)} %pad_maximum_fusion), channel_id=1, source_target_pairs={{0,1},{1,0},{2,3},{3,2},{4,5},{5,4},{6,7},{7,6},{8,9},{9,8},{10,11... | collective-permute-start | bytes 6291464 | tf_op jit(solution)/shard_map/ppermute | solution.py:63
  55.3 48.4 %collective-permute-start.2 = (bf16[2,2,256,256]{3,2,1,0:T(8,128)(2,1)}, bf16[2,2,256,256]{3,2,1,0:T(8,128)(2,1)}, u32[]{:S(2)}, u32[]{:S(2)}) collective-permute-start(bf16[2,2,256,256]{3,2,1,0:T(8,128)(2,1)} %slice.43), channel_id=1, source_target_pairs={{0,2},{1,3},{2,4},{3,5},{4,6},{5,7},{6,0},{7,1},{8,10},{9,11},{10,... | collective-permute-start | bytes 1572872 | tf_op jit(solution)/shard_map/ppermute | solution.py:60
  98.9 10.2 %collective-permute-start.3 = (bf16[2,2,256,256]{3,2,1,0:T(8,128)(2,1)}, bf16[2,2,256,256]{3,2,1,0:T(8,128)(2,1)}, u32[]{:S(2)}, u32[]{:S(2)}) collective-permute-start(bf16[2,2,256,256]{3,2,1,0:T(8,128)(2,1)} %slice.44), channel_id=1, source_target_pairs={{0,6},{1,7},{2,0},{3,1},{4,2},{5,3},{6,4},{7,5},{8,14},{9,15},{10,... | collective-permute-start | bytes 1572872 | tf_op jit(solution)/shard_map/ppermute | solution.py:61
  103.7 20.4 %copy-start = (f32[4,1,2,1,256,256]{5,4,3,2,1,0:T(8,128)S(1)}, f32[4,1,2,1,256,256]{5,4,3,2,1,0:T(8,128)}, u32[]{:S(2)}) copy-start(f32[4,1,2,1,256,256]{5,4,3,2,1,0:T(8,128)} %param.7) | copy-start | bytes 6291460
  110.1 9.9 %collective-permute-start.6 = (bf16[4,2,256,256]{3,2,1,0:T(8,128)(2,1)S(1)}, bf16[4,2,256,256]{3,2,1,0:T(8,128)(2,1)S(1)}, u32[]{:S(2)}, u32[]{:S(2)}) collective-permute-start(bf16[4,2,256,256]{3,2,1,0:T(8,128)(2,1)S(1)} %constant_dynamic-update-slice_fusion), channel_id=1, source_target_pairs={{0,1},{1,0},{2,3},{3,2},{4,5},{5,4},{6,7},{7,6},{8,9},{9,8},{10,11... | collective-permute-start | bytes 3145736 | tf_op jit(solution)/shard_map/ppermute | solution.py:64
  137.9 1.4 copy-start.1
  139.3 26.2 %collective-permute-start.7 = (bf16[4,2,256,256]{3,2,1,0:T(8,128)(2,1)}, bf16[4,2,256,256]{3,2,1,0:T(8,128)(2,1)S(1)}, u32[]{:S(2)}, u32[]{:S(2)}) collective-permute-start(bf16[4,2,256,256]{3,2,1,0:T(8,128)(2,1)} %bitcast.40), channel_id=1, source_target_pairs={{0,2},{1,3},{2,4},{3,5},{4,6},{5,7},{6,0},{7,1},{8,10},{9,11},{10,... | collective-permute-start | bytes 3145736 | tf_op jit(solution)/shard_map/ppermute | solution.py:57
  141.0 24.7 %collective-permute-start.8 = (bf16[4,2,256,256]{3,2,1,0:T(8,128)(2,1)}, bf16[4,2,256,256]{3,2,1,0:T(8,128)(2,1)S(1)}, u32[]{:S(2)}, u32[]{:S(2)}) collective-permute-start(bf16[4,2,256,256]{3,2,1,0:T(8,128)(2,1)} %bitcast.40), channel_id=1, source_target_pairs={{0,6},{1,7},{2,0},{3,1},{4,2},{5,3},{6,4},{7,5},{8,14},{9,15},{10,... | collective-permute-start | bytes 3145736 | tf_op jit(solution)/shard_map/ppermute | solution.py:58
  165.6 5.5 %copy-start.4 = (bf16[4,2,256,256]{3,2,1,0:T(8,128)(2,1)}, bf16[4,2,256,256]{3,2,1,0:T(8,128)(2,1)S(1)}, u32[]{:S(2)}) copy-start(bf16[4,2,256,256]{3,2,1,0:T(8,128)(2,1)S(1)} %collective-permute-done.7) | copy-start | bytes 3145732
  165.6 10.8 %copy-start.5 = (bf16[4,2,256,256]{3,2,1,0:T(8,128)(2,1)}, bf16[4,2,256,256]{3,2,1,0:T(8,128)(2,1)S(1)}, u32[]{:S(2)}) copy-start(bf16[4,2,256,256]{3,2,1,0:T(8,128)(2,1)S(1)} %collective-permute-done.8) | copy-start | bytes 3145732
  167.3 28.1 %collective-permute-start.12 = (bf16[2,4,2,256,256]{4,3,2,1,0:T(8,128)(2,1)}, bf16[2,4,2,256,256]{4,3,2,1,0:T(8,128)(2,1)}, u32[]{:S(2)}, u32[]{:S(2)}) collective-permute-start(bf16[2,4,2,256,256]{4,3,2,1,0:T(8,128)(2,1)} %pad_maximum_fusion.1), channel_id=1, source_target_pairs={{0,1},{1,0},{2,3},{3,2},{4,5},{5,4},{6,7},{7,6},{8,9},{9,8},{10,11... | collective-permute-start | bytes 6291464 | tf_op jit(solution)/shard_map/ppermute | solution.py:63
  168.9 15.9 %collective-permute-start.9 = (bf16[2,2,256,256]{3,2,1,0:T(8,128)(2,1)}, bf16[2,2,256,256]{3,2,1,0:T(8,128)(2,1)}, u32[]{:S(2)}, u32[]{:S(2)}) collective-permute-start(bf16[2,2,256,256]{3,2,1,0:T(8,128)(2,1)} %slice.45), channel_id=1, source_target_pairs={{0,2},{1,3},{2,4},{3,5},{4,6},{5,7},{6,0},{7,1},{8,10},{9,11},{10,... | collective-permute-start | bytes 1572872 | tf_op jit(solution)/shard_map/ppermute | solution.py:60
  174.2 14.3 %collective-permute-start.10 = (bf16[2,2,256,256]{3,2,1,0:T(8,128)(2,1)}, bf16[2,2,256,256]{3,2,1,0:T(8,128)(2,1)S(1)}, u32[]{:S(2)}, u32[]{:S(2)}) collective-permute-start(bf16[2,2,256,256]{3,2,1,0:T(8,128)(2,1)} %slice.46), channel_id=1, source_target_pairs={{0,6},{1,7},{2,0},{3,1},{4,2},{5,3},{6,4},{7,5},{8,14},{9,15},{10,... | collective-permute-start | bytes 1572872 | tf_op jit(solution)/shard_map/ppermute | solution.py:61
  176.2 18.1 %collective-permute-start.11 = (bf16[4,2,256,256]{3,2,1,0:T(8,128)(2,1)}, bf16[4,2,256,256]{3,2,1,0:T(8,128)(2,1)S(1)}, u32[]{:S(2)}, u32[]{:S(2)}) collective-permute-start(bf16[4,2,256,256]{3,2,1,0:T(8,128)(2,1)} %bitcast.40), channel_id=1, source_target_pairs={{0,1},{1,0},{2,3},{3,2},{4,5},{5,4},{6,7},{7,6},{8,9},{9,8},{10,11... | collective-permute-start | bytes 3145736 | tf_op jit(solution)/shard_map/ppermute | solution.py:59
  178.7 71.5 %copy-start.2 = (f32[8,256,256]{2,1,0:T(8,128)S(1)}, f32[8,256,256]{2,1,0:T(8,128)}, u32[]{:S(2)}) copy-start(f32[8,256,256]{2,1,0:T(8,128)} %copy-done.1) | copy-start | bytes 6291460
  188.5 10.1 %collective-permute-start.13 = (bf16[4,2,256,256]{3,2,1,0:T(8,128)(2,1)S(1)}, bf16[4,2,256,256]{3,2,1,0:T(8,128)(2,1)S(1)}, u32[]{:S(2)}, u32[]{:S(2)}) collective-permute-start(bf16[4,2,256,256]{3,2,1,0:T(8,128)(2,1)S(1)} %constant_dynamic-update-slice_fusion.5), channel_id=1, source_target_pairs={{0,1},{1,0},{2,3},{3,2},{4,5},{5,4},{6,7},{7,6},{8,9},{9,8},{10,11... | collective-permute-start | bytes 3145736 | tf_op jit(solution)/shard_map/ppermute | solution.py:64
Sparse Core Ops, SparseCore 0:
  9.8 114.2 all-gather.5
  139.5 110.6 all-gather.3
